TPU v7x, 256 devices: a whole 4x4x8 slice. The times are simulated.
256 devices in a mesh: seq: 32 (over z, x_hi, core), fsdp: 8 (over x_lo, y).
Axes of the slice: x: 4 (x_hi: 2, x_lo: 2; x = x_hi * 2 + x_lo), y: 4, z: 8, core: 2. Of those that a mesh axis runs over, the one named last changes fastest.
Arguments:
- text_states: bfloat16 [8192, 8192], P('seq'), may hold values from -6 to 6
- images: bfloat16 [32, 1601, 8192], P('seq', None, 'fsdp'), may hold values from -6 to 6
- norm_gain: float32 [8192], replicated, may hold values from 0.1 to 1.9
- query_weight: bfloat16 [8192, 4096], P('seq', 'fsdp'), may hold values from -0.0625 to 0.0625
- image_projection_weight: bfloat16 [8192, 2048], P(('fsdp', 'seq')), may hold values from -0.0625 to 0.0625
- query_gain: float32 [128], replicated, may hold values from 0.5 to 2
- key_gain: float32 [128], replicated, may hold values from 0.5 to 2
- admission: int32 [32, 32], P('seq'), may hold values from 0 to 1, as said below
Outputs:
- attended: bfloat16 [8192, 4096], P('seq', 'fsdp')
Inputs may be any that keep to these rules, and one draw needn't show every extreme that they name: admission[c, m] is 1 for m = c and for at most 2 of the images m with c - 4 <= m < c, and 0 elsewhere; in every draw some text blocks, the last one among them, attend to exactly 3 images.
All inputs are finite; a program needn't handle non-finite values.
Results may differ from a plain program's by a relative error of at most 0.035.
Values may be sent and summed in bfloat16 or wider, within the bound.
No kernel may reach another device: no remote copies, remote signals or barrier semaphores. Data moves between devices by JAX's collectives and lax.ppermute only.
A program may use at most 128 MiB of HBM per device.

v0:
```python
import math

import jax
import jax.numpy as jnp
from jax import lax
from jax.sharding import PartitionSpec as P

KEY_VALUE_HEADS = 8
IMAGE_LOOKBACK = 4


def from_behind(value, axis, steps):
    count = lax.axis_size(axis)
    initial, last = (max(0, -steps), min(count, count - steps))
    return lax.ppermute(value, axis, [(source, source + steps) for source in range(initial, last)])


def rms_scale(values, gain):
    return values * lax.rsqrt(jnp.mean(values * values, axis=-1, keepdims=True) + 1e-05) * gain


def attend(query_heads, stacked, admitted):
    slot_count, kv_heads, image_tokens, double_width = stacked.shape
    head_dim = double_width // 2
    row_count, heads_local, _ = query_heads.shape
    heads_per_group = heads_local // kv_heads
    grouped = query_heads.reshape(row_count, kv_heads, heads_per_group, head_dim)
    grouped = grouped.transpose(1, 2, 0, 3).reshape(kv_heads, heads_per_group * row_count, head_dim)
    per_head = jnp.moveaxis(stacked, 1, 0).reshape(
        kv_heads, slot_count * image_tokens, double_width
    )
    column_live = jnp.repeat(admitted, image_tokens)
    score_scale = 1.0 / math.sqrt(head_dim)

    def one_head(operands):
        query_rows, key_value_pair = operands
        scores = (
            lax.dot_general(
                query_rows,
                key_value_pair[:, :head_dim],
                (((1,), (1,)), ((), ())),
                preferred_element_type=jnp.float32,
            )
            * score_scale
        )
        scores = jnp.where(column_live[None, :], scores, -jnp.inf)
        row_peak = jnp.max(scores, axis=1, keepdims=True)
        weights = jnp.exp(scores - row_peak)
        row_total = jnp.sum(weights, axis=1, keepdims=True)
        blended = jnp.dot(
            weights.astype(jnp.bfloat16),
            key_value_pair[:, head_dim:],
            preferred_element_type=jnp.float32,
        )
        return blended / row_total

    outputs = lax.map(one_head, (grouped, per_head))
    outputs = outputs.reshape(kv_heads, heads_per_group, row_count, head_dim).transpose(2, 0, 1, 3)
    return outputs.reshape(row_count, heads_local * head_dim).astype(jnp.bfloat16)


def on_device(
    text_states,
    images,
    norm_gain,
    query_weight,
    image_projection_weight,
    query_gain,
    key_gain,
    admission,
):
    head_dim = query_gain.shape[0]
    local_key_value = KEY_VALUE_HEADS // lax.axis_size("fsdp")
    heads_local = query_weight.shape[1] // head_dim
    row_count = text_states.shape[0]
    normed = rms_scale(text_states.astype(jnp.float32), norm_gain).astype(jnp.bfloat16)
    columns = normed
    queries = jnp.dot(
        columns,
        lax.all_gather(query_weight, "seq", axis=0, tiled=True),
        preferred_element_type=jnp.float32,
    )
    query_heads = rms_scale(queries.reshape(row_count, heads_local, head_dim), query_gain).astype(
        jnp.bfloat16
    )
    weight_block = lax.all_gather(image_projection_weight, "seq", axis=0, tiled=True)
    features = images[0]
    columns = weight_block
    score_product = jnp.dot(features, columns, preferred_element_type=jnp.float32)
    own_kv = lax.psum_scatter(
        score_product.reshape(
            features.shape[0], local_key_value * lax.axis_size("fsdp"), 2 * head_dim
        )
        .transpose(1, 0, 2)
        .astype(jnp.bfloat16),
        "fsdp",
        scatter_dimension=0,
        tiled=True,
    ).astype(jnp.float32)
    key_part = rms_scale(own_kv[..., :head_dim], key_gain)
    packed = jnp.concatenate([key_part, own_kv[..., head_dim:]], axis=-1).astype(jnp.bfloat16)
    image_window = [packed]
    for distance in range(1, IMAGE_LOOKBACK + 1):
        image_window.append(from_behind(packed, "seq", distance))
    stacked = jnp.stack(image_window)
    span_index = lax.axis_index("seq")
    image_ids = span_index - jnp.arange(IMAGE_LOOKBACK + 1, dtype=jnp.int32)
    admitted = (image_ids >= 0) & (jnp.take(admission[0], jnp.maximum(image_ids, 0)) == 1)
    return attend(query_heads, stacked, admitted)


def solution(mesh):
    placed = (
        P("seq", None),
        P("seq", None, "fsdp"),
        P(),
        P("seq", "fsdp"),
        P(("fsdp", "seq"), None),
        P(),
        P(),
        P("seq", None),
    )
    return jax.shard_map(
        on_device, mesh=mesh, in_specs=placed, out_specs=P("seq", "fsdp"), check_vma=False
    )
```

profile of v0, /device:TPU:133, one launch (start us, length us, event | category | flops | bytes accessed | tf_op | source)
XLA Modules:
  0.0 405.3 jit_solution(13469132266472897213)
XLA Ops:
  8.1 85.6 %all-gather.5.cloned.1.call-done = bf16[1024,2048]{1,0:T(8,128)(2,1)} async-done(((bf16[32,2048]{1,0:T(8,128)(2,1)}), bf16[1024,2048]{1,0:T(8,128)(2,1)}) %all-gather.5.cloned.1.call-update) | async-done | bytes 4194320 | tf_op jit(solution)/shard_map/all_gather | solution.py:86
  93.7 6.4 %copy.20 = bf16[2048,1024]{1,0:T(8,128)(2,1)} copy(bf16[2048,1024]{0,1:T(8,128)(2,1)} %bitcast.39) | data formatting | bytes 8388608 | tf_op jit(solution)/shard_map/dot_general | solution.py:89
  100.1 11.0 %convert_bitcast_fusion = bf16[8,1601,256]{2,1,0:T(8,128)(2,1)} fusion(bf16[8,256,1024]{2,1,0:T(8,128)(2,1)} %bitcast.40, bf16[1,1601,1024]{2,1,0:T(8,128)(2,1)S(1)} %copy-done), kind=kOutput, calls=%fused_computation.13 | convolution fusion | flops 6718359552 | bytes 14030848 | tf_op jit(solution)/shard_map/dot_general | solution.py:89
  112.5 3.1 fusion.6
  115.7 78.7 %all-gather.3.cloned.1.call-done = bf16[8192,512]{1,0:T(8,128)(2,1)} async-done(((bf16[256,512]{1,0:T(8,128)(2,1)}), bf16[8192,512]{1,0:T(8,128)(2,1)}) %all-gather.3.cloned.1.call-update) | async-done | bytes 8388624 | tf_op jit(solution)/shard_map/all_gather | solution.py:80
  194.3 7.0 %fusion.31 = (f32[256,512]{1,0:T(8,128)S(1)}, f32[256,512]{1,0:T(8,128)S(1)}) fusion(bf16[8192,512]{1,0:T(8,128)(2,1)} %all-gather.3.cloned.1.call-done, bf16[256,8192]{1,0:T(8,128)(2,1)} %param.8, f32[8192]{0:T(1024)S(1)} %copy-done.7, f32[256]{0:T(256)S(1)} %add_rsqrt_fusion.2), kind=kOutput, calls=%fused_computation.45 | convolution fusion | flops 2156003328 | bytes 13665280 | tf_op jit(solution)/shard_map/dot_general | solution.py:78
  202.4 74.4 %reduce-scatter.2.cloned.1.call-done = bf16[1,1601,256]{2,1,0:T(8,128)(2,1)} async-done(((bf16[8,1601,256]{2,1,0:T(8,128)(2,1)}), bf16[1,1601,256]{2,1,0:T(8,128)(2,1)}) %reduce-scatter.2.cloned.1.call-update) | async-done | bytes 819728 | tf_op jit(solution)/shard_map/reduce_scatter | solution.py:90
  276.8 1.4 convert_element_type.62
  278.9 3.0 collective-permute-start
  282.3 2.3 collective-permute-start.3
  284.6 1.9 collective-permute-start.2
  286.5 4.5 %collective-permute-start.1 = (bf16[1,1601,256]{2,1,0:T(8,128)(2,1)S(1)}, bf16[1,1601,256]{2,1,0:T(8,128)(2,1)S(1)}, u32[]{:S(2)}, u32[]{:S(2)}) collective-permute-start(bf16[1,1601,256]{2,1,0:T(8,128)(2,1)S(1)} %pad_maximum_fusion), channel_id=1, source_target_pairs={{0,16},{8,24},{16,32},{24,40},{32,48},{40,56},{48,64},{56,72},{64,... | collective-permute-start | bytes 2459144 | tf_op jit(solution)/shard_map/ppermute | solution.py:15
  291.1 1.0 maximum_dynamic-update-slice_fusion
  292.1 5.5 %collective-permute-done = bf16[1,1601,256]{2,1,0:T(8,128)(2,1)S(1)} collective-permute-done((bf16[1,1601,256]{2,1,0:T(8,128)(2,1)S(1)}, bf16[1,1601,256]{2,1,0:T(8,128)(2,1)S(1)}, u32[]{:S(2)}, u32[]{:S(2)}) %collective-permute-start) | collective-permute-done | bytes 819744 | tf_op jit(solution)/shard_map/ppermute | solution.py:15
  297.5 1.0 bitcast_dynamic-update-slice_fusion.3
  298.5 45.7 %collective-permute-done.1 = bf16[1,1601,256]{2,1,0:T(8,128)(2,1)S(1)} collective-permute-done((bf16[1,1601,256]{2,1,0:T(8,128)(2,1)S(1)}, bf16[1,1601,256]{2,1,0:T(8,128)(2,1)S(1)}, u32[]{:S(2)}, u32[]{:S(2)}) %collective-permute-start.1) | collective-permute-done | bytes 819744 | tf_op jit(solution)/shard_map/ppermute | solution.py:15
  344.2 1.0 bitcast_dynamic-update-slice_fusion.2
  345.2 1.0 bitcast_dynamic-update-slice_fusion.1
  346.2 1.0 bitcast_dynamic-update-slice_fusion
  347.1 5.2 %squeeze.19 = bf16[8005,256]{1,0:T(8,128)(2,1)} reshape(bf16[5,1,1601,256]{3,2,1,0:T(8,128)(2,1)} %bitcast_dynamic-update-slice_fusion) | data formatting | bytes 8197120 | tf_op jit(solution)/shard_map/while/body/jit(dynamic_index_in_dim)/squeeze | solution.py:57
  352.3 13.8 %fusion = (f32[1024]{0:T(1024)S(1)}, f32[1024,8005]{0,1:T(8,128)}) fusion(pred[8005]{0:T(1024)(128)(4,1)S(1)} %broadcast_in_dim.38, bf16[1024,128]{1,0:T(8,128)(2,1)S(1)} %bitcast.41, bf16[8005,256]{1,0:T(8,128)(2,1)} %squeeze.19), kind=kOutput, calls=%fused_computation.3 | convolution fusion | flops 2123053056 | bytes 35112772 | tf_op jit(solution)/shard_map/while/body/eval_jaxpr/dot_general | solution.py:38
  366.1 15.1 %fusion.1 = f32[1024]{0:T(1024)S(1)} fusion(f32[1024,8005]{0,1:T(8,128)} %get-tuple-element.22, f32[1024]{0:T(1024)S(1)} %get-tuple-element.20, pred[8005]{0:T(1024)(128)(4,1)S(1)} %broadcast_in_dim.38), kind=kLoop, calls=%fused_computation.4 | loop fusion | flops 32787456 | bytes 32804676 | tf_op jit(solution)/shard_map/while/body/eval_jaxpr/reduce_sum | solution.py:49
  381.2 16.6 %fusion.22 = bf16[1024,128]{1,0:T(8,128)(2,1)S(1)} fusion(bf16[8005,256]{1,0:T(8,128)(2,1)S(1)} %copy-done.3, f32[1024,8005]{0,1:T(8,128)} %get-tuple-element.22, f32[1024]{0:T(1024)S(1)} %get-tuple-element.20, pred[8005]{0:T(1024)(128)(4,1)S(1)} %broadcast_in_dim.38, f32[1024]{0:T(1024)S(1)} %fusion.1), kind=kOutput, calls=%fused_computation.22 | convolution fusion | flops 2131513344 | bytes 35117056 | tf_op jit(solution)/shard_map/while/body/eval_jaxpr/dot_general | solution.py:50
  398.0 0.7 copy.29
  (46 shorter events, 5.2 us)
Async XLA Ops:
  6.5 93.5 %copy-start = (bf16[1,1601,1024]{2,1,0:T(8,128)(2,1)S(1)}, bf16[1,1601,1024]{2,1,0:T(8,128)(2,1)}, u32[]{:S(2)}) copy-start(bf16[1,1601,1024]{2,1,0:T(8,128)(2,1)} %param.9) | copy-start | bytes 9836548
  6.5 87.1 %all-gather.5.cloned.1.call-start = ((), (), s32[]{:S(2)}) async-start(), calls=%async_computation.2 | async-start | bytes 4325376 | tf_op jit(solution)/shard_map/all_gather | solution.py:86
  7.3 187.1 %all-gather.3.cloned.1.call-start = ((), (), s32[]{:S(2)}) async-start(), calls=%async_computation.1 | async-start | bytes 8650752 | tf_op jit(solution)/shard_map/all_gather | solution.py:80
  8.0 268.8 %reduce-scatter.2.cloned.1.call-start = ((), (), s32[]{:S(2)}) async-start(), calls=%async_computation.3 | async-start | bytes 7409664 | tf_op jit(solution)/shard_map/reduce_scatter | solution.py:90
  111.0 0.7 copy-start.2
  111.0 83.3 %copy-start.7 = (f32[8192]{0:T(1024)S(1)}, f32[8192]{0:T(1024)}, u32[]{:S(2)}) copy-start(f32[8192]{0:T(1024)} %param.10) | copy-start | bytes 98308
  115.7 86.6 %copy-start.6 = (f32[128]{0:T(128)S(1)}, f32[128]{0:T(128)}, u32[]{:S(2)}) copy-start(f32[128]{0:T(128)} %param.13) | copy-start | bytes 1540
  201.4 77.2 %copy-start.5 = (f32[128]{0:T(128)S(1)}, f32[128]{0:T(128)}, u32[]{:S(2)}) copy-start(f32[128]{0:T(128)} %param.14) | copy-start | bytes 1540
  276.8 2.0 slice-start
  276.8 14.2 %copy-start.4 = (bf16[1,1601,256]{2,1,0:T(8,128)(2,1)S(1)}, bf16[1,1601,256]{2,1,0:T(8,128)(2,1)}, u32[]{:S(2)}) copy-start(bf16[1,1601,256]{2,1,0:T(8,128)(2,1)} %reduce-scatter.2.cloned.1.call-done) | copy-start | bytes 2459140
  278.9 18.6 %collective-permute-start = (bf16[1,1601,256]{2,1,0:T(8,128)(2,1)S(1)}, bf16[1,1601,256]{2,1,0:T(8,128)(2,1)S(1)}, u32[]{:S(2)}, u32[]{:S(2)}) collective-permute-start(bf16[1,1601,256]{2,1,0:T(8,128)(2,1)S(1)} %pad_maximum_fusion), channel_id=1, source_target_pairs={{0,8},{8,16},{16,24},{24,32},{32,40},{40,48},{48,56},{56,64},{64,7... | collective-permute-start | bytes 2459144 | tf_op jit(solution)/shard_map/ppermute | solution.py:15
  282.3 63.9 %collective-permute-start.3 = (bf16[1,1601,256]{2,1,0:T(8,128)(2,1)S(1)}, bf16[1,1601,256]{2,1,0:T(8,128)(2,1)S(1)}, u32[]{:S(2)}, u32[]{:S(2)}) collective-permute-start(bf16[1,1601,256]{2,1,0:T(8,128)(2,1)S(1)} %pad_maximum_fusion), channel_id=1, source_target_pairs={{0,32},{8,40},{16,48},{24,56},{32,64},{40,72},{48,80},{56,88},{64,... | collective-permute-start | bytes 2459144 | tf_op jit(solution)/shard_map/ppermute | solution.py:15
  284.6 60.6 %collective-permute-start.2 = (bf16[1,1601,256]{2,1,0:T(8,128)(2,1)S(1)}, bf16[1,1601,256]{2,1,0:T(8,128)(2,1)S(1)}, u32[]{:S(2)}, u32[]{:S(2)}) collective-permute-start(bf16[1,1601,256]{2,1,0:T(8,128)(2,1)S(1)} %pad_maximum_fusion), channel_id=1, source_target_pairs={{0,24},{8,32},{16,40},{24,48},{32,56},{40,64},{48,72},{56,80},{64,... | collective-permute-start | bytes 2459144 | tf_op jit(solution)/shard_map/ppermute | solution.py:15
  286.5 57.7 %collective-permute-start.1 = (bf16[1,1601,256]{2,1,0:T(8,128)(2,1)S(1)}, bf16[1,1601,256]{2,1,0:T(8,128)(2,1)S(1)}, u32[]{:S(2)}, u32[]{:S(2)}) collective-permute-start(bf16[1,1601,256]{2,1,0:T(8,128)(2,1)S(1)} %pad_maximum_fusion), channel_id=1, source_target_pairs={{0,16},{8,24},{16,32},{24,40},{32,48},{40,56},{48,64},{56,72},{64,... | collective-permute-start | bytes 2459144 | tf_op jit(solution)/shard_map/ppermute | solution.py:15
  366.1 15.1 %copy-start.3 = (bf16[8005,256]{1,0:T(8,128)(2,1)S(1)}, bf16[8005,256]{1,0:T(8,128)(2,1)}, u32[]{:S(2)}) copy-start(bf16[8005,256]{1,0:T(8,128)(2,1)} %squeeze.19) | copy-start | bytes 12295684
  381.2 17.6 %copy-start.1 = (bf16[1,1601,1024]{2,1,0:T(8,128)(2,1)S(1)}, bf16[1,1601,1024]{2,1,0:T(8,128)(2,1)}, u32[]{:S(2)}) copy-start(bf16[1,1601,1024]{2,1,0:T(8,128)(2,1)} %param.9) | copy-start | bytes 9836548
Sparse Core Ops, SparseCore 0:
  10.1 83.4 all-gather.4
  96.4 97.8 all-gather.2
  196.9 79.8 reduce-scatter.1
where the time goes:
time: 411 us; the launch traced here: 405 us
  waiting for transfers between devices  291 us (71%)
  matrix products  48.4 us (12%)
  other arithmetic  22.1 us (5%)
  local copies, waits for them, and re-layouts  18.3 us (4%)
  between operations  13.4 us (3%)
  starting transfers between devices  11.8 us (3%)
    all_gather x1, waiting for transfers between devices, on_device(): lax.all_gather(image_projection_weight, 'seq', axis=0, tiled=True)  85.6 us
    all_gather x1, waiting for transfers between devices, on_device(): lax.all_gather(query_weight, 'seq', axis=0, tiled=True)  78.7 us
    reduce_scatter x1, waiting for transfers between devices, on_device(): lax.psum_scatter(score_product.reshape(features.shape[0], local_key_value...  74.4 us
    ppermute x4, waiting for transfers between devices, from_behind(): lax.ppermute(value, axis, [(source, source + steps) for source in range(i...  51.2 us
    dot_general x1, matrix products, one_head(): jnp.dot(weights.astype(jnp.bfloat16), key_value_pair[:, head_dim:], prefe...  16.6 us
    reduce_sum x1, other arithmetic, one_head(): row_total = jnp.sum(weights, axis=1, keepdims=True)  15.1 us
    dot_general x1, matrix products, one_head(): lax.dot_general(query_rows, key_value_pair[:, :head_dim], (((1,), (1,)),...  13.8 us
    ppermute x4, starting transfers between devices, from_behind(): lax.ppermute(value, axis, [(source, source + steps) for source in range(i...  11.8 us
  transfers between devices with their start and end apart: 7, of which 5 were waited for; matrix products, arithmetic and copies ran while one was open for 8% of the time, Pallas kernels for 0%

commit v1 on v0

--- a/solution.py
+++ b/solution.py
@@ -74,16 +74,18 @@
     heads_local = query_weight.shape[1] // head_dim
     row_count = text_states.shape[0]
     normed = rms_scale(text_states.astype(jnp.float32), norm_gain).astype(jnp.bfloat16)
-    columns = normed
-    queries = jnp.dot(
-        columns,
-        lax.all_gather(query_weight, "seq", axis=0, tiled=True),
-        preferred_element_type=jnp.float32,
+    kv_rows, kv_width = image_projection_weight.shape
+    query_width = query_weight.shape[1]
+    kv_as_rows = image_projection_weight.reshape(kv_rows * kv_width // query_width, query_width)
+    both = lax.all_gather(
+        jnp.concatenate([kv_as_rows, query_weight], axis=0), "seq", axis=0, tiled=False
     )
+    weight_block = both[:, : kv_as_rows.shape[0]].reshape(-1, kv_width)
+    query_block = both[:, kv_as_rows.shape[0] :].reshape(-1, query_width)
+    queries = jnp.dot(normed, query_block, preferred_element_type=jnp.float32)
     query_heads = rms_scale(queries.reshape(row_count, heads_local, head_dim), query_gain).astype(
         jnp.bfloat16
     )
-    weight_block = lax.all_gather(image_projection_weight, "seq", axis=0, tiled=True)
     features = images[0]
     columns = weight_block
     score_product = jnp.dot(features, columns, preferred_element_type=jnp.float32)

time: 411 us -> 369 us (0.90)
  waiting for transfers between devices: 291 us -> 215 us
  local copies, waits for them, and re-layouts: 18.3 us -> 51.6 us
    all_gather x2 -> x1, waiting for transfers between devices: 164 us -> 115 us  [on_device(): lax.all_gather(jnp.concatenate([kv_as_rows, query_weight], axis=0), 'seq'...]
    reduce_scatter x1, waiting for transfers between devices: 74.4 us -> 48.8 us  [on_device(): lax.psum_scatter(score_product.reshape(features.shape[0], local_key_value...]
    reshape x1 -> x3, local copies, waits for them, and re-layouts: 0.19 us -> 20.7 us  [the longest x1 12 us: on_device(): query_block = both[:, kv_as_rows.shape[0]:].reshape(-1, query_width)]
    slice x0 -> x2, local copies, waits for them, and re-layouts: none -> 12 us  [the longest x1 7.47 us: on_device(): query_block = both[:, kv_as_rows.shape[0]:].reshape(-1, query_width)]
    dot_general x1 -> x0, local copies, waits for them, and re-layouts: 6.39 us -> none  [on_device(): jnp.dot(features, columns, preferred_element_type=jnp.float32)]
    convert_element_type x0 -> x2, local copies, waits for them, and re-layouts: none -> 4.62 us  [on_device(): own_kv = lax.psum_scatter(score_product.reshape(features.shape[0], local_...]
  transfers between devices with their start and end apart: 7 -> 6, of which waited for: 5 -> 4; matrix products, arithmetic and copies ran while one was open for 8% -> 10% of each run, Pallas kernels for 0% -> 0%
where the time goes in v1:
time: 369 us; the launch traced here: 362 us
  waiting for transfers between devices  215 us (58%)
  local copies, waits for them, and re-layouts  51.6 us (14%)
  matrix products  46.7 us (13%)
  other arithmetic  23.5 us (6%)
  between operations  13.6 us (4%)
  starting transfers between devices  11.8 us (3%)
    all_gather x1, waiting for transfers between devices, on_device(): lax.all_gather(jnp.concatenate([kv_as_rows, query_weight], axis=0), 'seq'...  115 us
    ppermute x4, waiting for transfers between devices, from_behind(): lax.ppermute(value, axis, [(source, source + steps) for source in range(i...  51.2 us
    reduce_scatter x1, waiting for transfers between devices, on_device(): lax.psum_scatter(score_product.reshape(features.shape[0], local_key_value...  48.8 us
    dot_general x1, matrix products, one_head(): jnp.dot(weights.astype(jnp.bfloat16), key_value_pair[:, head_dim:], prefe...  16.6 us
    reduce_sum x1, other arithmetic, one_head(): row_total = jnp.sum(weights, axis=1, keepdims=True)  15.1 us
    dot_general x1, matrix products, one_head(): lax.dot_general(query_rows, key_value_pair[:, :head_dim], (((1,), (1,)),...  13.8 us
    reshape x1, local copies, waits for them, and re-layouts, on_device(): query_block = both[:, kv_as_rows.shape[0]:].reshape(-1, query_width)  12 us
    ppermute x4, starting transfers between devices, from_behind(): lax.ppermute(value, axis, [(source, source + steps) for source in range(i...  11.8 us
  transfers between devices with their start and end apart: 6, of which 4 were waited for; matrix products, arithmetic and copies ran while one was open for 10% of the time, Pallas kernels for 0%

profile of v1, /device:TPU:133, one launch (start us, length us, event | category | flops | bytes accessed | tf_op | source)
XLA Modules:
  0.0 362.3 jit_solution(18006811424758606231)
XLA Ops:
  6.5 1.1 reshape.137
  7.7 1.7 pad_maximum_fusion.1
  9.5 115.0 %all-gather.3.cloned.1.call-done = bf16[12288,512]{1,0:T(8,128)(2,1)} async-done(((bf16[384,512]{1,0:T(8,128)(2,1)}), bf16[12288,512]{1,0:T(8,128)(2,1)}) %all-gather.3.cloned.1.call-update) | async-done | bytes 12582928 | tf_op jit(solution)/shard_map/all_gather | solution.py:80
  124.4 4.6 %slice.29 = bf16[32,128,512]{2,1,0:T(8,128)(2,1)} slice(bf16[32,384,512]{2,1,0:T(8,128)(2,1)} %bitcast.56), slice={[0:32], [0:128], [0:512]} | slice | bytes 8388608 | tf_op jit(solution)/shard_map/slice | solution.py:83
  129.0 7.5 %reshape.140 = bf16[1024,2048]{1,0:T(8,128)(2,1)} reshape(bf16[32,128,512]{2,1,0:T(8,128)(2,1)} %slice.29) | data formatting | bytes 8388608 | tf_op jit(solution)/shard_map/reshape | solution.py:83
  136.5 9.6 %convolution_convert_fusion = bf16[2048,1601]{0,1:T(8,128)(2,1)S(1)} fusion(bf16[1024,2048]{1,0:T(8,128)(2,1)} %reshape.140, bf16[1,1601,1024]{2,1,0:T(8,128)(2,1)S(1)} %copy-done), kind=kOutput, calls=%fused_computation.13 | convolution fusion | flops 6718359552 | bytes 14030848 | tf_op jit(solution)/shard_map/dot_general | solution.py:91
  146.1 2.9 copy.20
  149.5 4.1 %copy.24 = bf16[1601,8,256]{2,0,1:T(8,128)(2,1)} copy(bf16[1601,8,256]{2,1,0:T(8,128)(2,1)S(1)} %slice.34) | data formatting | bytes 13115392 | tf_op jit(solution)/shard_map/convert_element_type | solution.py:97
  155.1 3.1 fusion.6
  158.2 7.5 %slice.28 = bf16[32,256,512]{2,1,0:T(8,128)(2,1)} slice(bf16[32,384,512]{2,1,0:T(8,128)(2,1)} %bitcast.57), slice={[0:32], [128:384], [0:512]} | slice | bytes 16777216 | tf_op jit(solution)/shard_map/slice | solution.py:84
  165.7 12.0 %copy.19 = bf16[8192,512]{0,1:T(8,128)(2,1)} copy(bf16[8192,512]{1,0:T(8,128)(2,1)} %bitcast.53) | data formatting | bytes 16777216 | tf_op jit(solution)/shard_map/reshape | solution.py:84
  177.7 6.7 %multiply_reduce_fusion.1 = (f32[256,4]{0,1:T(4,128)S(1)}, f32[256,4,128]{2,0,1:T(8,128)S(1)}) fusion(bf16[4,128,8192]{2,1,0:T(8,128)(2,1)} %bitcast.58, bf16[256,8192]{1,0:T(8,128)(2,1)} %param.8, f32[8192]{0:T(1024)S(1)} %copy-done.7, f32[256]{0:T(256)S(1)} %add_rsqrt_fusion.2), kind=kOutput, calls=%fused_computation.35 | convolution fusion | flops 2156133376 | bytes 13145088 | tf_op jit(solution)/shard_map/dot_general | solution.py:85
  184.7 48.8 %reduce-scatter.2.cloned.1.call-done = bf16[1,1601,256]{2,1,0:T(8,128)(2,1)} async-done(((bf16[8,1601,256]{2,1,0:T(8,128)(2,1)}), bf16[1,1601,256]{2,1,0:T(8,128)(2,1)}) %reduce-scatter.2.cloned.1.call-update) | async-done | bytes 819728 | tf_op jit(solution)/shard_map/reduce_scatter | solution.py:92
  233.5 1.4 convert_element_type.63
  235.6 3.3 collective-permute-start
  239.2 2.3 collective-permute-start.3
  241.5 1.9 collective-permute-start.2
  243.4 4.3 %collective-permute-start.1 = (bf16[1,1601,256]{2,1,0:T(8,128)(2,1)S(1)}, bf16[1,1601,256]{2,1,0:T(8,128)(2,1)S(1)}, u32[]{:S(2)}, u32[]{:S(2)}) collective-permute-start(bf16[1,1601,256]{2,1,0:T(8,128)(2,1)S(1)} %pad_maximum_fusion), channel_id=1, source_target_pairs={{0,16},{8,24},{16,32},{24,40},{32,48},{40,56},{48,64},{56,72},{64,... | collective-permute-start | bytes 2459144 | tf_op jit(solution)/shard_map/ppermute | solution.py:15
  248.8 5.3 %collective-permute-done = bf16[1,1601,256]{2,1,0:T(8,128)(2,1)S(1)} collective-permute-done((bf16[1,1601,256]{2,1,0:T(8,128)(2,1)S(1)}, bf16[1,1601,256]{2,1,0:T(8,128)(2,1)S(1)}, u32[]{:S(2)}, u32[]{:S(2)}) %collective-permute-start) | collective-permute-done | bytes 819744 | tf_op jit(solution)/shard_map/ppermute | solution.py:15
  255.1 45.9 %collective-permute-done.1 = bf16[1,1601,256]{2,1,0:T(8,128)(2,1)S(1)} collective-permute-done((bf16[1,1601,256]{2,1,0:T(8,128)(2,1)S(1)}, bf16[1,1601,256]{2,1,0:T(8,128)(2,1)S(1)}, u32[]{:S(2)}, u32[]{:S(2)}) %collective-permute-start.1) | collective-permute-done | bytes 819744 | tf_op jit(solution)/shard_map/ppermute | solution.py:15
  303.8 5.2 %squeeze.19 = bf16[8005,256]{1,0:T(8,128)(2,1)} reshape(bf16[5,1,1601,256]{3,2,1,0:T(8,128)(2,1)} %bitcast_dynamic-update-slice_fusion) | data formatting | bytes 8197120 | tf_op jit(solution)/shard_map/while/body/jit(dynamic_index_in_dim)/squeeze | solution.py:57
  309.0 13.8 %fusion = (f32[1024]{0:T(1024)S(1)}, f32[1024,8005]{0,1:T(8,128)}) fusion(pred[8005]{0:T(1024)(128)(4,1)S(1)} %broadcast_in_dim.38, bf16[1024,128]{1,0:T(8,128)(2,1)S(1)} %bitcast.60, bf16[8005,256]{1,0:T(8,128)(2,1)} %squeeze.19), kind=kOutput, calls=%fused_computation.3 | convolution fusion | flops 2123053056 | bytes 35112772 | tf_op jit(solution)/shard_map/while/body/eval_jaxpr/dot_general | solution.py:38
  322.8 15.1 %fusion.1 = f32[1024]{0:T(1024)S(1)} fusion(f32[1024,8005]{0,1:T(8,128)} %get-tuple-element.22, f32[1024]{0:T(1024)S(1)} %get-tuple-element.20, pred[8005]{0:T(1024)(128)(4,1)S(1)} %broadcast_in_dim.38), kind=kLoop, calls=%fused_computation.4 | loop fusion | flops 32787456 | bytes 32804676 | tf_op jit(solution)/shard_map/while/body/eval_jaxpr/reduce_sum | solution.py:49
  338.0 16.6 %fusion.23 = bf16[1024,128]{1,0:T(8,128)(2,1)S(1)} fusion(bf16[8005,256]{1,0:T(8,128)(2,1)S(1)} %copy-done.3, f32[1024,8005]{0,1:T(8,128)} %get-tuple-element.22, f32[1024]{0:T(1024)S(1)} %get-tuple-element.20, pred[8005]{0:T(1024)(128)(4,1)S(1)} %broadcast_in_dim.38, f32[1024]{0:T(1024)S(1)} %fusion.1), kind=kOutput, calls=%fused_computation.24 | convolution fusion | flops 2131513344 | bytes 35117056 | tf_op jit(solution)/shard_map/while/body/eval_jaxpr/dot_general | solution.py:50
  (47 shorter events, 9.0 us)
Async XLA Ops:
  6.5 130.0 %copy-start = (bf16[1,1601,1024]{2,1,0:T(8,128)(2,1)S(1)}, bf16[1,1601,1024]{2,1,0:T(8,128)(2,1)}, u32[]{:S(2)}) copy-start(bf16[1,1601,1024]{2,1,0:T(8,128)(2,1)} %param.9) | copy-start | bytes 9836548
  6.5 117.9 %all-gather.3.cloned.1.call-start = ((), (), s32[]{:S(2)}) async-start(), calls=%async_computation.2 | async-start | bytes 12976128 | tf_op jit(solution)/shard_map/all_gather | solution.py:80
  9.4 224.0 %reduce-scatter.2.cloned.1.call-start = ((), (), s32[]{:S(2)}) async-start(), calls=%async_computation.1 | async-start | bytes 7409664 | tf_op jit(solution)/shard_map/reduce_scatter | solution.py:92
  153.6 0.7 copy-start.2
  165.7 12.0 %copy-start.7 = (f32[8192]{0:T(1024)S(1)}, f32[8192]{0:T(1024)}, u32[]{:S(2)}) copy-start(f32[8192]{0:T(1024)} %param.10) | copy-start | bytes 98308
  177.7 6.8 %copy-start.6 = (f32[128]{0:T(128)S(1)}, f32[128]{0:T(128)}, u32[]{:S(2)}) copy-start(f32[128]{0:T(128)} %param.13) | copy-start | bytes 1540
  177.7 57.5 %copy-start.5 = (f32[128]{0:T(128)S(1)}, f32[128]{0:T(128)}, u32[]{:S(2)}) copy-start(f32[128]{0:T(128)} %param.14) | copy-start | bytes 1540
  233.5 2.0 slice-start
  233.5 14.3 %copy-start.4 = (bf16[1,1601,256]{2,1,0:T(8,128)(2,1)S(1)}, bf16[1,1601,256]{2,1,0:T(8,128)(2,1)}, u32[]{:S(2)}) copy-start(bf16[1,1601,256]{2,1,0:T(8,128)(2,1)} %reduce-scatter.2.cloned.1.call-done) | copy-start | bytes 2459140
  235.6 18.5 %collective-permute-start = (bf16[1,1601,256]{2,1,0:T(8,128)(2,1)S(1)}, bf16[1,1601,256]{2,1,0:T(8,128)(2,1)S(1)}, u32[]{:S(2)}, u32[]{:S(2)}) collective-permute-start(bf16[1,1601,256]{2,1,0:T(8,128)(2,1)S(1)} %pad_maximum_fusion), channel_id=1, source_target_pairs={{0,8},{8,16},{16,24},{24,32},{32,40},{40,48},{48,56},{56,64},{64,7... | collective-permute-start | bytes 2459144 | tf_op jit(solution)/shard_map/ppermute | solution.py:15
  239.2 63.7 %collective-permute-start.3 = (bf16[1,1601,256]{2,1,0:T(8,128)(2,1)S(1)}, bf16[1,1601,256]{2,1,0:T(8,128)(2,1)S(1)}, u32[]{:S(2)}, u32[]{:S(2)}) collective-permute-start(bf16[1,1601,256]{2,1,0:T(8,128)(2,1)S(1)} %pad_maximum_fusion), channel_id=1, source_target_pairs={{0,32},{8,40},{16,48},{24,56},{32,64},{40,72},{48,80},{56,88},{64,... | collective-permute-start | bytes 2459144 | tf_op jit(solution)/shard_map/ppermute | solution.py:15
  241.5 60.4 %collective-permute-start.2 = (bf16[1,1601,256]{2,1,0:T(8,128)(2,1)S(1)}, bf16[1,1601,256]{2,1,0:T(8,128)(2,1)S(1)}, u32[]{:S(2)}, u32[]{:S(2)}) collective-permute-start(bf16[1,1601,256]{2,1,0:T(8,128)(2,1)S(1)} %pad_maximum_fusion), channel_id=1, source_target_pairs={{0,24},{8,32},{16,40},{24,48},{32,56},{40,64},{48,72},{56,80},{64,... | collective-permute-start | bytes 2459144 | tf_op jit(solution)/shard_map/ppermute | solution.py:15
  243.4 57.5 %collective-permute-start.1 = (bf16[1,1601,256]{2,1,0:T(8,128)(2,1)S(1)}, bf16[1,1601,256]{2,1,0:T(8,128)(2,1)S(1)}, u32[]{:S(2)}, u32[]{:S(2)}) collective-permute-start(bf16[1,1601,256]{2,1,0:T(8,128)(2,1)S(1)} %pad_maximum_fusion), channel_id=1, source_target_pairs={{0,16},{8,24},{16,32},{24,40},{32,48},{40,56},{48,64},{56,72},{64,... | collective-permute-start | bytes 2459144 | tf_op jit(solution)/shard_map/ppermute | solution.py:15
  322.8 15.1 %copy-start.3 = (bf16[8005,256]{1,0:T(8,128)(2,1)S(1)}, bf16[8005,256]{1,0:T(8,128)(2,1)}, u32[]{:S(2)}) copy-start(bf16[8005,256]{1,0:T(8,128)(2,1)} %squeeze.19) | copy-start | bytes 12295684
  337.9 17.6 %copy-start.1 = (bf16[1,1601,1024]{2,1,0:T(8,128)(2,1)S(1)}, bf16[1,1601,1024]{2,1,0:T(8,128)(2,1)}, u32[]{:S(2)}) copy-start(bf16[1,1601,1024]{2,1,0:T(8,128)(2,1)} %param.9) | copy-start | bytes 9836548
Sparse Core Ops, SparseCore 0:
  10.1 114.2 all-gather.2
  153.7 79.7 reduce-scatter.1

commit v2 on v1

--- a/solution.py
+++ b/solution.py
@@ -76,19 +76,32 @@
     normed = rms_scale(text_states.astype(jnp.float32), norm_gain).astype(jnp.bfloat16)
     kv_rows, kv_width = image_projection_weight.shape
     query_width = query_weight.shape[1]
-    kv_as_rows = image_projection_weight.reshape(kv_rows * kv_width // query_width, query_width)
+    column_blocks = kv_width // query_width
+    kv_as_rows = (
+        image_projection_weight.reshape(kv_rows, column_blocks, query_width)
+        .transpose(1, 0, 2)
+        .reshape(column_blocks * kv_rows, query_width)
+    )
     both = lax.all_gather(
         jnp.concatenate([kv_as_rows, query_weight], axis=0), "seq", axis=0, tiled=False
     )
-    weight_block = both[:, : kv_as_rows.shape[0]].reshape(-1, kv_width)
-    query_block = both[:, kv_as_rows.shape[0] :].reshape(-1, query_width)
+    query_block = both[:, column_blocks * kv_rows :].reshape(-1, query_width)
     queries = jnp.dot(normed, query_block, preferred_element_type=jnp.float32)
     query_heads = rms_scale(queries.reshape(row_count, heads_local, head_dim), query_gain).astype(
         jnp.bfloat16
     )
     features = images[0]
-    columns = weight_block
-    score_product = jnp.dot(features, columns, preferred_element_type=jnp.float32)
+    score_product = jnp.concatenate(
+        [
+            jnp.dot(
+                features,
+                both[:, block * kv_rows : (block + 1) * kv_rows].reshape(-1, query_width),
+                preferred_element_type=jnp.float32,
+            )
+            for block in range(column_blocks)
+        ],
+        axis=1,
+    )
     own_kv = lax.psum_scatter(
         score_product.reshape(
             features.shape[0], local_key_value * lax.axis_size("fsdp"), 2 * head_dim

time: 369 us -> 360 us (0.976)
  local copies, waits for them, and re-layouts: 51.6 us -> 42 us
    reshape x3 -> x2, local copies, waits for them, and re-layouts: 20.7 us -> 12.9 us  [the longest x1 11.8 us: on_device(): query_block = both[:, column_blocks * kv_rows:].reshape(-1, query_width)]
    dot_general x1 -> x4, matrix products: 9.55 us -> 7.47 us  [on_device(): jnp.dot(features, both[:, block * kv_rows:(block + 1) * kv_rows].reshape(...]
where the time goes in v2:
time: 360 us; the launch traced here: 354 us
  waiting for transfers between devices  215 us (60%)
  matrix products  44.6 us (12%)
  local copies, waits for them, and re-layouts  42 us (12%)
  other arithmetic  26.3 us (7%)
  between operations  13.7 us (4%)
  starting transfers between devices  11.9 us (3%)
    all_gather x1, waiting for transfers between devices, on_device(): lax.all_gather(jnp.concatenate([kv_as_rows, query_weight], axis=0), 'seq'...  115 us
    ppermute x4, waiting for transfers between devices, from_behind(): lax.ppermute(value, axis, [(source, source + steps) for source in range(i...  51.2 us
    reduce_scatter x1, waiting for transfers between devices, on_device(): lax.psum_scatter(score_product.reshape(features.shape[0], local_key_value...  49 us
    dot_general x1, matrix products, one_head(): jnp.dot(weights.astype(jnp.bfloat16), key_value_pair[:, head_dim:], prefe...  16.6 us
    reduce_sum x1, other arithmetic, one_head(): row_total = jnp.sum(weights, axis=1, keepdims=True)  15.1 us
    dot_general x1, matrix products, one_head(): lax.dot_general(query_rows, key_value_pair[:, :head_dim], (((1,), (1,)),...  13.8 us
    ppermute x4, starting transfers between devices, from_behind(): lax.ppermute(value, axis, [(source, source + steps) for source in range(i...  11.8 us
    reshape x1, local copies, waits for them, and re-layouts, on_device(): query_block = both[:, column_blocks * kv_rows:].reshape(-1, query_width)  11.8 us
  transfers between devices with their start and end apart: 6, of which 4 were waited for; matrix products, arithmetic and copies ran while one was open for 10% of the time, Pallas kernels for 0%

profile of v2, /device:TPU:133, one launch (start us, length us, event | category | flops | bytes accessed | tf_op | source)
XLA Modules:
  0.0 353.6 jit_solution(9674289110483211452)
XLA Ops:
  9.5 114.9 %all-gather.3.cloned.1.call-done = bf16[12288,512]{1,0:T(8,128)(2,1)} async-done(((bf16[384,512]{1,0:T(8,128)(2,1)}), bf16[12288,512]{1,0:T(8,128)(2,1)}) %all-gather.3.cloned.1.call-update) | async-done | bytes 12582928 | tf_op jit(solution)/shard_map/all_gather | solution.py:85
  124.4 2.5 fusion.61
  127.0 1.9 fusion.34
  128.9 1.9 fusion.43
  130.8 1.9 fusion.37
  132.6 1.9 fusion.40
  134.5 2.8 pad_maximum_fusion
  137.3 2.9 copy.22
  140.7 4.1 %copy.26 = bf16[1601,8,256]{2,0,1:T(8,128)(2,1)} copy(bf16[1601,8,256]{2,1,0:T(8,128)(2,1)S(1)} %slice.49) | data formatting | bytes 13115392 | tf_op jit(solution)/shard_map/convert_element_type | solution.py:110
  146.3 3.1 fusion.6
  149.4 7.5 %slice.40 = bf16[32,256,512]{2,1,0:T(8,128)(2,1)} slice(bf16[32,384,512]{2,1,0:T(8,128)(2,1)} %bitcast.96), slice={[0:32], [128:384], [0:512]} | slice | bytes 16777216 | tf_op jit(solution)/shard_map/slice | solution.py:88
  156.9 11.8 %copy.21 = bf16[8192,512]{0,1:T(8,128)(2,1)} copy(bf16[8192,512]{1,0:T(8,128)(2,1)} %bitcast.91) | data formatting | bytes 16777216 | tf_op jit(solution)/shard_map/reshape | solution.py:88
  168.7 6.7 %multiply_reduce_fusion.1 = (f32[256,4]{0,1:T(4,128)S(1)}, f32[256,4,128]{2,0,1:T(8,128)S(1)}) fusion(bf16[4,128,8192]{2,1,0:T(8,128)(2,1)} %bitcast.97, bf16[256,8192]{1,0:T(8,128)(2,1)} %param.8, f32[8192]{0:T(1024)S(1)} %copy-done.7, f32[256]{0:T(256)S(1)} %add_rsqrt_fusion.2), kind=kOutput, calls=%fused_computation.50 | convolution fusion | flops 2156133376 | bytes 13145088 | tf_op jit(solution)/shard_map/dot_general | solution.py:89
  175.7 49.0 %reduce-scatter.2.cloned.1.call-done = bf16[1,1601,256]{2,1,0:T(8,128)(2,1)} async-done(((bf16[8,1601,256]{2,1,0:T(8,128)(2,1)}), bf16[1,1601,256]{2,1,0:T(8,128)(2,1)}) %reduce-scatter.2.cloned.1.call-update) | async-done | bytes 819728 | tf_op jit(solution)/shard_map/reduce_scatter | solution.py:105
  226.9 3.1 collective-permute-start
  230.2 2.3 collective-permute-start.3
  232.5 1.9 collective-permute-start.2
  234.5 4.5 %collective-permute-start.1 = (bf16[1,1601,256]{2,1,0:T(8,128)(2,1)S(1)}, bf16[1,1601,256]{2,1,0:T(8,128)(2,1)S(1)}, u32[]{:S(2)}, u32[]{:S(2)}) collective-permute-start(bf16[1,1601,256]{2,1,0:T(8,128)(2,1)S(1)} %pad_maximum_fusion.1), channel_id=1, source_target_pairs={{0,16},{8,24},{16,32},{24,40},{32,48},{40,56},{48,64},{56,72},{64,... | collective-permute-start | bytes 2459144 | tf_op jit(solution)/shard_map/ppermute | solution.py:15
  240.0 5.5 %collective-permute-done = bf16[1,1601,256]{2,1,0:T(8,128)(2,1)S(1)} collective-permute-done((bf16[1,1601,256]{2,1,0:T(8,128)(2,1)S(1)}, bf16[1,1601,256]{2,1,0:T(8,128)(2,1)S(1)}, u32[]{:S(2)}, u32[]{:S(2)}) %collective-permute-start) | collective-permute-done | bytes 819744 | tf_op jit(solution)/shard_map/ppermute | solution.py:15
  246.5 45.7 %collective-permute-done.1 = bf16[1,1601,256]{2,1,0:T(8,128)(2,1)S(1)} collective-permute-done((bf16[1,1601,256]{2,1,0:T(8,128)(2,1)S(1)}, bf16[1,1601,256]{2,1,0:T(8,128)(2,1)S(1)}, u32[]{:S(2)}, u32[]{:S(2)}) %collective-permute-start.1) | collective-permute-done | bytes 819744 | tf_op jit(solution)/shard_map/ppermute | solution.py:15
  295.1 5.2 %squeeze.19 = bf16[8005,256]{1,0:T(8,128)(2,1)} reshape(bf16[5,1,1601,256]{3,2,1,0:T(8,128)(2,1)} %bitcast_dynamic-update-slice_fusion) | data formatting | bytes 8197120 | tf_op jit(solution)/shard_map/while/body/jit(dynamic_index_in_dim)/squeeze | solution.py:57
  300.3 13.8 %fusion = (f32[1024]{0:T(1024)S(1)}, f32[1024,8005]{0,1:T(8,128)}) fusion(pred[8005]{0:T(1024)(128)(4,1)S(1)} %broadcast_in_dim.38, bf16[1024,128]{1,0:T(8,128)(2,1)S(1)} %bitcast.98, bf16[8005,256]{1,0:T(8,128)(2,1)} %squeeze.19), kind=kOutput, calls=%fused_computation.3 | convolution fusion | flops 2123053056 | bytes 35112772 | tf_op jit(solution)/shard_map/while/body/eval_jaxpr/dot_general | solution.py:38
  314.1 15.1 %fusion.1 = f32[1024]{0:T(1024)S(1)} fusion(f32[1024,8005]{0,1:T(8,128)} %get-tuple-element.27, f32[1024]{0:T(1024)S(1)} %get-tuple-element.26, pred[8005]{0:T(1024)(128)(4,1)S(1)} %broadcast_in_dim.38), kind=kLoop, calls=%fused_computation.4 | loop fusion | flops 32787456 | bytes 32804676 | tf_op jit(solution)/shard_map/while/body/eval_jaxpr/reduce_sum | solution.py:49
  329.2 16.6 %fusion.54 = bf16[1024,128]{1,0:T(8,128)(2,1)S(1)} fusion(bf16[8005,256]{1,0:T(8,128)(2,1)S(1)} %copy-done.3, f32[1024,8005]{0,1:T(8,128)} %get-tuple-element.27, f32[1024]{0:T(1024)S(1)} %get-tuple-element.26, pred[8005]{0:T(1024)(128)(4,1)S(1)} %broadcast_in_dim.38, f32[1024]{0:T(1024)S(1)} %fusion.1), kind=kOutput, calls=%fused_computation.39 | convolution fusion | flops 2131513344 | bytes 35117056 | tf_op jit(solution)/shard_map/while/body/eval_jaxpr/dot_general | solution.py:50
  (51 shorter events, 13.4 us)
Async XLA Ops:
  6.5 120.5 %copy-start = (bf16[1,1601,1024]{2,1,0:T(8,128)(2,1)S(1)}, bf16[1,1601,1024]{2,1,0:T(8,128)(2,1)}, u32[]{:S(2)}) copy-start(bf16[1,1601,1024]{2,1,0:T(8,128)(2,1)} %param.9) | copy-start | bytes 9836548
  6.5 117.9 %all-gather.3.cloned.1.call-start = ((), (), s32[]{:S(2)}) async-start(), calls=%async_computation.2 | async-start | bytes 12976128 | tf_op jit(solution)/shard_map/all_gather | solution.py:85
  9.5 215.2 %reduce-scatter.2.cloned.1.call-start = ((), (), s32[]{:S(2)}) async-start(), calls=%async_computation.1 | async-start | bytes 7409664 | tf_op jit(solution)/shard_map/reduce_scatter | solution.py:105
  144.8 0.7 copy-start.2
  156.9 11.8 %copy-start.7 = (f32[8192]{0:T(1024)S(1)}, f32[8192]{0:T(1024)}, u32[]{:S(2)}) copy-start(f32[8192]{0:T(1024)} %param.10) | copy-start | bytes 98308
  168.7 6.8 %copy-start.6 = (f32[128]{0:T(128)S(1)}, f32[128]{0:T(128)}, u32[]{:S(2)}) copy-start(f32[128]{0:T(128)} %param.13) | copy-start | bytes 1540
  168.7 57.7 %copy-start.5 = (f32[128]{0:T(128)S(1)}, f32[128]{0:T(128)}, u32[]{:S(2)}) copy-start(f32[128]{0:T(128)} %param.14) | copy-start | bytes 1540
  224.7 2.0 slice-start
  224.7 14.3 %copy-start.4 = (bf16[1,1601,256]{2,1,0:T(8,128)(2,1)S(1)}, bf16[1,1601,256]{2,1,0:T(8,128)(2,1)}, u32[]{:S(2)}) copy-start(bf16[1,1601,256]{2,1,0:T(8,128)(2,1)} %reduce-scatter.2.cloned.1.call-done) | copy-start | bytes 2459140
  226.9 18.7 %collective-permute-start = (bf16[1,1601,256]{2,1,0:T(8,128)(2,1)S(1)}, bf16[1,1601,256]{2,1,0:T(8,128)(2,1)S(1)}, u32[]{:S(2)}, u32[]{:S(2)}) collective-permute-start(bf16[1,1601,256]{2,1,0:T(8,128)(2,1)S(1)} %pad_maximum_fusion.1), channel_id=1, source_target_pairs={{0,8},{8,16},{16,24},{24,32},{32,40},{40,48},{48,56},{56,64},{64,7... | collective-permute-start | bytes 2459144 | tf_op jit(solution)/shard_map/ppermute | solution.py:15
  230.2 63.9 %collective-permute-start.3 = (bf16[1,1601,256]{2,1,0:T(8,128)(2,1)S(1)}, bf16[1,1601,256]{2,1,0:T(8,128)(2,1)S(1)}, u32[]{:S(2)}, u32[]{:S(2)}) collective-permute-start(bf16[1,1601,256]{2,1,0:T(8,128)(2,1)S(1)} %pad_maximum_fusion.1), channel_id=1, source_target_pairs={{0,32},{8,40},{16,48},{24,56},{32,64},{40,72},{48,80},{56,88},{64,... | collective-permute-start | bytes 2459144 | tf_op jit(solution)/shard_map/ppermute | solution.py:15
  232.5 60.6 %collective-permute-start.2 = (bf16[1,1601,256]{2,1,0:T(8,128)(2,1)S(1)}, bf16[1,1601,256]{2,1,0:T(8,128)(2,1)S(1)}, u32[]{:S(2)}, u32[]{:S(2)}) collective-permute-start(bf16[1,1601,256]{2,1,0:T(8,128)(2,1)S(1)} %pad_maximum_fusion.1), channel_id=1, source_target_pairs={{0,24},{8,32},{16,40},{24,48},{32,56},{40,64},{48,72},{56,80},{64,... | collective-permute-start | bytes 2459144 | tf_op jit(solution)/shard_map/ppermute | solution.py:15
  234.5 57.7 %collective-permute-start.1 = (bf16[1,1601,256]{2,1,0:T(8,128)(2,1)S(1)}, bf16[1,1601,256]{2,1,0:T(8,128)(2,1)S(1)}, u32[]{:S(2)}, u32[]{:S(2)}) collective-permute-start(bf16[1,1601,256]{2,1,0:T(8,128)(2,1)S(1)} %pad_maximum_fusion.1), channel_id=1, source_target_pairs={{0,16},{8,24},{16,32},{24,40},{32,48},{40,56},{48,64},{56,72},{64,... | collective-permute-start | bytes 2459144 | tf_op jit(solution)/shard_map/ppermute | solution.py:15
  314.1 15.1 %copy-start.3 = (bf16[8005,256]{1,0:T(8,128)(2,1)S(1)}, bf16[8005,256]{1,0:T(8,128)(2,1)}, u32[]{:S(2)}) copy-start(bf16[8005,256]{1,0:T(8,128)(2,1)} %squeeze.19) | copy-start | bytes 12295684
  329.2 17.6 %copy-start.1 = (bf16[1,1601,1024]{2,1,0:T(8,128)(2,1)S(1)}, bf16[1,1601,1024]{2,1,0:T(8,128)(2,1)}, u32[]{:S(2)}) copy-start(bf16[1,1601,1024]{2,1,0:T(8,128)(2,1)} %param.9) | copy-start | bytes 9836548
Sparse Core Ops, SparseCore 0:
  10.1 114.2 all-gather.2
  145.0 79.7 reduce-scatter.1

commit v3 on v2

--- a/solution.py
+++ b/solution.py
@@ -19,42 +19,39 @@
     return values * lax.rsqrt(jnp.mean(values * values, axis=-1, keepdims=True) + 1e-05) * gain
 
 
-def attend(query_heads, stacked, admitted):
-    slot_count, kv_heads, image_tokens, double_width = stacked.shape
+def attend_part(grouped, key_value_pair, column_live):
+    head_dim = grouped.shape[-1]
+    scores = jnp.einsum(
+        "kqd,knd->kqn", grouped, key_value_pair[..., :head_dim], preferred_element_type=jnp.float32
+    ) * (1.0 / math.sqrt(head_dim))
+    scores = jnp.where(column_live[None, None, :], scores, -jnp.inf)
+    row_peak = jnp.max(scores, axis=-1, keepdims=True)
+    weights = jnp.exp(scores - jnp.where(row_peak == -jnp.inf, 0.0, row_peak))
+    row_total = jnp.sum(weights, axis=-1, keepdims=True)
+    blended = jnp.einsum(
+        "kqn,knd->kqd",
+        weights.astype(jnp.bfloat16),
+        key_value_pair[..., head_dim:],
+        preferred_element_type=jnp.float32,
+    )
+    return row_peak, row_total, blended
+
+
+def attend(query_heads, own, own_live, earlier, earlier_live):
+    kv_heads, _, double_width = own.shape
     head_dim = double_width // 2
     row_count, heads_local, _ = query_heads.shape
     heads_per_group = heads_local // kv_heads
     grouped = query_heads.reshape(row_count, kv_heads, heads_per_group, head_dim)
     grouped = grouped.transpose(1, 2, 0, 3).reshape(kv_heads, heads_per_group * row_count, head_dim)
-    per_head = jnp.moveaxis(stacked, 1, 0).reshape(
-        kv_heads, slot_count * image_tokens, double_width
+    own_peak, own_total, own_blend = attend_part(grouped, own, own_live)
+    far_peak, far_total, far_blend = attend_part(grouped, earlier, earlier_live)
+    peak = jnp.maximum(own_peak, far_peak)
+    own_scale = jnp.exp(own_peak - peak)
+    far_scale = jnp.exp(far_peak - peak)
+    outputs = (own_blend * own_scale + far_blend * far_scale) / (
+        own_total * own_scale + far_total * far_scale
     )
-    column_live = jnp.repeat(admitted, image_tokens)
-    score_scale = 1.0 / math.sqrt(head_dim)
-
-    def one_head(operands):
-        query_rows, key_value_pair = operands
-        scores = (
-            lax.dot_general(
-                query_rows,
-                key_value_pair[:, :head_dim],
-                (((1,), (1,)), ((), ())),
-                preferred_element_type=jnp.float32,
-            )
-            * score_scale
-        )
-        scores = jnp.where(column_live[None, :], scores, -jnp.inf)
-        row_peak = jnp.max(scores, axis=1, keepdims=True)
-        weights = jnp.exp(scores - row_peak)
-        row_total = jnp.sum(weights, axis=1, keepdims=True)
-        blended = jnp.dot(
-            weights.astype(jnp.bfloat16),
-            key_value_pair[:, head_dim:],
-            preferred_element_type=jnp.float32,
-        )
-        return blended / row_total
-
-    outputs = lax.map(one_head, (grouped, per_head))
     outputs = outputs.reshape(kv_heads, heads_per_group, row_count, head_dim).transpose(2, 0, 1, 3)
     return outputs.reshape(row_count, heads_local * head_dim).astype(jnp.bfloat16)
 
@@ -114,14 +111,31 @@
     ).astype(jnp.float32)
     key_part = rms_scale(own_kv[..., :head_dim], key_gain)
     packed = jnp.concatenate([key_part, own_kv[..., head_dim:]], axis=-1).astype(jnp.bfloat16)
-    image_window = [packed]
-    for distance in range(1, IMAGE_LOOKBACK + 1):
-        image_window.append(from_behind(packed, "seq", distance))
-    stacked = jnp.stack(image_window)
     span_index = lax.axis_index("seq")
     image_ids = span_index - jnp.arange(IMAGE_LOOKBACK + 1, dtype=jnp.int32)
     admitted = (image_ids >= 0) & (jnp.take(admission[0], jnp.maximum(image_ids, 0)) == 1)
-    return attend(query_heads, stacked, admitted)
+    earlier_admitted = admitted[1:]
+    nearest = jnp.argmax(earlier_admitted)
+    farthest = IMAGE_LOOKBACK - 1 - jnp.argmax(earlier_admitted[::-1])
+    admitted_count = jnp.sum(earlier_admitted.astype(jnp.int32))
+    received = [from_behind(packed, "seq", distance) for distance in range(1, IMAGE_LOOKBACK + 1)]
+
+    def pick(slot):
+        chosen = received[-1]
+        for distance in range(IMAGE_LOOKBACK - 2, -1, -1):
+            chosen = jnp.where(slot == distance, received[distance], chosen)
+        return chosen
+
+    earlier = jnp.concatenate([pick(nearest), pick(farthest)], axis=1)
+    image_tokens = packed.shape[1]
+    earlier_live = jnp.concatenate(
+        [
+            jnp.broadcast_to(admitted_count >= 1, (image_tokens,)),
+            jnp.broadcast_to(admitted_count >= 2, (image_tokens,)),
+        ]
+    )
+    own_live = jnp.broadcast_to(admitted[0], (image_tokens,))
+    return attend(query_heads, packed, own_live, earlier, earlier_live)
 
 
 def solution(mesh):

time: 360 us -> 319 us (0.89)
  matrix products: 44.6 us -> 23.4 us
  other arithmetic: 26.3 us -> 17.9 us
  waiting for transfers between devices: 215 us -> 207 us
  local copies, waits for them, and re-layouts: 42 us -> 34.5 us
  between operations: 13.7 us -> 17.4 us
    dot_general x2 -> x4, matrix products: 30.4 us -> 9.21 us  [the longest x2 6.12 us: attend_part(): jnp.einsum('kqn,knd->kqd', weights.astype(jnp.bfloat16), key_value_pair[....]
    reduce_sum x1 -> x3, other arithmetic: 15.1 us -> 5.63 us  [the longest x2 4.92 us: attend_part(): row_total = jnp.sum(weights, axis=-1, keepdims=True)]
    reduce_scatter x1, waiting for transfers between devices: 49 us -> 42.6 us  [on_device(): lax.psum_scatter(score_product.reshape(features.shape[0], local_key_value...]
    squeeze x1 -> x0, local copies, waits for them, and re-layouts: 5.2 us -> none  [attend(): outputs = lax.map(one_head, (grouped, per_head))]
  transfers between devices with their start and end apart: 6 -> 6, of which waited for: 4 -> 6; matrix products, arithmetic and copies ran while one was open for 10% -> 11% of each run, Pallas kernels for 0% -> 0%
where the time goes in v3:
time: 319 us; the launch traced here: 313 us
  waiting for transfers between devices  207 us (65%)
  local copies, waits for them, and re-layouts  34.5 us (11%)
  matrix products  23.4 us (7%)
  other arithmetic  17.9 us (6%)
  between operations  17.4 us (5%)
  starting transfers between devices  12.6 us (4%)
    all_gather x1, waiting for transfers between devices, on_device(): lax.all_gather(jnp.concatenate([kv_as_rows, query_weight], axis=0), 'seq'...  115 us
    ppermute x4, waiting for transfers between devices, from_behind(): lax.ppermute(value, axis, [(source, source + steps) for source in range(i...  49.5 us
    reduce_scatter x1, waiting for transfers between devices, on_device(): lax.psum_scatter(score_product.reshape(features.shape[0], local_key_value...  42.6 us
    ppermute x4, starting transfers between devices, from_behind(): lax.ppermute(value, axis, [(source, source + steps) for source in range(i...  12.5 us
    reshape x1, local copies, waits for them, and re-layouts, on_device(): query_block = both[:, column_blocks * kv_rows:].reshape(-1, query_width)  12 us
    slice x1, local copies, waits for them, and re-layouts, on_device(): query_block = both[:, column_blocks * kv_rows:].reshape(-1, query_width)  7.88 us
    dot_general x4, matrix products, on_device(): jnp.dot(features, both[:, block * kv_rows:(block + 1) * kv_rows].reshape(...  7.47 us
    dot_general x1, matrix products, on_device(): queries = jnp.dot(normed, query_block, preferred_element_type=jnp.float32)  6.72 us
  transfers between devices with their start and end apart: 6, of which 6 were waited for; matrix products, arithmetic and copies ran while one was open for 11% of the time, Pallas kernels for 0%

profile of v3, /device:TPU:133, one launch (start us, length us, event | category | flops | bytes accessed | tf_op | source)
XLA Modules:
  0.0 313.1 jit_solution(9970453757251791114)
XLA Ops:
  9.5 115.2 %all-gather.3.cloned.1.call-done = bf16[12288,512]{1,0:T(8,128)(2,1)} async-done(((bf16[384,512]{1,0:T(8,128)(2,1)}), bf16[12288,512]{1,0:T(8,128)(2,1)}) %all-gather.3.cloned.1.call-update) | async-done | bytes 12582928 | tf_op jit(solution)/shard_map/all_gather | solution.py:82
  124.7 2.5 fusion.91
  127.3 1.9 fusion.40
  129.2 1.9 fusion.49
  131.0 1.9 fusion.43
  134.8 2.8 pad_maximum_fusion
  137.6 2.9 copy.17
  141.0 4.1 %copy.21 = bf16[1601,8,256]{2,0,1:T(8,128)(2,1)} copy(bf16[1601,8,256]{2,1,0:T(8,128)(2,1)S(1)} %slice.65) | data formatting | bytes 13115392 | tf_op jit(solution)/shard_map/convert_element_type | solution.py:107
  152.5 3.1 fusion.3
  155.6 7.9 %slice.56 = bf16[32,256,512]{2,1,0:T(8,128)(2,1)} slice(bf16[32,384,512]{2,1,0:T(8,128)(2,1)} %bitcast.103), slice={[0:32], [128:384], [0:512]} | slice | bytes 16777216 | tf_op jit(solution)/shard_map/slice | solution.py:85
  163.5 12.0 %copy.16 = bf16[8192,512]{0,1:T(8,128)(2,1)} copy(bf16[8192,512]{1,0:T(8,128)(2,1)} %bitcast.98) | data formatting | bytes 16777216 | tf_op jit(solution)/shard_map/reshape | solution.py:85
  175.4 6.7 %multiply_reduce_fusion = (f32[256,4]{0,1:T(4,128)S(1)}, f32[256,4,128]{2,0,1:T(8,128)S(1)}) fusion(bf16[4,128,8192]{2,1,0:T(8,128)(2,1)} %bitcast.104, bf16[256,8192]{1,0:T(8,128)(2,1)} %param.8, f32[8192]{0:T(1024)S(1)} %copy-done.6, f32[256]{0:T(256)S(1)} %add_rsqrt_fusion.2), kind=kOutput, calls=%fused_computation.64 | convolution fusion | flops 2156133376 | bytes 13145088 | tf_op jit(solution)/shard_map/dot_general | solution.py:86
  182.4 42.6 %reduce-scatter.2.cloned.1.call-done = bf16[1,1601,256]{2,1,0:T(8,128)(2,1)} async-done(((bf16[8,1601,256]{2,1,0:T(8,128)(2,1)}), bf16[1,1601,256]{2,1,0:T(8,128)(2,1)}) %reduce-scatter.2.cloned.1.call-update) | async-done | bytes 819728 | tf_op jit(solution)/shard_map/reduce_scatter | solution.py:102
  228.7 2.3 collective-permute-start.3
  231.0 3.1 collective-permute-start.2
  234.1 2.6 collective-permute-start.1
  236.7 4.6 %collective-permute-start = (bf16[1,1601,256]{2,1,0:T(8,128)(2,1)S(1)}, bf16[1,1601,256]{2,1,0:T(8,128)(2,1)S(1)}, u32[]{:S(2)}, u32[]{:S(2)}) collective-permute-start(bf16[1,1601,256]{2,1,0:T(8,128)(2,1)S(1)} %pad_maximum_fusion.1), channel_id=1, source_target_pairs={{0,8},{8,16},{16,24},{24,32},{32,40},{40,48},{48,56},{56,64},{64,7... | collective-permute-start | bytes 2459144 | tf_op jit(solution)/shard_map/ppermute | solution.py:15
  243.8 7.3 %collective-permute-done.3 = bf16[1,1601,256]{2,1,0:T(8,128)(2,1)S(1)} collective-permute-done((bf16[1,1601,256]{2,1,0:T(8,128)(2,1)S(1)}, bf16[1,1601,256]{2,1,0:T(8,128)(2,1)S(1)}, u32[]{:S(2)}, u32[]{:S(2)}) %collective-permute-start.3) | collective-permute-done | bytes 819744 | tf_op jit(solution)/shard_map/ppermute | solution.py:15
  251.1 14.6 %collective-permute-done.2 = bf16[1,1601,256]{2,1,0:T(8,128)(2,1)S(1)} collective-permute-done((bf16[1,1601,256]{2,1,0:T(8,128)(2,1)S(1)}, bf16[1,1601,256]{2,1,0:T(8,128)(2,1)S(1)}, u32[]{:S(2)}, u32[]{:S(2)}) %collective-permute-start.2) | collective-permute-done | bytes 819744 | tf_op jit(solution)/shard_map/ppermute | solution.py:15
  265.7 17.6 %collective-permute-done.1 = bf16[1,1601,256]{2,1,0:T(8,128)(2,1)S(1)} collective-permute-done((bf16[1,1601,256]{2,1,0:T(8,128)(2,1)S(1)}, bf16[1,1601,256]{2,1,0:T(8,128)(2,1)S(1)}, u32[]{:S(2)}, u32[]{:S(2)}) %collective-permute-start.1) | collective-permute-done | bytes 819744 | tf_op jit(solution)/shard_map/ppermute | solution.py:15
  283.4 9.9 %collective-permute-done = bf16[1,1601,256]{2,1,0:T(8,128)(2,1)S(1)} collective-permute-done((bf16[1,1601,256]{2,1,0:T(8,128)(2,1)S(1)}, bf16[1,1601,256]{2,1,0:T(8,128)(2,1)S(1)}, u32[]{:S(2)}, u32[]{:S(2)}) %collective-permute-start) | collective-permute-done | bytes 819744 | tf_op jit(solution)/shard_map/ppermute | solution.py:15
  293.5 2.0 fusion
  295.5 3.6 %fusion.1 = f32[1024]{0:T(1024)S(1)} fusion(f32[1024,3202]{0,1:T(8,128)S(1)} %get-tuple-element.21, f32[1024]{0:T(1024)S(1)} %compare_select_fusion, pred[3202]{0:T(1024)(128)(4,1)S(1)} %concatenate.27), kind=kLoop, calls=%fused_computation.6 | loop fusion | flops 13114368 | bytes 13126786 | tf_op jit(solution)/shard_map/reduce_sum | solution.py:30
  299.1 4.4 %fusion.58 = f32[1024,128]{1,0:T(8,128)S(1)} fusion(f32[1024,3202]{0,1:T(8,128)S(1)} %get-tuple-element.21, f32[1024]{0:T(1024)S(1)} %compare_select_fusion, pred[3202]{0:T(1024)(128)(4,1)S(1)} %concatenate.27, bf16[1,1601,256]{2,1,0:T(8,128)(2,1)S(1)} %get-tuple-element.16, bf16[1,1601,256]{2,1,0:T(8,128)(2,1)S(1)} %get-tuple-element.17, ...), kind=kOutput, calls=%fused_computation.46 | convolution fusion | flops 854270976 | bytes 15290498 | tf_op jit(solution)/shard_map/kqn,knd->kqd/dot_general | solution.py:31
  (51 shorter events, 18.3 us)
Async XLA Ops:
  6.5 120.7 %copy-start = (bf16[1,1601,1024]{2,1,0:T(8,128)(2,1)S(1)}, bf16[1,1601,1024]{2,1,0:T(8,128)(2,1)}, u32[]{:S(2)}) copy-start(bf16[1,1601,1024]{2,1,0:T(8,128)(2,1)} %param.9) | copy-start | bytes 9836548
  6.5 118.2 %all-gather.3.cloned.1.call-start = ((), (), s32[]{:S(2)}) async-start(), calls=%async_computation.2 | async-start | bytes 12976128 | tf_op jit(solution)/shard_map/all_gather | solution.py:82
  9.5 215.5 %reduce-scatter.2.cloned.1.call-start = ((), (), s32[]{:S(2)}) async-start(), calls=%async_computation.1 | async-start | bytes 7409664 | tf_op jit(solution)/shard_map/reduce_scatter | solution.py:102
  145.1 0.7 copy-start.2
  163.5 12.0 %copy-start.6 = (f32[8192]{0:T(1024)S(1)}, f32[8192]{0:T(1024)}, u32[]{:S(2)}) copy-start(f32[8192]{0:T(1024)} %param.10) | copy-start | bytes 98308
  175.4 6.7 %copy-start.4 = (f32[128]{0:T(128)S(1)}, f32[128]{0:T(128)}, u32[]{:S(2)}) copy-start(f32[128]{0:T(128)} %param.13) | copy-start | bytes 1540
  175.4 51.9 %copy-start.5 = (f32[128]{0:T(128)S(1)}, f32[128]{0:T(128)}, u32[]{:S(2)}) copy-start(f32[128]{0:T(128)} %param.14) | copy-start | bytes 1540
  228.7 22.3 %collective-permute-start.3 = (bf16[1,1601,256]{2,1,0:T(8,128)(2,1)S(1)}, bf16[1,1601,256]{2,1,0:T(8,128)(2,1)S(1)}, u32[]{:S(2)}, u32[]{:S(2)}) collective-permute-start(bf16[1,1601,256]{2,1,0:T(8,128)(2,1)S(1)} %pad_maximum_fusion.1), channel_id=1, source_target_pairs={{0,32},{8,40},{16,48},{24,56},{32,64},{40,72},{48,80},{56,88},{64,... | collective-permute-start | bytes 2459144 | tf_op jit(solution)/shard_map/ppermute | solution.py:15
  231.0 34.7 %collective-permute-start.2 = (bf16[1,1601,256]{2,1,0:T(8,128)(2,1)S(1)}, bf16[1,1601,256]{2,1,0:T(8,128)(2,1)S(1)}, u32[]{:S(2)}, u32[]{:S(2)}) collective-permute-start(bf16[1,1601,256]{2,1,0:T(8,128)(2,1)S(1)} %pad_maximum_fusion.1), channel_id=1, source_target_pairs={{0,24},{8,32},{16,40},{24,48},{32,56},{40,64},{48,72},{56,80},{64,... | collective-permute-start | bytes 2459144 | tf_op jit(solution)/shard_map/ppermute | solution.py:15
  234.1 49.3 %collective-permute-start.1 = (bf16[1,1601,256]{2,1,0:T(8,128)(2,1)S(1)}, bf16[1,1601,256]{2,1,0:T(8,128)(2,1)S(1)}, u32[]{:S(2)}, u32[]{:S(2)}) collective-permute-start(bf16[1,1601,256]{2,1,0:T(8,128)(2,1)S(1)} %pad_maximum_fusion.1), channel_id=1, source_target_pairs={{0,16},{8,24},{16,32},{24,40},{32,48},{40,56},{48,64},{56,72},{64,... | collective-permute-start | bytes 2459144 | tf_op jit(solution)/shard_map/ppermute | solution.py:15
  236.7 56.6 %collective-permute-start = (bf16[1,1601,256]{2,1,0:T(8,128)(2,1)S(1)}, bf16[1,1601,256]{2,1,0:T(8,128)(2,1)S(1)}, u32[]{:S(2)}, u32[]{:S(2)}) collective-permute-start(bf16[1,1601,256]{2,1,0:T(8,128)(2,1)S(1)} %pad_maximum_fusion.1), channel_id=1, source_target_pairs={{0,8},{8,16},{16,24},{24,32},{32,40},{40,48},{48,56},{56,64},{64,7... | collective-permute-start | bytes 2459144 | tf_op jit(solution)/shard_map/ppermute | solution.py:15
  299.1 4.5 %copy-start.3 = (bf16[1,1601,256]{2,1,0:T(8,128)(2,1)S(1)}, bf16[1,1601,256]{2,1,0:T(8,128)(2,1)}, u32[]{:S(2)}) copy-start(bf16[1,1601,256]{2,1,0:T(8,128)(2,1)} %reduce-scatter.2.cloned.1.call-done) | copy-start | bytes 2459140
  303.6 2.7 copy-start.1
Sparse Core Ops, SparseCore 0:
  10.1 114.5 all-gather.2
  145.2 79.7 reduce-scatter.1

commit v4 on v3

--- a/solution.py
+++ b/solution.py
@@ -71,44 +71,27 @@
     heads_local = query_weight.shape[1] // head_dim
     row_count = text_states.shape[0]
     normed = rms_scale(text_states.astype(jnp.float32), norm_gain).astype(jnp.bfloat16)
-    kv_rows, kv_width = image_projection_weight.shape
-    query_width = query_weight.shape[1]
-    column_blocks = kv_width // query_width
-    kv_as_rows = (
-        image_projection_weight.reshape(kv_rows, column_blocks, query_width)
-        .transpose(1, 0, 2)
-        .reshape(column_blocks * kv_rows, query_width)
+    weight_block = lax.all_gather(image_projection_weight, "seq", axis=0, tiled=True)
+    query_block = lax.all_gather(query_weight, "seq", axis=0, tiled=True)
+    features = images[0]
+    pair_width = 2 * head_dim
+    head_count = weight_block.shape[1] // pair_width
+    partials = jnp.stack(
+        [
+            jnp.dot(
+                features,
+                weight_block[:, head * pair_width : (head + 1) * pair_width],
+                preferred_element_type=jnp.float32,
+            ).astype(jnp.bfloat16)
+            for head in range(head_count)
+        ]
     )
-    both = lax.all_gather(
-        jnp.concatenate([kv_as_rows, query_weight], axis=0), "seq", axis=0, tiled=False
-    )
-    query_block = both[:, column_blocks * kv_rows :].reshape(-1, query_width)
+    gathered_partials = lax.all_to_all(partials, "fsdp", 0, 0, tiled=True)
+    own_kv = jnp.sum(gathered_partials.astype(jnp.float32), axis=0, keepdims=True)
     queries = jnp.dot(normed, query_block, preferred_element_type=jnp.float32)
     query_heads = rms_scale(queries.reshape(row_count, heads_local, head_dim), query_gain).astype(
         jnp.bfloat16
     )
-    features = images[0]
-    score_product = jnp.concatenate(
-        [
-            jnp.dot(
-                features,
-                both[:, block * kv_rows : (block + 1) * kv_rows].reshape(-1, query_width),
-                preferred_element_type=jnp.float32,
-            )
-            for block in range(column_blocks)
-        ],
-        axis=1,
-    )
-    own_kv = lax.psum_scatter(
-        score_product.reshape(
-            features.shape[0], local_key_value * lax.axis_size("fsdp"), 2 * head_dim
-        )
-        .transpose(1, 0, 2)
-        .astype(jnp.bfloat16),
-        "fsdp",
-        scatter_dimension=0,
-        tiled=True,
-    ).astype(jnp.float32)
     key_part = rms_scale(own_kv[..., :head_dim], key_gain)
     packed = jnp.concatenate([key_part, own_kv[..., head_dim:]], axis=-1).astype(jnp.bfloat16)
     span_index = lax.axis_index("seq")

time: 319 us -> 333 us (1.044)
  the two profiles are of different devices: /device:TPU:133 before, /device:TPU:32 now
where the time goes in v4:
time: 333 us; the launch traced here: 332 us
  waiting for transfers between devices  233 us (70%)
  matrix products  35.1 us (11%)
  other arithmetic  22 us (7%)
  starting transfers between devices  17.6 us (5%)
  between operations  17.3 us (5%)
  local copies, waits for them, and re-layouts  7.58 us (2%)
    all_to_all x1, waiting for transfers between devices, on_device(): gathered_partials = lax.all_to_all(partials, 'fsdp', 0, 0, tiled=True)  94.6 us
    all_gather x1, waiting for transfers between devices, on_device(): lax.all_gather(image_projection_weight, 'seq', axis=0, tiled=True)  91 us
    ppermute x4, waiting for transfers between devices, from_behind(): lax.ppermute(value, axis, [(source, source + steps) for source in range(i...  45.7 us
    dot_general x8, matrix products, on_device(): jnp.dot(features, weight_block[:, head * pair_width:(head + 1) * pair_wid...  16.9 us
    ppermute x4, starting transfers between devices, from_behind(): lax.ppermute(value, axis, [(source, source + steps) for source in range(i...  12.6 us
    dot_general x1, matrix products, on_device(): queries = jnp.dot(normed, query_block, preferred_element_type=jnp.float32)  8.04 us
  transfers between devices with their start and end apart: 7, of which 6 were waited for; matrix products, arithmetic and copies ran while one was open for 10% of the time, Pallas kernels for 0%

profile of v4, /device:TPU:32, one launch (start us, length us, event | category | flops | bytes accessed | tf_op | source)
XLA Modules:
  0.0 332.4 jit_solution(16271540887248885853)
XLA Ops:
  8.0 91.0 %all-gather.5.cloned.1.call-done = bf16[1024,2048]{1,0:T(8,128)(2,1)} async-done(((bf16[32,2048]{1,0:T(8,128)(2,1)}), bf16[1024,2048]{1,0:T(8,128)(2,1)}) %all-gather.5.cloned.1.call-update) | async-done | bytes 4194320 | tf_op jit(solution)/shard_map/all_gather | solution.py:74
  99.0 3.1 fusion.104
  102.1 2.0 fusion.98
  106.0 2.0 fusion.86
  110.0 2.0 fusion.74
  115.8 5.0 %all-to-all-start = ((bf16[8,1601,256]{2,1,0:T(8,128)(2,1)}), bf16[8,1601,256]{2,1,0:T(8,128)(2,1)}, u32[]{:S(2)}, u32[]{:S(2)}) async-start(bf16[8,1601,256]{2,1,0:T(8,128)(2,1)} %fusion.62), calls=%async_computation | async-start | bytes 13172736 | tf_op jit(solution)/shard_map/all_to_all | solution.py:89
  122.4 94.6 %all-to-all-done = bf16[8,1601,256]{2,1,0:T(8,128)(2,1)} async-done(((bf16[8,1601,256]{2,1,0:T(8,128)(2,1)}), bf16[8,1601,256]{2,1,0:T(8,128)(2,1)}, u32[]{:S(2)}, u32[]{:S(2)}) %all-to-all-start) | async-done | bytes 6557728 | tf_op jit(solution)/shard_map/all_to_all | solution.py:89
  217.0 4.1 %convert_reduce_fusion = f32[1601,256]{1,0:T(8,128)S(1)} fusion(bf16[8,1601,256]{2,1,0:T(8,128)(2,1)} %all-to-all-done), kind=kLoop, calls=%fused_computation.1 | loop fusion | flops 6147840 | bytes 8197120 | tf_op jit(solution)/shard_map/reduce_sum | solution.py:90
  224.4 2.5 collective-permute-start.3
  228.9 6.1 %collective-permute-start.1 = (bf16[1,1601,256]{2,1,0:T(8,128)(2,1)}, bf16[1,1601,256]{2,1,0:T(8,128)(2,1)}, u32[]{:S(2)}, u32[]{:S(2)}) collective-permute-start(bf16[1,1601,256]{2,1,0:T(8,128)(2,1)} %pad_maximum_fusion), channel_id=1, source_target_pairs={{0,16},{8,24},{16,32},{24,40},{32,48},{40,56},{48,64},{56,72},{64,... | collective-permute-start | bytes 2459144 | tf_op jit(solution)/shard_map/ppermute | solution.py:15
  235.0 2.1 collective-permute-start
  242.2 3.1 fusion.3
  245.3 2.6 collective-permute-done.3
  247.9 7.4 %collective-permute-done.2 = bf16[1,1601,256]{2,1,0:T(8,128)(2,1)} collective-permute-done((bf16[1,1601,256]{2,1,0:T(8,128)(2,1)}, bf16[1,1601,256]{2,1,0:T(8,128)(2,1)}, u32[]{:S(2)}, u32[]{:S(2)}) %collective-permute-start.2) | collective-permute-done | bytes 819744 | tf_op jit(solution)/shard_map/ppermute | solution.py:15
  255.3 28.7 %collective-permute-done.1 = bf16[1,1601,256]{2,1,0:T(8,128)(2,1)} collective-permute-done((bf16[1,1601,256]{2,1,0:T(8,128)(2,1)}, bf16[1,1601,256]{2,1,0:T(8,128)(2,1)}, u32[]{:S(2)}, u32[]{:S(2)}) %collective-permute-start.1) | collective-permute-done | bytes 819744 | tf_op jit(solution)/shard_map/ppermute | solution.py:15
  283.9 7.0 %collective-permute-done = bf16[1,1601,256]{2,1,0:T(8,128)(2,1)} collective-permute-done((bf16[1,1601,256]{2,1,0:T(8,128)(2,1)}, bf16[1,1601,256]{2,1,0:T(8,128)(2,1)}, u32[]{:S(2)}, u32[]{:S(2)}) %collective-permute-start) | collective-permute-done | bytes 819744 | tf_op jit(solution)/shard_map/ppermute | solution.py:15
  291.0 3.2 select_select_fusion
  294.2 8.0 %fusion.152 = (f32[256,512]{1,0:T(8,128)}, f32[256,512]{1,0:T(8,128)}) fusion(bf16[8192,512]{1,0:T(8,128)(2,1)} %all-gather.3.cloned.1.call-done, bf16[256,8192]{1,0:T(8,128)(2,1)} %param.8, f32[8192]{0:T(1024)S(1)} %copy-done.10, f32[256]{0:T(256)S(1)} %add_rsqrt_fusion.2), kind=kOutput, calls=%fused_computation.121 | convolution fusion | flops 2156003328 | bytes 13665280 | tf_op jit(solution)/shard_map/dot_general | solution.py:91
  302.2 2.0 mul.128
  305.7 2.0 reshape.238
  309.1 2.1 fusion.9
  311.2 2.0 fusion
  314.6 3.7 %fusion.1 = f32[1024]{0:T(1024)S(1)} fusion(f32[1024,3202]{0,1:T(8,128)S(1)} %get-tuple-element.17, f32[1024]{0:T(1024)S(1)} %compare_select_fusion, pred[3202]{0:T(1024)(128)(4,1)S(1)} %concatenate.18), kind=kLoop, calls=%fused_computation.7 | loop fusion | flops 13114368 | bytes 13126786 | tf_op jit(solution)/shard_map/reduce_sum | solution.py:30
  318.4 4.4 %fusion.113 = f32[1024,128]{1,0:T(8,128)S(1)} fusion(f32[1024,3202]{0,1:T(8,128)S(1)} %get-tuple-element.17, f32[1024]{0:T(1024)S(1)} %compare_select_fusion, pred[3202]{0:T(1024)(128)(4,1)S(1)} %concatenate.18, bf16[1,1601,256]{2,1,0:T(8,128)(2,1)S(1)} %copy-done.5, bf16[1,1601,256]{2,1,0:T(8,128)(2,1)S(1)} %copy-done.6, f32[1024]{0:T(1024)S(1)} %get-tuple-element.11), kind=kOutput, calls=%fused_computation.68 | convolution fusion | flops 854270976 | bytes 15290498 | tf_op jit(solution)/shard_map/kqn,knd->kqd/dot_general | solution.py:31
  (60 shorter events, 24.3 us)
Async XLA Ops:
  6.5 92.4 %copy-start = (bf16[1,1601,1024]{2,1,0:T(8,128)(2,1)S(1)}, bf16[1,1601,1024]{2,1,0:T(8,128)(2,1)}, u32[]{:S(2)}) copy-start(bf16[1,1601,1024]{2,1,0:T(8,128)(2,1)} %param.9) | copy-start | bytes 9836548
  6.5 92.4 %all-gather.5.cloned.1.call-start = ((), (), s32[]{:S(2)}) async-start(), calls=%async_computation.2 | async-start | bytes 4325376 | tf_op jit(solution)/shard_map/all_gather | solution.py:74
  7.3 286.9 %all-gather.3.cloned.1.call-start = ((), (), s32[]{:S(2)}) async-start(), calls=%async_computation.1 | async-start | bytes 8650752 | tf_op jit(solution)/shard_map/all_gather | solution.py:75
  99.0 3.2 copy-start.9
  115.8 5.0 %copy-start.1 = (s32[1,32]{1,0:T(1,128)S(1)}, s32[1,32]{1,0:T(1,128)}, u32[]{:S(2)}) copy-start(s32[1,32]{1,0:T(1,128)} %param.15) | copy-start | bytes 388
  115.8 101.1 %all-to-all-start = ((bf16[8,1601,256]{2,1,0:T(8,128)(2,1)}), bf16[8,1601,256]{2,1,0:T(8,128)(2,1)}, u32[]{:S(2)}, u32[]{:S(2)}) async-start(bf16[8,1601,256]{2,1,0:T(8,128)(2,1)} %fusion.62), calls=%async_computation | async-start | bytes 13172736 | tf_op jit(solution)/shard_map/all_to_all | solution.py:89
  120.8 101.5 %copy-start.7 = (f32[128]{0:T(128)S(1)}, f32[128]{0:T(128)}, u32[]{:S(2)}) copy-start(f32[128]{0:T(128)} %param.14) | copy-start | bytes 1540
  221.1 1.3 copy-start.2
  221.1 73.0 %copy-start.10 = (f32[8192]{0:T(1024)S(1)}, f32[8192]{0:T(1024)}, u32[]{:S(2)}) copy-start(f32[8192]{0:T(1024)} %param.10) | copy-start | bytes 98308
  222.6 0.8 copy-start.4
  224.4 23.5 %collective-permute-start.3 = (bf16[1,1601,256]{2,1,0:T(8,128)(2,1)}, bf16[1,1601,256]{2,1,0:T(8,128)(2,1)}, u32[]{:S(2)}, u32[]{:S(2)}) collective-permute-start(bf16[1,1601,256]{2,1,0:T(8,128)(2,1)} %pad_maximum_fusion), channel_id=1, source_target_pairs={{0,32},{8,40},{16,48},{24,56},{32,64},{40,72},{48,80},{56,88},{64,... | collective-permute-start | bytes 2459144 | tf_op jit(solution)/shard_map/ppermute | solution.py:15
  226.9 28.3 %collective-permute-start.2 = (bf16[1,1601,256]{2,1,0:T(8,128)(2,1)}, bf16[1,1601,256]{2,1,0:T(8,128)(2,1)}, u32[]{:S(2)}, u32[]{:S(2)}) collective-permute-start(bf16[1,1601,256]{2,1,0:T(8,128)(2,1)} %pad_maximum_fusion), channel_id=1, source_target_pairs={{0,24},{8,32},{16,40},{24,48},{32,56},{40,64},{48,72},{56,80},{64,... | collective-permute-start | bytes 2459144 | tf_op jit(solution)/shard_map/ppermute | solution.py:15
  228.9 55.1 %collective-permute-start.1 = (bf16[1,1601,256]{2,1,0:T(8,128)(2,1)}, bf16[1,1601,256]{2,1,0:T(8,128)(2,1)}, u32[]{:S(2)}, u32[]{:S(2)}) collective-permute-start(bf16[1,1601,256]{2,1,0:T(8,128)(2,1)} %pad_maximum_fusion), channel_id=1, source_target_pairs={{0,16},{8,24},{16,32},{24,40},{32,48},{40,56},{48,64},{56,72},{64,... | collective-permute-start | bytes 2459144 | tf_op jit(solution)/shard_map/ppermute | solution.py:15
  235.0 56.0 %collective-permute-start = (bf16[1,1601,256]{2,1,0:T(8,128)(2,1)}, bf16[1,1601,256]{2,1,0:T(8,128)(2,1)}, u32[]{:S(2)}, u32[]{:S(2)}) collective-permute-start(bf16[1,1601,256]{2,1,0:T(8,128)(2,1)} %pad_maximum_fusion), channel_id=1, source_target_pairs={{0,8},{8,16},{16,24},{24,32},{32,40},{40,48},{48,56},{56,64},{64,7... | collective-permute-start | bytes 2459144 | tf_op jit(solution)/shard_map/ppermute | solution.py:15
  294.2 13.6 %copy-start.8 = (f32[128]{0:T(128)S(1)}, f32[128]{0:T(128)}, u32[]{:S(2)}) copy-start(f32[128]{0:T(128)} %param.13) | copy-start | bytes 1540
  307.7 3.5 %copy-start.5 = (bf16[1,1601,256]{2,1,0:T(8,128)(2,1)S(1)}, bf16[1,1601,256]{2,1,0:T(8,128)(2,1)}, u32[]{:S(2)}) copy-start(bf16[1,1601,256]{2,1,0:T(8,128)(2,1)} %get-tuple-element.12) | copy-start | bytes 2459140
  307.7 3.5 %copy-start.6 = (bf16[1,1601,256]{2,1,0:T(8,128)(2,1)S(1)}, bf16[1,1601,256]{2,1,0:T(8,128)(2,1)}, u32[]{:S(2)}) copy-start(bf16[1,1601,256]{2,1,0:T(8,128)(2,1)} %get-tuple-element.13) | copy-start | bytes 2459140
  318.4 4.5 %copy-start.3 = (f32[1601,256]{1,0:T(8,128)S(1)}, f32[1601,256]{1,0:T(8,128)}, u32[]{:S(2)}) copy-start(f32[1601,256]{1,0:T(8,128)} %copy-done.2) | copy-start | bytes 4918276
Sparse Core Ops, SparseCore 0:
  10.1 88.7 all-gather.4
  101.8 121.3 all-gather.2

commit v5 on v3

--- a/solution.py
+++ b/solution.py
@@ -88,27 +88,21 @@
         jnp.bfloat16
     )
     features = images[0]
-    score_product = jnp.concatenate(
+    pair_width = 2 * head_dim
+    pairs_per_block = query_width // pair_width
+    partials = jnp.stack(
         [
             jnp.dot(
                 features,
-                both[:, block * kv_rows : (block + 1) * kv_rows].reshape(-1, query_width),
+                both[:, block * kv_rows : (block + 1) * kv_rows, pair * pair_width : (pair + 1) * pair_width]
+                .reshape(-1, pair_width),
                 preferred_element_type=jnp.float32,
-            )
+            ).astype(jnp.bfloat16)
             for block in range(column_blocks)
-        ],
-        axis=1,
+            for pair in range(pairs_per_block)
+        ]
     )
-    own_kv = lax.psum_scatter(
-        score_product.reshape(
-            features.shape[0], local_key_value * lax.axis_size("fsdp"), 2 * head_dim
-        )
-        .transpose(1, 0, 2)
-        .astype(jnp.bfloat16),
-        "fsdp",
-        scatter_dimension=0,
-        tiled=True,
-    ).astype(jnp.float32)
+    own_kv = lax.psum_scatter(partials, "fsdp", scatter_dimension=0, tiled=True).astype(jnp.float32)
     key_part = rms_scale(own_kv[..., :head_dim], key_gain)
     packed = jnp.concatenate([key_part, own_kv[..., head_dim:]], axis=-1).astype(jnp.bfloat16)
     span_index = lax.axis_index("seq")
@@ -118,7 +112,20 @@
     nearest = jnp.argmax(earlier_admitted)
     farthest = IMAGE_LOOKBACK - 1 - jnp.argmax(earlier_admitted[::-1])
     admitted_count = jnp.sum(earlier_admitted.astype(jnp.int32))
-    received = [from_behind(packed, "seq", distance) for distance in range(1, IMAGE_LOOKBACK + 1)]
+    two_behind = from_behind(packed, "seq", 2)
+    four_behind = from_behind(packed, "seq", 4)
+    partner = lax.ppermute(
+        jnp.stack([packed, two_behind, four_behind]),
+        "seq",
+        [(source, source ^ 1) for source in range(lax.axis_size("seq"))],
+    )
+    first_core = span_index % 2 == 0
+    received = [
+        jnp.where(first_core, partner[1], partner[0]),
+        two_behind,
+        jnp.where(first_core, partner[2], partner[1]),
+        four_behind,
+    ]
 
     def pick(slot):
         chosen = received[-1]

time: 319 us -> 298 us (0.934)
  the two profiles are of different devices: /device:TPU:133 before, /device:TPU:129 now
where the time goes in v5:
time: 298 us
  waiting for transfers between devices  200 us (67%)
  local copies, waits for them, and re-layouts  28.3 us (9%)
  matrix products  27.2 us (9%)
  between operations  17.4 us (6%)
  other arithmetic  16.9 us (6%)
  starting transfers between devices  8.3 us (3%)
    all_gather x1, waiting for transfers between devices, on_device(): lax.all_gather(jnp.concatenate([kv_as_rows, query_weight], axis=0), 'seq'...  118 us
    reduce_scatter x1, waiting for transfers between devices, on_device(): lax.psum_scatter(partials, 'fsdp', scatter_dimension=0, tiled=True)  48 us
    ppermute x2, waiting for transfers between devices, from_behind(): lax.ppermute(value, axis, [(source, source + steps) for source in range(i...  34 us
    dot_general x8, matrix products, on_device(): jnp.dot(features, both[:, block * kv_rows:(block + 1) * kv_rows, pair * p...  15.5 us
    reshape x1, local copies, waits for them, and re-layouts, on_device(): query_block = both[:, column_blocks * kv_rows:].reshape(-1, query_width)  11.8 us
    slice x1, local copies, waits for them, and re-layouts, on_device(): query_block = both[:, column_blocks * kv_rows:].reshape(-1, query_width)  8.08 us
    ppermute x2, starting transfers between devices, from_behind(): lax.ppermute(value, axis, [(source, source + steps) for source in range(i...  6.76 us
    dot_general x2, matrix products, attend_part(): jnp.einsum('kqn,knd->kqd', weights.astype(jnp.bfloat16), key_value_pair[....  6.12 us
  transfers between devices with their start and end apart: 5, of which 4 were waited for; matrix products, arithmetic and copies ran while one was open for 11% of the time, Pallas kernels for 0%

profile of v5, /device:TPU:129, one launch (start us, length us, event | category | flops | bytes accessed | tf_op | source)
XLA Modules:
  0.0 297.8 jit_solution(6264609616765405049)
XLA Ops:
  9.5 117.7 %all-gather.3.cloned.1.call-done = bf16[12288,512]{1,0:T(8,128)(2,1)} async-done(((bf16[384,512]{1,0:T(8,128)(2,1)}), bf16[12288,512]{1,0:T(8,128)(2,1)}) %all-gather.3.cloned.1.call-update) | async-done | bytes 12582928 | tf_op jit(solution)/shard_map/all_gather | solution.py:82
  127.2 2.7 fusion.145
  129.9 1.9 fusion.105
  131.8 1.9 fusion.99
  133.7 1.9 fusion.93
  135.7 1.9 fusion.87
  137.6 1.9 fusion.81
  139.5 2.0 fusion.75
  141.5 1.9 fusion.69
  143.4 1.9 fusion.63
  152.1 3.1 %fusion.3 = f32[256]{0:T(256)S(1)} fusion(bf16[256,8192]{1,0:T(8,128)(2,1)} %param.8), kind=kLoop, calls=%fused_computation.8 | loop fusion | flops 6291200 | bytes 4195328 | tf_op jit(solution)/shard_map/reduce_sum | solution.py:19
  155.3 8.1 %slice.83 = bf16[32,256,512]{2,1,0:T(8,128)(2,1)} slice(bf16[32,384,512]{2,1,0:T(8,128)(2,1)} %bitcast.200), slice={[0:32], [128:384], [0:512]} | slice | bytes 16777216 | tf_op jit(solution)/shard_map/slice | solution.py:85
  163.3 11.8 %copy.15 = bf16[8192,512]{0,1:T(8,128)(2,1)} copy(bf16[8192,512]{1,0:T(8,128)(2,1)} %bitcast.198) | data formatting | bytes 16777216 | tf_op jit(solution)/shard_map/reshape | solution.py:85
  175.1 48.0 %reduce-scatter.2.cloned.1.call-done = bf16[1,1601,256]{2,1,0:T(8,128)(2,1)} async-done(((bf16[8,1601,256]{2,1,0:T(8,128)(2,1)}), bf16[1,1601,256]{2,1,0:T(8,128)(2,1)}) %reduce-scatter.2.cloned.1.call-update) | async-done | bytes 819728 | tf_op jit(solution)/shard_map/reduce_scatter | solution.py:105
  225.2 1.8 slice.140
  227.1 2.3 collective-permute-start.1
  229.4 4.5 %collective-permute-start = (bf16[1,1601,256]{2,1,0:T(8,128)(2,1)S(1)}, bf16[1,1601,256]{2,1,0:T(8,128)(2,1)S(1)}, u32[]{:S(2)}, u32[]{:S(2)}) collective-permute-start(bf16[1,1601,256]{2,1,0:T(8,128)(2,1)S(1)} %pad_maximum_fusion.1), channel_id=1, source_target_pairs={{0,16},{8,24},{16,32},{24,40},{32,48},{40,56},{48,64},{56,72},{64,... | collective-permute-start | bytes 2459144 | tf_op jit(solution)/shard_map/ppermute | solution.py:15
  235.2 14.3 %collective-permute-done.1 = bf16[1,1601,256]{2,1,0:T(8,128)(2,1)S(1)} collective-permute-done((bf16[1,1601,256]{2,1,0:T(8,128)(2,1)S(1)}, bf16[1,1601,256]{2,1,0:T(8,128)(2,1)S(1)}, u32[]{:S(2)}, u32[]{:S(2)}) %collective-permute-start.1) | collective-permute-done | bytes 819744 | tf_op jit(solution)/shard_map/ppermute | solution.py:15
  249.4 19.7 %collective-permute-done = bf16[1,1601,256]{2,1,0:T(8,128)(2,1)S(1)} collective-permute-done((bf16[1,1601,256]{2,1,0:T(8,128)(2,1)S(1)}, bf16[1,1601,256]{2,1,0:T(8,128)(2,1)S(1)}, u32[]{:S(2)}, u32[]{:S(2)}) %collective-permute-start) | collective-permute-done | bytes 819744 | tf_op jit(solution)/shard_map/ppermute | solution.py:15
  269.2 1.8 pad_maximum_fusion
  272.5 2.6 multiply_reduce_fusion.1
  278.1 2.0 fusion
  280.1 3.8 %fusion.1 = f32[1024]{0:T(1024)S(1)} fusion(f32[1024,3202]{0,1:T(8,128)S(1)} %get-tuple-element.25, f32[1024]{0:T(1024)S(1)} %compare_select_fusion, pred[3202]{0:T(1024)(128)(4,1)S(1)} %concatenate.36), kind=kLoop, calls=%fused_computation.6 | loop fusion | flops 13114368 | bytes 13126786 | tf_op jit(solution)/shard_map/reduce_sum | solution.py:30
  283.9 4.4 %fusion.114 = f32[1024,128]{1,0:T(8,128)S(1)} fusion(f32[1024,3202]{0,1:T(8,128)S(1)} %get-tuple-element.25, f32[1024]{0:T(1024)S(1)} %compare_select_fusion, pred[3202]{0:T(1024)(128)(4,1)S(1)} %concatenate.36, bf16[1,1601,256]{2,1,0:T(8,128)(2,1)S(1)} %get-tuple-element.20, bf16[1,1601,256]{2,1,0:T(8,128)(2,1)S(1)} %get-tuple-element.21, ...), kind=kOutput, calls=%fused_computation.69 | convolution fusion | flops 854270976 | bytes 15290498 | tf_op jit(solution)/shard_map/kqn,knd->kqd/dot_general | solution.py:31
  (57 shorter events, 16.5 us)
Async XLA Ops:
  6.5 123.3 %copy-start = (bf16[1,1601,1024]{2,1,0:T(8,128)(2,1)S(1)}, bf16[1,1601,1024]{2,1,0:T(8,128)(2,1)}, u32[]{:S(2)}) copy-start(bf16[1,1601,1024]{2,1,0:T(8,128)(2,1)} %param.9) | copy-start | bytes 9836548
  6.5 120.7 %all-gather.3.cloned.1.call-start = ((), (), s32[]{:S(2)}) async-start(), calls=%async_computation.2 | async-start | bytes 12976128 | tf_op jit(solution)/shard_map/all_gather | solution.py:82
  9.5 213.6 %reduce-scatter.2.cloned.1.call-start = ((), (), s32[]{:S(2)}) async-start(), calls=%async_computation.1 | async-start | bytes 7409664 | tf_op jit(solution)/shard_map/reduce_scatter | solution.py:105
  143.4 2.0 copy-start.2
  163.3 61.5 %copy-start.6 = (f32[128]{0:T(128)S(1)}, f32[128]{0:T(128)}, u32[]{:S(2)}) copy-start(f32[128]{0:T(128)} %param.14) | copy-start | bytes 1540
  175.1 97.4 %copy-start.8 = (f32[8192]{0:T(1024)S(1)}, f32[8192]{0:T(1024)}, u32[]{:S(2)}) copy-start(f32[8192]{0:T(1024)} %param.10) | copy-start | bytes 98308
  223.1 49.4 %copy-start.3 = (bf16[8192,512]{0,1:T(8,128)(2,1)S(1)}, bf16[8192,512]{0,1:T(8,128)(2,1)}, u32[]{:S(2)}) copy-start(bf16[8192,512]{0,1:T(8,128)(2,1)} %copy.15) | copy-start | bytes 25165828
  223.1 49.4 %copy-start.4 = (bf16[256,8192]{1,0:T(8,128)(2,1)S(1)}, bf16[256,8192]{1,0:T(8,128)(2,1)}, u32[]{:S(2)}) copy-start(bf16[256,8192]{1,0:T(8,128)(2,1)} %param.8) | copy-start | bytes 12582916
  227.1 22.4 %collective-permute-start.1 = (bf16[1,1601,256]{2,1,0:T(8,128)(2,1)S(1)}, bf16[1,1601,256]{2,1,0:T(8,128)(2,1)S(1)}, u32[]{:S(2)}, u32[]{:S(2)}) collective-permute-start(bf16[1,1601,256]{2,1,0:T(8,128)(2,1)S(1)} %pad_maximum_fusion.1), channel_id=1, source_target_pairs={{0,32},{8,40},{16,48},{24,56},{32,64},{40,72},{48,80},{56,88},{64,... | collective-permute-start | bytes 2459144 | tf_op jit(solution)/shard_map/ppermute | solution.py:15
  229.4 39.8 %collective-permute-start = (bf16[1,1601,256]{2,1,0:T(8,128)(2,1)S(1)}, bf16[1,1601,256]{2,1,0:T(8,128)(2,1)S(1)}, u32[]{:S(2)}, u32[]{:S(2)}) collective-permute-start(bf16[1,1601,256]{2,1,0:T(8,128)(2,1)S(1)} %pad_maximum_fusion.1), channel_id=1, source_target_pairs={{0,16},{8,24},{16,32},{24,40},{32,48},{40,56},{48,64},{56,72},{64,... | collective-permute-start | bytes 2459144 | tf_op jit(solution)/shard_map/ppermute | solution.py:15
  271.0 6.8 %collective-permute-start.2 = (bf16[3,1,1601,256]{3,2,1,0:T(8,128)(2,1)}, bf16[3,1,1601,256]{3,2,1,0:T(8,128)(2,1)S(1)}, u32[]{:S(2)}, u32[]{:S(2)}) collective-permute-start(bf16[3,1,1601,256]{3,2,1,0:T(8,128)(2,1)} %pad_maximum_fusion), channel_id=1, source_target_pairs={{0,8},{8,0},{16,24},{24,16},{32,40},{40,32},{48,56},{56,48},{64,72... | collective-permute-start | bytes 7377416 | tf_op jit(solution)/shard_map/ppermute | solution.py:117
  272.5 2.6 copy-start.7
  283.9 4.5 %copy-start.5 = (bf16[1,1601,256]{2,1,0:T(8,128)(2,1)S(1)}, bf16[1,1601,256]{2,1,0:T(8,128)(2,1)}, u32[]{:S(2)}) copy-start(bf16[1,1601,256]{2,1,0:T(8,128)(2,1)} %reduce-scatter.2.cloned.1.call-done) | copy-start | bytes 2459140
  288.3 2.7 copy-start.1
Sparse Core Ops, SparseCore 0:
  10.1 117.0 all-gather.2
  145.5 77.6 reduce-scatter.1

commit v6 on v5

--- a/solution.py
+++ b/solution.py
@@ -3,9 +3,10 @@
 import jax
 import jax.numpy as jnp
 from jax import lax
-from jax.sharding import PartitionSpec as P
+from jax.sharding import Mesh, PartitionSpec as P
 
 KEY_VALUE_HEADS = 8
+SEQ = ("chip", "core")
 IMAGE_LOOKBACK = 4
 
 
@@ -79,24 +80,42 @@
         .transpose(1, 0, 2)
         .reshape(column_blocks * kv_rows, query_width)
     )
-    both = lax.all_gather(
-        jnp.concatenate([kv_as_rows, query_weight], axis=0), "seq", axis=0, tiled=False
+    stacked_rows = jnp.concatenate([kv_as_rows, query_weight], axis=0)
+    mine = lax.all_gather(stacked_rows, "chip", axis=0, tiled=False)
+    swap = [(0, 1), (1, 0)]
+    other_kv = lax.ppermute(mine[:, : column_blocks * kv_rows], "core", swap)
+    other_query = lax.ppermute(mine[:, column_blocks * kv_rows :], "core", swap)
+    first_core = lax.axis_index("core") == 0
+    chip_count = mine.shape[0]
+
+    def by_parity(columns, block):
+        split = columns.reshape(columns.shape[0], chip_count, 2, block)
+        even = split[:, :, 0].reshape(columns.shape[0], chip_count * block)
+        odd = split[:, :, 1].reshape(columns.shape[0], chip_count * block)
+        return jnp.where(first_core, even, odd), jnp.where(first_core, odd, even)
+
+    normed_mine, normed_other = by_parity(normed, query_weight.shape[0])
+    query_mine = mine[:, column_blocks * kv_rows :].reshape(-1, query_width)
+    queries = jnp.dot(normed_mine, query_mine, preferred_element_type=jnp.float32) + jnp.dot(
+        normed_other, other_query.reshape(-1, query_width), preferred_element_type=jnp.float32
     )
-    query_block = both[:, column_blocks * kv_rows :].reshape(-1, query_width)
-    queries = jnp.dot(normed, query_block, preferred_element_type=jnp.float32)
     query_heads = rms_scale(queries.reshape(row_count, heads_local, head_dim), query_gain).astype(
         jnp.bfloat16
     )
-    features = images[0]
+    features_mine, features_other = by_parity(images[0], kv_rows)
     pair_width = 2 * head_dim
     pairs_per_block = query_width // pair_width
+
+    def head_weight(rows, block, pair):
+        return rows[:, block * kv_rows : (block + 1) * kv_rows, pair * pair_width : (pair + 1) * pair_width].reshape(
+            -1, pair_width
+        )
+
     partials = jnp.stack(
         [
-            jnp.dot(
-                features,
-                both[:, block * kv_rows : (block + 1) * kv_rows, pair * pair_width : (pair + 1) * pair_width]
-                .reshape(-1, pair_width),
-                preferred_element_type=jnp.float32,
+            (
+                jnp.dot(features_mine, head_weight(mine, block, pair), preferred_element_type=jnp.float32)
+                + jnp.dot(features_other, head_weight(other_kv, block, pair), preferred_element_type=jnp.float32)
             ).astype(jnp.bfloat16)
             for block in range(column_blocks)
             for pair in range(pairs_per_block)
@@ -105,19 +124,19 @@
     own_kv = lax.psum_scatter(partials, "fsdp", scatter_dimension=0, tiled=True).astype(jnp.float32)
     key_part = rms_scale(own_kv[..., :head_dim], key_gain)
     packed = jnp.concatenate([key_part, own_kv[..., head_dim:]], axis=-1).astype(jnp.bfloat16)
-    span_index = lax.axis_index("seq")
+    span_index = lax.axis_index(SEQ)
     image_ids = span_index - jnp.arange(IMAGE_LOOKBACK + 1, dtype=jnp.int32)
     admitted = (image_ids >= 0) & (jnp.take(admission[0], jnp.maximum(image_ids, 0)) == 1)
     earlier_admitted = admitted[1:]
     nearest = jnp.argmax(earlier_admitted)
     farthest = IMAGE_LOOKBACK - 1 - jnp.argmax(earlier_admitted[::-1])
     admitted_count = jnp.sum(earlier_admitted.astype(jnp.int32))
-    two_behind = from_behind(packed, "seq", 2)
-    four_behind = from_behind(packed, "seq", 4)
+    two_behind = from_behind(packed, SEQ, 2)
+    four_behind = from_behind(packed, SEQ, 4)
     partner = lax.ppermute(
         jnp.stack([packed, two_behind, four_behind]),
-        "seq",
-        [(source, source ^ 1) for source in range(lax.axis_size("seq"))],
+        SEQ,
+        [(source, source ^ 1) for source in range(lax.axis_size(SEQ))],
     )
     first_core = span_index % 2 == 0
     received = [
@@ -147,15 +166,17 @@
 
 def solution(mesh):
     placed = (
-        P("seq", None),
-        P("seq", None, "fsdp"),
+        P(SEQ, None),
+        P(SEQ, None, "fsdp"),
         P(),
-        P("seq", "fsdp"),
-        P(("fsdp", "seq"), None),
+        P(SEQ, "fsdp"),
+        P(("fsdp",) + SEQ, None),
         P(),
         P(),
-        P("seq", None),
+        P(SEQ, None),
     )
+    rows, columns = mesh.devices.shape
+    split_mesh = Mesh(mesh.devices.reshape(rows // 2, 2, columns), ("chip", "core", "fsdp"))
     return jax.shard_map(
-        on_device, mesh=mesh, in_specs=placed, out_specs=P("seq", "fsdp"), check_vma=False
+        on_device, mesh=split_mesh, in_specs=placed, out_specs=P(SEQ, "fsdp"), check_vma=False
     )

time: 298 us -> 310 us (1.040)
  the two profiles are of different devices: /device:TPU:129 before, /device:TPU:133 now
where the time goes in v6:
time: 310 us; the launch traced here: 309 us
  waiting for transfers between devices  193 us (62%)
  matrix products  34.9 us (11%)
  other arithmetic  30.5 us (10%)
  local copies, waits for them, and re-layouts  25.4 us (8%)
  between operations  17.4 us (6%)
  starting transfers between devices  8.01 us (3%)
    all_gather x1, waiting for transfers between devices, on_device(): mine = lax.all_gather(stacked_rows, 'chip', axis=0, tiled=False)  104 us
    reduce_scatter x1, waiting for transfers between devices, on_device(): lax.psum_scatter(partials, 'fsdp', scatter_dimension=0, tiled=True)  53.3 us
    ppermute x2, waiting for transfers between devices, from_behind(): lax.ppermute(value, axis, [(source, source + steps) for source in range(i...  35.1 us
    unnamed x25, local copies, waits for them, and re-layouts  13 us
    dot_general x8, matrix products, on_device(): jnp.dot(features_other, head_weight(other_kv, block, pair), preferred_ele...  12.6 us
    select_n x2, other arithmetic, by_parity(): return (jnp.where(first_core, even, odd), jnp.where(first_core, odd, even))  6.86 us
  transfers between devices with their start and end apart: 7, of which 4 were waited for; matrix products, arithmetic and copies ran while one was open for 18% of the time, Pallas kernels for 0%

profile of v6, /device:TPU:133, one launch (start us, length us, event | category | flops | bytes accessed | tf_op | source)
XLA Modules:
  0.0 309.0 jit_solution(1541910611904541365)
XLA Ops:
  7.6 1.7 pad_maximum_fusion.3
  9.4 5.5 %copy.30 = bf16[1,1601,1024]{1,2,0:T(8,128)(2,1)} copy(bf16[1,1601,1024]{2,1,0:T(8,128)(2,1)} %param.9) | data formatting | bytes 6557696 | tf_op args[1]
  14.8 2.3 broadcast_select_fusion.2
  17.1 104.3 %all-gather.3.cloned.1.call-done = bf16[6144,512]{1,0:T(8,128)(2,1)} async-done(((bf16[384,512]{1,0:T(8,128)(2,1)}), bf16[6144,512]{1,0:T(8,128)(2,1)}) %all-gather.3.cloned.1.call-update) | async-done | bytes 6291472 | tf_op jit(solution)/shard_map/all_gather | solution.py:84
  123.1 1.7 slice.142
  144.6 6.7 %copy.26 = bf16[256,8192]{0,1:T(8,128)(2,1)} copy(bf16[256,8192]{1,0:T(8,128)(2,1)} %param.8) | data formatting | bytes 8388608 | tf_op args[0]
  151.3 3.5 %fusion.3 = f32[256]{0:T(256)S(1)} fusion(bf16[256,8192]{0,1:T(8,128)(2,1)} %copy.26), kind=kLoop, calls=%fused_computation.8 | loop fusion | flops 6291200 | bytes 4195328 | tf_op jit(solution)/shard_map/reduce_sum | solution.py:20
  154.8 2.6 fusion.5
  157.4 2.5 slice.138
  166.4 4.6 %broadcast_select_fusion = (bf16[256,16,1,256]{0,3,2,1:T(8,128)(2,1)}, bf16[256,16,1,256]{0,3,2,1:T(8,128)(2,1)}) fusion(pred[]{:T(512)S(6)} %eq.49, bf16[256,16,2,256]{0,3,2,1:T(8,128)(2,1)} %bitcast.165), kind=kLoop, calls=%fused_computation.53 | loop fusion | flops 2097152 | bytes 8388609 | tf_op jit(solution)/shard_map/jit(_where)/select_n | solution.py:95
  171.0 53.3 %reduce-scatter.2.cloned.1.call-done = bf16[1,1601,256]{2,1,0:T(8,128)(2,1)} async-done(((bf16[8,1601,256]{2,1,0:T(8,128)(2,1)}), bf16[1,1601,256]{2,1,0:T(8,128)(2,1)}) %reduce-scatter.2.cloned.1.call-update) | async-done | bytes 819728 | tf_op jit(solution)/shard_map/reduce_scatter | solution.py:124
  226.4 2.6 collective-permute-start.2
  229.0 2.3 collective-permute-start.3
  231.6 17.5 %collective-permute-done.2 = bf16[1,1601,256]{2,1,0:T(8,128)(2,1)S(1)} collective-permute-done((bf16[1,1601,256]{2,1,0:T(8,128)(2,1)S(1)}, bf16[1,1601,256]{2,1,0:T(8,128)(2,1)S(1)}, u32[]{:S(2)}, u32[]{:S(2)}) %collective-permute-start.2) | collective-permute-done | bytes 819744 | tf_op jit(solution)/shard_map/ppermute | solution.py:16
  249.1 17.7 %collective-permute-done.3 = bf16[1,1601,256]{2,1,0:T(8,128)(2,1)S(1)} collective-permute-done((bf16[1,1601,256]{2,1,0:T(8,128)(2,1)S(1)}, bf16[1,1601,256]{2,1,0:T(8,128)(2,1)S(1)}, u32[]{:S(2)}, u32[]{:S(2)}) %collective-permute-start.3) | collective-permute-done | bytes 819744 | tf_op jit(solution)/shard_map/ppermute | solution.py:16
  266.7 1.7 pad_maximum_fusion
  269.9 3.6 %fusion.82 = f32[256,512]{1,0:T(8,128)S(1)} fusion(bf16[256,4096]{0,1:T(8,128)(2,1)S(1)} %bitcast.177, bf16[4096,512]{1,0:T(8,128)(2,1)} %bitcast.8), kind=kOutput, calls=%fused_computation.117 | convolution fusion | flops 1073741824 | bytes 6815744 | tf_op jit(solution)/shard_map/dot_general | solution.py:99
  273.6 4.4 %fusion.80 = (f32[256,512]{1,0:T(8,128)}, f32[256,512]{1,0:T(8,128)}) fusion(f32[256,512]{1,0:T(8,128)S(1)} %fusion.82, bf16[256,4096]{0,1:T(8,128)(2,1)S(1)} %bitcast.176, bf16[4096,512]{1,0:T(8,128)(2,1)} %bitcast.10), kind=kOutput, calls=%fused_computation.114 | convolution fusion | flops 1074003968 | bytes 7864320 | tf_op jit(solution)/shard_map/dot_general | solution.py:99
  278.0 2.1 reshape.399
  280.1 2.0 mul.132
  287.3 1.9 select_select_fusion
  289.2 2.0 fusion
  291.2 3.8 %fusion.1 = f32[1024]{0:T(1024)S(1)} fusion(f32[1024,3202]{0,1:T(8,128)S(1)} %get-tuple-element.37, f32[1024]{0:T(1024)S(1)} %compare_select_fusion, pred[3202]{0:T(1024)(128)(4,1)S(1)} %concatenate.36), kind=kLoop, calls=%fused_computation.6 | loop fusion | flops 13114368 | bytes 13126786 | tf_op jit(solution)/shard_map/reduce_sum | solution.py:31
  295.1 4.4 %fusion.45 = f32[1024,128]{1,0:T(8,128)S(1)} fusion(f32[1024,3202]{0,1:T(8,128)S(1)} %get-tuple-element.37, f32[1024]{0:T(1024)S(1)} %compare_select_fusion, pred[3202]{0:T(1024)(128)(4,1)S(1)} %concatenate.36, bf16[1,1601,256]{2,1,0:T(8,128)(2,1)S(1)} %get-tuple-element.22, bf16[1,1601,256]{2,1,0:T(8,128)(2,1)S(1)} %get-tuple-element.23, ...), kind=kOutput, calls=%fused_computation.61 | convolution fusion | flops 854270976 | bytes 15290498 | tf_op jit(solution)/shard_map/kqn,knd->kqd/dot_general | solution.py:32
  (86 shorter events, 37.1 us)
Async XLA Ops:
  6.5 153.4 %copy-start = (s32[1,32]{1,0:T(1,128)S(1)}, s32[1,32]{1,0:T(1,128)}, u32[]{:S(2)}) copy-start(s32[1,32]{1,0:T(1,128)} %param.15) | copy-start | bytes 388
  6.5 114.8 %all-gather.3.cloned.1.call-start = ((), (), s32[]{:S(2)}) async-start(), calls=%async_computation.2 | async-start | bytes 6684672 | tf_op jit(solution)/shard_map/all_gather | solution.py:84
  9.3 215.0 %reduce-scatter.2.cloned.1.call-start = ((), (), s32[]{:S(2)}) async-start(), calls=%async_computation.1 | async-start | bytes 7409664 | tf_op jit(solution)/shard_map/reduce_scatter | solution.py:124
  124.8 6.8 %collective-permute-start.1 = (bf16[16,128,512]{2,1,0:T(8,128)(2,1)S(1)}, bf16[16,128,512]{2,1,0:T(8,128)(2,1)S(1)}, u32[]{:S(2)}, u32[]{:S(2)}) collective-permute-start(bf16[16,128,512]{2,1,0:T(8,128)(2,1)S(1)} %slice.142), channel_id=1, source_target_pairs={{0,8},{8,0},{1,9},{9,1},{2,10},{10,2},{3,11},{11,3},{4,12},{12,4},... | collective-permute-start | bytes 6291464 | tf_op jit(solution)/shard_map/ppermute | solution.py:86
  144.6 10.2 %copy-start.6 = (f32[8192]{0:T(1024)S(1)}, f32[8192]{0:T(1024)}, u32[]{:S(2)}) copy-start(f32[8192]{0:T(1024)} %param.10) | copy-start | bytes 98308
  144.6 12.8 %slice-start = ((s8[6291456]{0:T(1024)(128)(4,1)}), s8[2097152]{0:T(1024)(128)(4,1)S(1)}, s32[]{:S(2)}) async-start(s8[6291456]{0:T(1024)(128)(4,1)} %bitcast.169), calls=%async_computation.3 | async-start | bytes 4194304
  151.3 3.5 %copy-start.2 = (bf16[256,8192]{0,1:T(8,128)(2,1)S(1)}, bf16[256,8192]{0,1:T(8,128)(2,1)}, u32[]{:S(2)}) copy-start(bf16[256,8192]{0,1:T(8,128)(2,1)} %copy.26) | copy-start | bytes 12582916
  151.3 6.1 %slice-start.1 = ((s8[6291456]{0:T(1024)(128)(4,1)}), s8[4194304]{0:T(1024)(128)(4,1)S(1)}, s32[]{:S(2)}) async-start(s8[6291456]{0:T(1024)(128)(4,1)} %bitcast.169), calls=%async_computation.4 | async-start | bytes 8388608
  159.9 113.7 %collective-permute-start = (bf16[16,256,512]{2,1,0:T(8,128)(2,1)}, bf16[16,256,512]{2,1,0:T(8,128)(2,1)}, u32[]{:S(2)}, u32[]{:S(2)}) collective-permute-start(bf16[16,256,512]{2,1,0:T(8,128)(2,1)} %slice.138), channel_id=1, source_target_pairs={{0,8},{8,0},{1,9},{9,1},{2,10},{10,2},{3,11},{11,3},{4,12},{12,4},... | collective-permute-start | bytes 12582920 | tf_op jit(solution)/shard_map/ppermute | solution.py:87
  171.0 55.0 %copy-start.7 = (f32[128]{0:T(128)S(1)}, f32[128]{0:T(128)}, u32[]{:S(2)}) copy-start(f32[128]{0:T(128)} %param.14) | copy-start | bytes 1540
  224.3 2.0 slice-start.2
  225.7 5.6 %copy-start.3 = (bf16[1,1601,256]{2,1,0:T(8,128)(2,1)S(1)}, bf16[1,1601,256]{2,1,0:T(8,128)(2,1)}, u32[]{:S(2)}) copy-start(bf16[1,1601,256]{2,1,0:T(8,128)(2,1)} %reduce-scatter.2.cloned.1.call-done) | copy-start | bytes 2459140
  226.4 22.6 %collective-permute-start.2 = (bf16[1,1601,256]{2,1,0:T(8,128)(2,1)S(1)}, bf16[1,1601,256]{2,1,0:T(8,128)(2,1)S(1)}, u32[]{:S(2)}, u32[]{:S(2)}) collective-permute-start(bf16[1,1601,256]{2,1,0:T(8,128)(2,1)S(1)} %pad_maximum_fusion.1), channel_id=1, source_target_pairs={{0,16},{8,24},{16,32},{24,40},{32,48},{40,56},{48,64},{56,72},{64,... | collective-permute-start | bytes 2459144 | tf_op jit(solution)/shard_map/ppermute | solution.py:16
  229.0 37.7 %collective-permute-start.3 = (bf16[1,1601,256]{2,1,0:T(8,128)(2,1)S(1)}, bf16[1,1601,256]{2,1,0:T(8,128)(2,1)S(1)}, u32[]{:S(2)}, u32[]{:S(2)}) collective-permute-start(bf16[1,1601,256]{2,1,0:T(8,128)(2,1)S(1)} %pad_maximum_fusion.1), channel_id=1, source_target_pairs={{0,32},{8,40},{16,48},{24,56},{32,64},{40,72},{48,80},{56,88},{64,... | collective-permute-start | bytes 2459144 | tf_op jit(solution)/shard_map/ppermute | solution.py:16
  266.7 3.2 %copy-start.5 = (bf16[256,16,1,256]{0,3,2,1:T(8,128)(2,1)S(1)}, bf16[256,16,1,256]{0,3,2,1:T(8,128)(2,1)}, u32[]{:S(2)}) copy-start(bf16[256,16,1,256]{0,3,2,1:T(8,128)(2,1)} %get-tuple-element.21) | copy-start | bytes 6291460
  268.5 18.8 %collective-permute-start.4 = (bf16[3,1,1601,256]{3,2,1,0:T(8,128)(2,1)}, bf16[3,1,1601,256]{3,2,1,0:T(8,128)(2,1)}, u32[]{:S(2)}, u32[]{:S(2)}) collective-permute-start(bf16[3,1,1601,256]{3,2,1,0:T(8,128)(2,1)} %pad_maximum_fusion), channel_id=1, source_target_pairs={{0,8},{8,0},{16,24},{24,16},{32,40},{40,32},{48,56},{56,48},{64,72... | collective-permute-start | bytes 7377416 | tf_op jit(solution)/shard_map/ppermute | solution.py:136
  269.9 3.6 %copy-start.4 = (bf16[256,16,1,256]{0,3,2,1:T(8,128)(2,1)S(1)}, bf16[256,16,1,256]{0,3,2,1:T(8,128)(2,1)}, u32[]{:S(2)}) copy-start(bf16[256,16,1,256]{0,3,2,1:T(8,128)(2,1)} %get-tuple-element.20) | copy-start | bytes 6291460
  278.0 5.6 %copy-start.8 = (f32[128]{0:T(128)S(1)}, f32[128]{0:T(128)}, u32[]{:S(2)}) copy-start(f32[128]{0:T(128)} %param.13) | copy-start | bytes 1540
  299.5 2.6 copy-start.1
Sparse Core Ops, SparseCore 0:
  9.9 111.3 all-gather.2
  144.7 79.6 reduce-scatter.1

commit v7 on v5

--- a/solution.py
+++ b/solution.py
@@ -102,7 +102,9 @@
             for pair in range(pairs_per_block)
         ]
     )
-    own_kv = lax.psum_scatter(partials, "fsdp", scatter_dimension=0, tiled=True).astype(jnp.float32)
+    own_kv = jnp.sum(
+        lax.all_to_all(partials, "fsdp", 0, 0, tiled=True).astype(jnp.float32), axis=0, keepdims=True
+    )
     key_part = rms_scale(own_kv[..., :head_dim], key_gain)
     packed = jnp.concatenate([key_part, own_kv[..., head_dim:]], axis=-1).astype(jnp.bfloat16)
     span_index = lax.axis_index("seq")

time: 298 us -> 302 us (1.013)
  the two profiles are of different devices: /device:TPU:129 before, /device:TPU:33 now
where the time goes in v7:
time: 302 us; the launch traced here: 301 us
  waiting for transfers between devices  199 us (66%)
  matrix products  27.2 us (9%)
  local copies, waits for them, and re-layouts  24.6 us (8%)
  other arithmetic  19.5 us (6%)
  between operations  17.4 us (6%)
  starting transfers between devices  13 us (4%)
    all_gather x1, waiting for transfers between devices, on_device(): lax.all_gather(jnp.concatenate([kv_as_rows, query_weight], axis=0), 'seq'...  121 us
    all_to_all x1, waiting for transfers between devices, on_device(): lax.all_to_all(partials, 'fsdp', 0, 0, tiled=True).astype(jnp.float32)  45.4 us
    ppermute x2, waiting for transfers between devices, from_behind(): lax.ppermute(value, axis, [(source, source + steps) for source in range(i...  33 us
    dot_general x8, matrix products, on_device(): jnp.dot(features, both[:, block * kv_rows:(block + 1) * kv_rows, pair * p...  15.4 us
    reshape x1, local copies, waits for them, and re-layouts, on_device(): query_block = both[:, column_blocks * kv_rows:].reshape(-1, query_width)  11.4 us
    slice x1, local copies, waits for them, and re-layouts, on_device(): query_block = both[:, column_blocks * kv_rows:].reshape(-1, query_width)  7.46 us
    ppermute x2, starting transfers between devices, from_behind(): lax.ppermute(value, axis, [(source, source + steps) for source in range(i...  6.26 us
    dot_general x2, matrix products, attend_part(): jnp.einsum('kqn,knd->kqd', weights.astype(jnp.bfloat16), key_value_pair[....  6.13 us
  transfers between devices with their start and end apart: 5, of which 4 were waited for; matrix products, arithmetic and copies ran while one was open for 10% of the time, Pallas kernels for 0%

profile of v7, /device:TPU:33, one launch (start us, length us, event | category | flops | bytes accessed | tf_op | source)
XLA Modules:
  0.0 301.2 jit_solution(15412787378420482302)
XLA Ops:
  9.5 120.9 %all-gather.3.cloned.1.call-done = bf16[12288,512]{1,0:T(8,128)(2,1)} async-done(((bf16[384,512]{1,0:T(8,128)(2,1)}), bf16[12288,512]{1,0:T(8,128)(2,1)}) %all-gather.3.cloned.1.call-update) | async-done | bytes 12582928 | tf_op jit(solution)/shard_map/all_gather | solution.py:82
  130.4 2.7 fusion.145
  133.1 1.9 fusion.105
  135.0 1.9 fusion.99
  136.9 2.0 fusion.93
  138.9 1.9 fusion.87
  140.8 1.9 fusion.81
  142.7 1.9 fusion.75
  144.6 1.9 fusion.69
  146.5 2.0 fusion.63
  148.5 5.1 %all-to-all-start = ((bf16[8,1601,256]{2,1,0:T(8,128)(2,1)}), bf16[8,1601,256]{2,1,0:T(8,128)(2,1)}, u32[]{:S(2)}, u32[]{:S(2)}) async-start(bf16[8,1601,256]{2,1,0:T(8,128)(2,1)} %fusion.63), calls=%async_computation | async-start | bytes 13172736 | tf_op jit(solution)/shard_map/all_to_all | solution.py:106
  160.4 3.1 %fusion.3 = f32[256]{0:T(256)S(1)} fusion(bf16[256,8192]{1,0:T(8,128)(2,1)} %param.8), kind=kLoop, calls=%fused_computation.9 | loop fusion | flops 6291200 | bytes 4195328 | tf_op jit(solution)/shard_map/reduce_sum | solution.py:19
  163.5 7.5 %slice.83 = bf16[32,256,512]{2,1,0:T(8,128)(2,1)} slice(bf16[32,384,512]{2,1,0:T(8,128)(2,1)} %bitcast.207), slice={[0:32], [128:384], [0:512]} | slice | bytes 16777216 | tf_op jit(solution)/shard_map/slice | solution.py:85
  171.0 11.4 %copy.29 = bf16[8192,512]{0,1:T(8,128)(2,1)} copy(bf16[8192,512]{1,0:T(8,128)(2,1)} %bitcast.199) | data formatting | bytes 16777216 | tf_op jit(solution)/shard_map/reshape | solution.py:85
  182.4 45.4 %all-to-all-done = bf16[8,1601,256]{2,1,0:T(8,128)(2,1)} async-done(((bf16[8,1601,256]{2,1,0:T(8,128)(2,1)}), bf16[8,1601,256]{2,1,0:T(8,128)(2,1)}, u32[]{:S(2)}, u32[]{:S(2)}) %all-to-all-start) | async-done | bytes 6557728 | tf_op jit(solution)/shard_map/all_to_all | solution.py:106
  227.8 4.1 %convert_reduce_fusion = f32[1601,256]{1,0:T(8,128)S(1)} fusion(bf16[8,1601,256]{2,1,0:T(8,128)(2,1)} %all-to-all-done), kind=kLoop, calls=%fused_computation.1 | loop fusion | flops 6147840 | bytes 8197120 | tf_op jit(solution)/shard_map/reduce_sum | solution.py:105
  232.7 3.3 %collective-permute-start.1 = (bf16[1,1601,256]{2,1,0:T(8,128)(2,1)S(1)}, bf16[1,1601,256]{2,1,0:T(8,128)(2,1)S(1)}, u32[]{:S(2)}, u32[]{:S(2)}) collective-permute-start(bf16[1,1601,256]{2,1,0:T(8,128)(2,1)S(1)} %pad_maximum_fusion.1), channel_id=1, source_target_pairs={{0,32},{8,40},{16,48},{24,56},{32,64},{40,72},{48,80},{56,88},{64,... | collective-permute-start | bytes 2459144 | tf_op jit(solution)/shard_map/ppermute | solution.py:15
  236.1 2.9 collective-permute-start
  239.3 14.7 %collective-permute-done.1 = bf16[1,1601,256]{2,1,0:T(8,128)(2,1)S(1)} collective-permute-done((bf16[1,1601,256]{2,1,0:T(8,128)(2,1)S(1)}, bf16[1,1601,256]{2,1,0:T(8,128)(2,1)S(1)}, u32[]{:S(2)}, u32[]{:S(2)}) %collective-permute-start.1) | collective-permute-done | bytes 819744 | tf_op jit(solution)/shard_map/ppermute | solution.py:15
  254.0 18.3 %collective-permute-done = bf16[1,1601,256]{2,1,0:T(8,128)(2,1)S(1)} collective-permute-done((bf16[1,1601,256]{2,1,0:T(8,128)(2,1)S(1)}, bf16[1,1601,256]{2,1,0:T(8,128)(2,1)S(1)}, u32[]{:S(2)}, u32[]{:S(2)}) %collective-permute-start) | collective-permute-done | bytes 819744 | tf_op jit(solution)/shard_map/ppermute | solution.py:15
  275.8 2.6 multiply_reduce_fusion.1
  281.4 2.0 fusion
  283.4 3.8 %fusion.1 = f32[1024]{0:T(1024)S(1)} fusion(f32[1024,3202]{0,1:T(8,128)S(1)} %get-tuple-element.25, f32[1024]{0:T(1024)S(1)} %compare_select_fusion, pred[3202]{0:T(1024)(128)(4,1)S(1)} %concatenate.36), kind=kLoop, calls=%fused_computation.7 | loop fusion | flops 13114368 | bytes 13126786 | tf_op jit(solution)/shard_map/reduce_sum | solution.py:30
  287.2 4.4 %fusion.114 = f32[1024,128]{1,0:T(8,128)S(1)} fusion(f32[1024,3202]{0,1:T(8,128)S(1)} %get-tuple-element.25, f32[1024]{0:T(1024)S(1)} %compare_select_fusion, pred[3202]{0:T(1024)(128)(4,1)S(1)} %concatenate.36, bf16[1,1601,256]{2,1,0:T(8,128)(2,1)S(1)} %get-tuple-element.20, bf16[1,1601,256]{2,1,0:T(8,128)(2,1)S(1)} %get-tuple-element.21, ...), kind=kOutput, calls=%fused_computation.70 | convolution fusion | flops 854270976 | bytes 15290498 | tf_op jit(solution)/shard_map/kqn,knd->kqd/dot_general | solution.py:31
  (57 shorter events, 16.1 us)
Async XLA Ops:
  6.5 126.5 %copy-start = (bf16[1,1601,1024]{2,1,0:T(8,128)(2,1)S(1)}, bf16[1,1601,1024]{2,1,0:T(8,128)(2,1)}, u32[]{:S(2)}) copy-start(bf16[1,1601,1024]{2,1,0:T(8,128)(2,1)} %param.9) | copy-start | bytes 9836548
  6.5 123.8 %all-gather.3.cloned.1.call-start = ((), (), s32[]{:S(2)}) async-start(), calls=%async_computation.1 | async-start | bytes 12976128 | tf_op jit(solution)/shard_map/all_gather | solution.py:82
  148.5 5.1 %copy-start.2 = (s32[1,32]{1,0:T(1,128)S(1)}, s32[1,32]{1,0:T(1,128)}, u32[]{:S(2)}) copy-start(s32[1,32]{1,0:T(1,128)} %param.15) | copy-start | bytes 388
  148.5 79.3 %all-to-all-start = ((bf16[8,1601,256]{2,1,0:T(8,128)(2,1)}), bf16[8,1601,256]{2,1,0:T(8,128)(2,1)}, u32[]{:S(2)}, u32[]{:S(2)}) async-start(bf16[8,1601,256]{2,1,0:T(8,128)(2,1)} %fusion.63), calls=%async_computation | async-start | bytes 13172736 | tf_op jit(solution)/shard_map/all_to_all | solution.py:106
  182.4 50.0 %copy-start.4 = (f32[128]{0:T(128)S(1)}, f32[128]{0:T(128)}, u32[]{:S(2)}) copy-start(f32[128]{0:T(128)} %param.14) | copy-start | bytes 1540
  227.8 48.0 %slice-start = ((s8[8388608]{0:T(1024)(128)(4,1)}), s8[4194304]{0:T(1024)(128)(4,1)S(1)}, s32[]{:S(2)}) async-start(s8[8388608]{0:T(1024)(128)(4,1)} %bitcast.208), calls=%async_computation.2 | async-start | bytes 8388608
  231.9 43.9 %copy-start.3 = (bf16[256,8192]{1,0:T(8,128)(2,1)S(1)}, bf16[256,8192]{1,0:T(8,128)(2,1)}, u32[]{:S(2)}) copy-start(bf16[256,8192]{1,0:T(8,128)(2,1)} %param.8) | copy-start | bytes 12582916
  231.9 43.9 %copy-start.6 = (f32[8192]{0:T(1024)S(1)}, f32[8192]{0:T(1024)}, u32[]{:S(2)}) copy-start(f32[8192]{0:T(1024)} %param.10) | copy-start | bytes 98308
  232.3 43.5 %slice-start.1 = ((s8[8388608]{0:T(1024)(128)(4,1)}), s8[4194304]{0:T(1024)(128)(4,1)S(1)}, s32[]{:S(2)}) async-start(s8[8388608]{0:T(1024)(128)(4,1)} %bitcast.208), calls=%async_computation.3 | async-start | bytes 8388608
  232.7 21.3 %collective-permute-start.1 = (bf16[1,1601,256]{2,1,0:T(8,128)(2,1)S(1)}, bf16[1,1601,256]{2,1,0:T(8,128)(2,1)S(1)}, u32[]{:S(2)}, u32[]{:S(2)}) collective-permute-start(bf16[1,1601,256]{2,1,0:T(8,128)(2,1)S(1)} %pad_maximum_fusion.1), channel_id=1, source_target_pairs={{0,32},{8,40},{16,48},{24,56},{32,64},{40,72},{48,80},{56,88},{64,... | collective-permute-start | bytes 2459144 | tf_op jit(solution)/shard_map/ppermute | solution.py:15
  236.1 36.3 %collective-permute-start = (bf16[1,1601,256]{2,1,0:T(8,128)(2,1)S(1)}, bf16[1,1601,256]{2,1,0:T(8,128)(2,1)S(1)}, u32[]{:S(2)}, u32[]{:S(2)}) collective-permute-start(bf16[1,1601,256]{2,1,0:T(8,128)(2,1)S(1)} %pad_maximum_fusion.1), channel_id=1, source_target_pairs={{0,16},{8,24},{16,32},{24,40},{32,48},{40,56},{48,64},{56,72},{64,... | collective-permute-start | bytes 2459144 | tf_op jit(solution)/shard_map/ppermute | solution.py:15
  274.1 7.0 %collective-permute-start.2 = (bf16[3,1,1601,256]{3,2,1,0:T(8,128)(2,1)}, bf16[3,1,1601,256]{3,2,1,0:T(8,128)(2,1)S(1)}, u32[]{:S(2)}, u32[]{:S(2)}) collective-permute-start(bf16[3,1,1601,256]{3,2,1,0:T(8,128)(2,1)} %pad_maximum_fusion), channel_id=1, source_target_pairs={{0,8},{8,0},{16,24},{24,16},{32,40},{40,32},{48,56},{56,48},{64,72... | collective-permute-start | bytes 7377416 | tf_op jit(solution)/shard_map/ppermute | solution.py:119
  275.8 2.6 copy-start.5
  291.6 2.7 copy-start.1
Sparse Core Ops, SparseCore 0:
  10.1 120.1 all-gather.2

commit v8 on v5

--- a/solution.py
+++ b/solution.py
@@ -6,6 +6,7 @@
 from jax.sharding import PartitionSpec as P
 
 KEY_VALUE_HEADS = 8
+SEQ_AXIS = "seq"
 IMAGE_LOOKBACK = 4
 
 
@@ -102,9 +103,13 @@
             for pair in range(pairs_per_block)
         ]
     )
-    own_kv = lax.psum_scatter(partials, "fsdp", scatter_dimension=0, tiled=True).astype(jnp.float32)
-    key_part = rms_scale(own_kv[..., :head_dim], key_gain)
-    packed = jnp.concatenate([key_part, own_kv[..., head_dim:]], axis=-1).astype(jnp.bfloat16)
+    own_kv = lax.psum_scatter(partials, "fsdp", scatter_dimension=0, tiled=True)
+
+    def finish(summed):
+        summed = summed.astype(jnp.float32)
+        key_part = rms_scale(summed[..., :head_dim], key_gain)
+        return jnp.concatenate([key_part, summed[..., head_dim:]], axis=-1).astype(jnp.bfloat16)
+
     span_index = lax.axis_index("seq")
     image_ids = span_index - jnp.arange(IMAGE_LOOKBACK + 1, dtype=jnp.int32)
     admitted = (image_ids >= 0) & (jnp.take(admission[0], jnp.maximum(image_ids, 0)) == 1)
@@ -112,18 +117,16 @@
     nearest = jnp.argmax(earlier_admitted)
     farthest = IMAGE_LOOKBACK - 1 - jnp.argmax(earlier_admitted[::-1])
     admitted_count = jnp.sum(earlier_admitted.astype(jnp.int32))
-    two_behind = from_behind(packed, "seq", 2)
-    four_behind = from_behind(packed, "seq", 4)
-    partner = lax.ppermute(
-        jnp.stack([packed, two_behind, four_behind]),
-        "seq",
-        [(source, source ^ 1) for source in range(lax.axis_size("seq"))],
-    )
+    two_behind = from_behind(own_kv, SEQ_AXIS, 2)
+    four_behind = from_behind(own_kv, SEQ_AXIS, 4)
+    swap = [(source, source ^ 1) for source in range(lax.axis_size(SEQ_AXIS))]
+    partner_own = lax.ppermute(own_kv, SEQ_AXIS, swap)
+    partner_far = lax.ppermute(jnp.stack([two_behind, four_behind]), SEQ_AXIS, swap)
     first_core = span_index % 2 == 0
     received = [
-        jnp.where(first_core, partner[1], partner[0]),
+        jnp.where(first_core, partner_far[0], partner_own),
         two_behind,
-        jnp.where(first_core, partner[2], partner[1]),
+        jnp.where(first_core, partner_far[1], partner_far[0]),
         four_behind,
     ]
 
@@ -133,7 +136,8 @@
             chosen = jnp.where(slot == distance, received[distance], chosen)
         return chosen
 
-    earlier = jnp.concatenate([pick(nearest), pick(farthest)], axis=1)
+    earlier = jnp.concatenate([finish(pick(nearest)), finish(pick(farthest))], axis=1)
+    packed = finish(own_kv)
     image_tokens = packed.shape[1]
     earlier_live = jnp.concatenate(
         [

time: 298 us -> 304 us (1.020)
  the two profiles are of different devices: /device:TPU:129 before, /device:TPU:133 now
where the time goes in v8:
time: 304 us; the launch traced here: 298 us
  waiting for transfers between devices  192 us (63%)
  local copies, waits for them, and re-layouts  35.8 us (12%)
  matrix products  31.1 us (10%)
  between operations  17.5 us (6%)
  other arithmetic  15.1 us (5%)
  starting transfers between devices  6.75 us (2%)
    all_gather x1, waiting for transfers between devices, on_device(): lax.all_gather(jnp.concatenate([kv_as_rows, query_weight], axis=0), 'seq'...  115 us
    reduce_scatter x1, waiting for transfers between devices, on_device(): own_kv = lax.psum_scatter(partials, 'fsdp', scatter_dimension=0, tiled=True)  51.1 us
    ppermute x2, waiting for transfers between devices, from_behind(): lax.ppermute(value, axis, [(source, source + steps) for source in range(i...  25.6 us
    dot_general x8, matrix products, on_device(): jnp.dot(features, both[:, block * kv_rows:(block + 1) * kv_rows, pair * p...  15.5 us
    reshape x1, local copies, waits for them, and re-layouts, on_device(): query_block = both[:, column_blocks * kv_rows:].reshape(-1, query_width)  11.4 us
    another operation x1, local copies, waits for them, and re-layouts, on_device(): jnp.stack([two_behind, four_behind])  8.95 us
    slice x1, local copies, waits for them, and re-layouts, on_device(): query_block = both[:, column_blocks * kv_rows:].reshape(-1, query_width)  7.46 us
    dot_general x1, matrix products, on_device(): queries = jnp.dot(normed, query_block, preferred_element_type=jnp.float32)  6.58 us
  transfers between devices with their start and end apart: 6, of which 4 were waited for; matrix products, arithmetic and copies ran while one was open for 12% of the time, Pallas kernels for 0%

profile of v8, /device:TPU:133, one launch (start us, length us, event | category | flops | bytes accessed | tf_op | source)
XLA Modules:
  0.0 298.2 jit_solution(17125306910068908868)
XLA Ops:
  9.5 115.2 %all-gather.3.cloned.1.call-done = bf16[12288,512]{1,0:T(8,128)(2,1)} async-done(((bf16[384,512]{1,0:T(8,128)(2,1)}), bf16[12288,512]{1,0:T(8,128)(2,1)}) %all-gather.3.cloned.1.call-update) | async-done | bytes 12582928 | tf_op jit(solution)/shard_map/all_gather | solution.py:83
  124.7 2.7 fusion.149
  127.4 1.9 fusion.105
  129.3 1.9 fusion.99
  131.2 1.9 fusion.93
  133.2 1.9 fusion.87
  135.1 1.9 fusion.81
  137.0 2.0 fusion.75
  139.0 1.9 fusion.69
  140.9 1.9 fusion.63
  149.7 3.1 %fusion.3 = f32[256]{0:T(256)S(1)} fusion(bf16[256,8192]{1,0:T(8,128)(2,1)} %param.8), kind=kLoop, calls=%fused_computation.8 | loop fusion | flops 6291200 | bytes 4195328 | tf_op jit(solution)/shard_map/reduce_sum | solution.py:20
  152.8 7.5 %slice.107 = bf16[32,256,512]{2,1,0:T(8,128)(2,1)} slice(bf16[32,384,512]{2,1,0:T(8,128)(2,1)} %bitcast.200), slice={[0:32], [128:384], [0:512]} | slice | bytes 16777216 | tf_op jit(solution)/shard_map/slice | solution.py:86
  160.3 11.4 %copy.21 = bf16[8192,512]{0,1:T(8,128)(2,1)} copy(bf16[8192,512]{1,0:T(8,128)(2,1)} %bitcast.198) | data formatting | bytes 16777216 | tf_op jit(solution)/shard_map/reshape | solution.py:86
  171.6 51.1 %reduce-scatter.2.cloned.1.call-done = bf16[1,1601,256]{2,1,0:T(8,128)(2,1)} async-done(((bf16[8,1601,256]{2,1,0:T(8,128)(2,1)}), bf16[1,1601,256]{2,1,0:T(8,128)(2,1)}) %reduce-scatter.2.cloned.1.call-update) | async-done | bytes 819728 | tf_op jit(solution)/shard_map/reduce_scatter | solution.py:106
  222.8 2.3 collective-permute-start.1
  225.0 2.8 collective-permute-start
  227.8 6.6 %multiply_reduce_fusion = (f32[256,4]{0,1:T(4,128)S(1)}, f32[256,4,128]{2,0,1:T(8,128)S(1)}) fusion(bf16[4,128,8192]{2,1,0:T(8,128)(2,1)} %bitcast.201, bf16[256,8192]{1,0:T(8,128)(2,1)} %param.8, f32[8192]{0:T(1024)S(1)} %copy-done.6, f32[256]{0:T(256)S(1)} %add_rsqrt_fusion.4), kind=kOutput, calls=%fused_computation.96 | convolution fusion | flops 2156133376 | bytes 13145088 | tf_op jit(solution)/shard_map/dot_general | solution.py:87
  234.5 10.9 %collective-permute-done.1 = bf16[1,1601,256]{2,1,0:T(8,128)(2,1)S(1)} collective-permute-done((bf16[1,1601,256]{2,1,0:T(8,128)(2,1)}, bf16[1,1601,256]{2,1,0:T(8,128)(2,1)S(1)}, u32[]{:S(2)}, u32[]{:S(2)}) %collective-permute-start.1) | collective-permute-done | bytes 819744 | tf_op jit(solution)/shard_map/ppermute | solution.py:16
  245.3 14.7 %collective-permute-done = bf16[1,1601,256]{2,1,0:T(8,128)(2,1)S(1)} collective-permute-done((bf16[1,1601,256]{2,1,0:T(8,128)(2,1)}, bf16[1,1601,256]{2,1,0:T(8,128)(2,1)S(1)}, u32[]{:S(2)}, u32[]{:S(2)}) %collective-permute-start) | collective-permute-done | bytes 819744 | tf_op jit(solution)/shard_map/ppermute | solution.py:16
  260.2 9.0 %copy.17 = bf16[2,1,1601,256]{3,0,2,1:T(2,128)(2,1)S(1)} copy(bf16[2,1,1601,256]{3,2,1,0:T(8,128)(2,1)S(1)} %pad_maximum_fusion) | data formatting | bytes 3278848 | tf_op jit(solution)/shard_map/stack | solution.py:124
  273.9 2.3 fusion.150
  278.6 1.9 fusion
  280.6 3.8 %fusion.1 = f32[1024]{0:T(1024)S(1)} fusion(f32[1024,3202]{0,1:T(8,128)S(1)} %get-tuple-element.29, f32[1024]{0:T(1024)S(1)} %compare_select_fusion, pred[3202]{0:T(1024)(128)(4,1)S(1)} %concatenate.44), kind=kLoop, calls=%fused_computation.6 | loop fusion | flops 13114368 | bytes 13126786 | tf_op jit(solution)/shard_map/reduce_sum | solution.py:31
  284.4 4.4 %fusion.114 = f32[1024,128]{1,0:T(8,128)S(1)} fusion(f32[1024,3202]{0,1:T(8,128)S(1)} %get-tuple-element.29, f32[1024]{0:T(1024)S(1)} %compare_select_fusion, pred[3202]{0:T(1024)(128)(4,1)S(1)} %concatenate.44, bf16[1,3202,256]{2,1,0:T(8,128)(2,1)S(1)} %maximum_maximum_fusion, f32[1024]{0:T(1024)S(1)} %get-tuple-element.11), kind=kOutput, calls=%fused_computation.68 | convolution fusion | flops 852631552 | bytes 14497792 | tf_op jit(solution)/shard_map/kqn,knd->kqd/dot_general | solution.py:32
  (59 shorter events, 15.8 us)
Async XLA Ops:
  6.5 120.9 %copy-start = (bf16[1,1601,1024]{2,1,0:T(8,128)(2,1)S(1)}, bf16[1,1601,1024]{2,1,0:T(8,128)(2,1)}, u32[]{:S(2)}) copy-start(bf16[1,1601,1024]{2,1,0:T(8,128)(2,1)} %param.9) | copy-start | bytes 9836548
  6.5 118.2 %all-gather.3.cloned.1.call-start = ((), (), s32[]{:S(2)}) async-start(), calls=%async_computation.2 | async-start | bytes 12976128 | tf_op jit(solution)/shard_map/all_gather | solution.py:83
  9.5 213.3 %reduce-scatter.2.cloned.1.call-start = ((), (), s32[]{:S(2)}) async-start(), calls=%async_computation.1 | async-start | bytes 7409664 | tf_op jit(solution)/shard_map/reduce_scatter | solution.py:106
  140.9 2.0 copy-start.2
  160.3 67.6 %copy-start.6 = (f32[8192]{0:T(1024)S(1)}, f32[8192]{0:T(1024)}, u32[]{:S(2)}) copy-start(f32[8192]{0:T(1024)} %param.10) | copy-start | bytes 98308
  222.8 22.6 %collective-permute-start.1 = (bf16[1,1601,256]{2,1,0:T(8,128)(2,1)}, bf16[1,1601,256]{2,1,0:T(8,128)(2,1)S(1)}, u32[]{:S(2)}, u32[]{:S(2)}) collective-permute-start(bf16[1,1601,256]{2,1,0:T(8,128)(2,1)} %reduce-scatter.2.cloned.1.call-done), channel_id=1, source_target_pairs={{0,32},{8,40},{16,48},{24,56},{32,64},{40,72},{48,80},{56,88},{64,... | collective-permute-start | bytes 2459144 | tf_op jit(solution)/shard_map/ppermute | solution.py:16
  225.0 35.0 %collective-permute-start = (bf16[1,1601,256]{2,1,0:T(8,128)(2,1)}, bf16[1,1601,256]{2,1,0:T(8,128)(2,1)S(1)}, u32[]{:S(2)}, u32[]{:S(2)}) collective-permute-start(bf16[1,1601,256]{2,1,0:T(8,128)(2,1)} %reduce-scatter.2.cloned.1.call-done), channel_id=1, source_target_pairs={{0,16},{8,24},{16,32},{24,40},{32,48},{40,56},{48,64},{56,72},{64,... | collective-permute-start | bytes 2459144 | tf_op jit(solution)/shard_map/ppermute | solution.py:16
  234.4 36.3 %copy-start.5 = (f32[128]{0:T(128)S(1)}, f32[128]{0:T(128)}, u32[]{:S(2)}) copy-start(f32[128]{0:T(128)} %param.13) | copy-start | bytes 1540
  234.4 36.5 %copy-start.3 = (bf16[1,1601,256]{2,1,0:T(8,128)(2,1)S(1)}, bf16[1,1601,256]{2,1,0:T(8,128)(2,1)}, u32[]{:S(2)}) copy-start(bf16[1,1601,256]{2,1,0:T(8,128)(2,1)} %reduce-scatter.2.cloned.1.call-done) | copy-start | bytes 2459140
  234.4 36.9 %copy-start.4 = (f32[128]{0:T(128)S(1)}, f32[128]{0:T(128)}, u32[]{:S(2)}) copy-start(f32[128]{0:T(128)} %param.14) | copy-start | bytes 1540
  269.1 4.8 %collective-permute-start.2 = (bf16[2,1,1601,256]{3,0,2,1:T(2,128)(2,1)S(1)}, bf16[2,1,1601,256]{3,0,2,1:T(2,128)(2,1)S(1)}, u32[]{:S(2)}, u32[]{:S(2)}) collective-permute-start(bf16[2,1,1601,256]{3,0,2,1:T(2,128)(2,1)S(1)} %copy.17), channel_id=1, source_target_pairs={{0,8},{8,0},{16,24},{24,16},{32,40},{40,32},{48,56},{56,48},{64,72... | collective-permute-start | bytes 4918280 | tf_op jit(solution)/shard_map/ppermute | solution.py:124
  270.9 5.3 %collective-permute-start.3 = (bf16[1,1601,256]{2,1,0:T(8,128)(2,1)S(1)}, bf16[1,1601,256]{2,1,0:T(8,128)(2,1)S(1)}, u32[]{:S(2)}, u32[]{:S(2)}) collective-permute-start(bf16[1,1601,256]{2,1,0:T(8,128)(2,1)S(1)} %copy-done.3), channel_id=1, source_target_pairs={{0,8},{8,0},{16,24},{24,16},{32,40},{40,32},{48,56},{56,48},{64,72... | collective-permute-start | bytes 2459144 | tf_op jit(solution)/shard_map/ppermute | solution.py:123
  288.8 2.6 copy-start.1
Sparse Core Ops, SparseCore 0:
  10.1 114.5 all-gather.2
  143.0 79.7 reduce-scatter.1

commit v9 on v3

--- a/solution.py
+++ b/solution.py
@@ -88,29 +88,28 @@
         jnp.bfloat16
     )
     features = images[0]
-    score_product = jnp.concatenate(
-        [
-            jnp.dot(
-                features,
-                both[:, block * kv_rows : (block + 1) * kv_rows].reshape(-1, query_width),
-                preferred_element_type=jnp.float32,
-            )
-            for block in range(column_blocks)
-        ],
-        axis=1,
-    )
-    own_kv = lax.psum_scatter(
-        score_product.reshape(
-            features.shape[0], local_key_value * lax.axis_size("fsdp"), 2 * head_dim
+    pair_width = 2 * head_dim
+    pairs_per_block = query_width // pair_width
+
+    def reduced_half(rows):
+        partials = jnp.stack(
+            [
+                jnp.dot(
+                    rows,
+                    both[:, block * kv_rows : (block + 1) * kv_rows, pair * pair_width : (pair + 1) * pair_width]
+                    .reshape(-1, pair_width),
+                    preferred_element_type=jnp.float32,
+                ).astype(jnp.bfloat16)
+                for block in range(column_blocks)
+                for pair in range(pairs_per_block)
+            ]
         )
-        .transpose(1, 0, 2)
-        .astype(jnp.bfloat16),
-        "fsdp",
-        scatter_dimension=0,
-        tiled=True,
-    ).astype(jnp.float32)
-    key_part = rms_scale(own_kv[..., :head_dim], key_gain)
-    packed = jnp.concatenate([key_part, own_kv[..., head_dim:]], axis=-1).astype(jnp.bfloat16)
+        own_kv = lax.psum_scatter(partials, "fsdp", scatter_dimension=0, tiled=True).astype(jnp.float32)
+        key_part = rms_scale(own_kv[..., :head_dim], key_gain)
+        return jnp.concatenate([key_part, own_kv[..., head_dim:]], axis=-1).astype(jnp.bfloat16)
+
+    token_cut = (features.shape[0] // 16) * 8
+    packed_halves = [reduced_half(features[:token_cut]), reduced_half(features[token_cut:])]
     span_index = lax.axis_index("seq")
     image_ids = span_index - jnp.arange(IMAGE_LOOKBACK + 1, dtype=jnp.int32)
     admitted = (image_ids >= 0) & (jnp.take(admission[0], jnp.maximum(image_ids, 0)) == 1)
@@ -118,7 +117,26 @@
     nearest = jnp.argmax(earlier_admitted)
     farthest = IMAGE_LOOKBACK - 1 - jnp.argmax(earlier_admitted[::-1])
     admitted_count = jnp.sum(earlier_admitted.astype(jnp.int32))
-    received = [from_behind(packed, "seq", distance) for distance in range(1, IMAGE_LOOKBACK + 1)]
+    first_core = span_index % 2 == 0
+    received_halves = []
+    for half in packed_halves:
+        two_behind = from_behind(half, "seq", 2)
+        four_behind = from_behind(half, "seq", 4)
+        partner = lax.ppermute(
+            jnp.stack([half, two_behind, four_behind]),
+            "seq",
+            [(source, source ^ 1) for source in range(lax.axis_size("seq"))],
+        )
+        received_halves.append(
+            [
+                jnp.where(first_core, partner[1], partner[0]),
+                two_behind,
+                jnp.where(first_core, partner[2], partner[1]),
+                four_behind,
+            ]
+        )
+    received = [jnp.concatenate(pieces, axis=1) for pieces in zip(*received_halves)]
+    packed = jnp.concatenate(packed_halves, axis=1)
 
     def pick(slot):
         chosen = received[-1]

time: 319 us -> 285 us (0.89); the launches traced: 313 us -> 284 us
  waiting for transfers between devices: 207 us -> 170 us
  starting transfers between devices: 12.6 us -> 20.1 us
  matrix products: 23.4 us -> 28.7 us
  local copies, waits for them, and re-layouts: 34.5 us -> 30.7 us
    ppermute x4, waiting for transfers between devices: 49.5 us -> 9.09 us  [from_behind(): lax.ppermute(value, axis, [(source, source + steps) for source in range(i...]
    ppermute x0 -> x2, starting transfers between devices: none -> 9.33 us  [on_device(): lax.ppermute(jnp.stack([half, two_behind, four_behind]), 'seq', [(source,...]
    dot_general x4 -> x16, matrix products: 7.47 us -> 12.8 us  [reduced_half(): jnp.dot(rows, both[:, block * kv_rows:(block + 1) * kv_rows, pair * pair_...]
    convert_element_type x2 -> x0, local copies, waits for them, and re-layouts: 4.61 us -> none  [on_device(): own_kv = lax.psum_scatter(score_product.reshape(features.shape[0], local_...]
    reduce_scatter x1 -> x2, waiting for transfers between devices: 42.6 us -> 44.7 us  [reduced_half(): lax.psum_scatter(partials, 'fsdp', scatter_dimension=0, tiled=True)]
  transfers between devices with their start and end apart: 6 -> 9, of which waited for: 6 -> 6; matrix products, arithmetic and copies ran while one was open for 11% -> 17% of each run, Pallas kernels for 0% -> 0%
where the time goes in v9:
time: 285 us; the launch traced here: 284 us
  waiting for transfers between devices  170 us (60%)
  local copies, waits for them, and re-layouts  30.7 us (11%)
  matrix products  28.7 us (10%)
  starting transfers between devices  20.1 us (7%)
  between operations  17.6 us (6%)
  other arithmetic  16.7 us (6%)
    all_gather x1, waiting for transfers between devices, on_device(): lax.all_gather(jnp.concatenate([kv_as_rows, query_weight], axis=0), 'seq'...  115 us
    reduce_scatter x2, waiting for transfers between devices, reduced_half(): lax.psum_scatter(partials, 'fsdp', scatter_dimension=0, tiled=True)  44.7 us
    dot_general x16, matrix products, reduced_half(): jnp.dot(rows, both[:, block * kv_rows:(block + 1) * kv_rows, pair * pair_...  12.8 us
    reshape x1, local copies, waits for them, and re-layouts, on_device(): query_block = both[:, column_blocks * kv_rows:].reshape(-1, query_width)  11.6 us
    ppermute x4, starting transfers between devices, from_behind(): lax.ppermute(value, axis, [(source, source + steps) for source in range(i...  10.5 us
    ppermute x2, starting transfers between devices, on_device(): lax.ppermute(jnp.stack([half, two_behind, four_behind]), 'seq', [(source,...  9.33 us
    ppermute x4, waiting for transfers between devices, from_behind(): lax.ppermute(value, axis, [(source, source + steps) for source in range(i...  9.09 us
    slice x1, local copies, waits for them, and re-layouts, on_device(): query_block = both[:, column_blocks * kv_rows:].reshape(-1, query_width)  7.56 us
  transfers between devices with their start and end apart: 9, of which 6 were waited for; matrix products, arithmetic and copies ran while one was open for 17% of the time, Pallas kernels for 0%

profile of v9, /device:TPU:133, one launch (start us, length us, event | category | flops | bytes accessed | tf_op | source)
XLA Modules:
  0.0 284.0 jit_solution(5135250171910001833)
XLA Ops:
  7.6 1.8 pad_maximum_fusion.7
  9.4 115.3 %all-gather.3.cloned.1.call-done = bf16[12288,512]{1,0:T(8,128)(2,1)} async-done(((bf16[384,512]{1,0:T(8,128)(2,1)}), bf16[12288,512]{1,0:T(8,128)(2,1)}) %all-gather.3.cloned.1.call-update) | async-done | bytes 12582928 | tf_op jit(solution)/shard_map/all_gather | solution.py:82
  124.7 2.8 fusion.249
  132.9 1.8 copy-done.3
  134.9 2.3 fusion.154
  137.3 2.1 fusion.148
  143.1 1.7 copy-done.2
  151.6 3.1 %fusion.3 = f32[256]{0:T(256)S(1)} fusion(bf16[256,8192]{1,0:T(8,128)(2,1)} %param.8), kind=kLoop, calls=%fused_computation.8 | loop fusion | flops 6291200 | bytes 4195328 | tf_op jit(solution)/shard_map/reduce_sum | solution.py:19
  154.8 7.6 %slice.128 = bf16[32,256,512]{2,1,0:T(8,128)(2,1)} slice(bf16[32,384,512]{2,1,0:T(8,128)(2,1)} %bitcast.323), slice={[0:32], [128:384], [0:512]} | slice | bytes 16777216 | tf_op jit(solution)/shard_map/slice | solution.py:85
  162.3 11.6 %copy.15 = bf16[8192,512]{0,1:T(8,128)(2,1)} copy(bf16[8192,512]{1,0:T(8,128)(2,1)} %bitcast.321) | data formatting | bytes 16777216 | tf_op jit(solution)/shard_map/reshape | solution.py:85
  173.9 6.7 %multiply_reduce_fusion = (f32[256,4]{0,1:T(4,128)S(1)}, f32[256,4,128]{2,0,1:T(8,128)S(1)}) fusion(bf16[4,128,8192]{2,1,0:T(8,128)(2,1)} %bitcast.324, bf16[256,8192]{1,0:T(8,128)(2,1)} %param.8, f32[8192]{0:T(1024)S(1)} %copy-done.25, f32[256]{0:T(256)S(1)} %add_rsqrt_fusion.3), kind=kOutput, calls=%fused_computation.125 | convolution fusion | flops 2156133376 | bytes 13145088 | tf_op jit(solution)/shard_map/dot_general | solution.py:86
  184.2 4.4 %collective-permute-start = (bf16[1,800,256]{2,1,0:T(8,128)(2,1)S(1)}, bf16[1,800,256]{2,1,0:T(8,128)(2,1)S(1)}, u32[]{:S(2)}, u32[]{:S(2)}) collective-permute-start(bf16[1,800,256]{2,1,0:T(8,128)(2,1)S(1)} %pad_maximum_fusion.6), channel_id=1, source_target_pairs={{0,16},{8,24},{16,32},{24,40},{32,48},{40,56},{48,64},{56,72},{64,... | collective-permute-start | bytes 1228808 | tf_op jit(solution)/shard_map/ppermute | solution.py:15
  188.6 2.3 collective-permute-start.1
  191.1 43.9 %reduce-scatter.5.cloned.1.call-done = bf16[1,801,256]{2,1,0:T(8,128)(2,1)} async-done(((bf16[8,801,256]{2,1,0:T(8,128)(2,1)}), bf16[1,801,256]{2,1,0:T(8,128)(2,1)}) %reduce-scatter.5.cloned.1.call-update) | async-done | bytes 410128 | tf_op jit(solution)/shard_map/reduce_scatter | solution.py:107
  237.6 1.9 collective-permute-start.3
  239.6 1.9 collective-permute-start.4
  243.0 4.5 %collective-permute-start.2 = (bf16[3,1,800,256]{3,2,1,0:T(8,128)(2,1)S(1)}, bf16[3,1,800,256]{3,2,1,0:T(8,128)(2,1)S(1)}, u32[]{:S(2)}, u32[]{:S(2)}) collective-permute-start(bf16[3,1,800,256]{3,2,1,0:T(8,128)(2,1)S(1)} %pad_maximum_fusion.1), channel_id=1, source_target_pairs={{0,8},{8,0},{16,24},{24,16},{32,40},{40,32},{48,56},{56,48},{64,72... | collective-permute-start | bytes 3686408 | tf_op jit(solution)/shard_map/ppermute | solution.py:125
  248.3 8.3 %collective-permute-done.4 = bf16[1,801,256]{2,1,0:T(8,128)(2,1)S(1)} collective-permute-done((bf16[1,801,256]{2,1,0:T(8,128)(2,1)S(1)}, bf16[1,801,256]{2,1,0:T(8,128)(2,1)S(1)}, u32[]{:S(2)}, u32[]{:S(2)}) %collective-permute-start.4) | collective-permute-done | bytes 410144 | tf_op jit(solution)/shard_map/ppermute | solution.py:15
  256.7 4.8 %collective-permute-start.5 = (bf16[3,1,801,256]{3,2,1,0:T(8,128)(2,1)S(1)}, bf16[3,1,801,256]{3,2,1,0:T(8,128)(2,1)S(1)}, u32[]{:S(2)}, u32[]{:S(2)}) collective-permute-start(bf16[3,1,801,256]{3,2,1,0:T(8,128)(2,1)S(1)} %pad_maximum_fusion), channel_id=1, source_target_pairs={{0,8},{8,0},{16,24},{24,16},{32,40},{40,32},{48,56},{56,48},{64,72... | collective-permute-start | bytes 3691016 | tf_op jit(solution)/shard_map/ppermute | solution.py:125
  261.5 1.4 fusion.10
  264.8 2.0 fusion
  266.8 3.5 %fusion.1 = f32[1024]{0:T(1024)S(1)} fusion(f32[1024,3202]{0,1:T(8,128)S(1)} %get-tuple-element.29, f32[1024]{0:T(1024)S(1)} %compare_select_fusion, pred[3202]{0:T(1024)(128)(4,1)S(1)} %concatenate.152), kind=kLoop, calls=%fused_computation.6 | loop fusion | flops 13114368 | bytes 13126786 | tf_op jit(solution)/shard_map/reduce_sum | solution.py:30
  270.4 4.4 %fusion.106 = f32[1024,128]{1,0:T(8,128)S(1)} fusion(f32[1024,3202]{0,1:T(8,128)S(1)} %get-tuple-element.29, f32[1024]{0:T(1024)S(1)} %compare_select_fusion, pred[3202]{0:T(1024)(128)(4,1)S(1)} %concatenate.152, bf16[1,1601,256]{2,1,0:T(8,128)(2,1)S(1)} %get-tuple-element.20, bf16[1,1601,256]{2,1,0:T(8,128)(2,1)S(1)} %get-tuple-element.21, ...), kind=kOutput, calls=%fused_computation.78 | convolution fusion | flops 854270976 | bytes 15290498 | tf_op jit(solution)/shard_map/kqn,knd->kqd/dot_general | solution.py:31
  274.8 1.7 fusion.208
  (124 shorter events, 24.6 us)
Async XLA Ops:
  6.5 138.3 %copy-start = (s32[1,32]{1,0:T(1,128)S(1)}, s32[1,32]{1,0:T(1,128)}, u32[]{:S(2)}) copy-start(s32[1,32]{1,0:T(1,128)} %param.15) | copy-start | bytes 388
  6.5 118.2 %all-gather.3.cloned.1.call-start = ((), (), s32[]{:S(2)}) async-start(), calls=%async_computation.4 | async-start | bytes 12976128 | tf_op jit(solution)/shard_map/all_gather | solution.py:82
  9.3 172.3 %reduce-scatter.3.cloned.1.call-start = ((), (), s32[]{:S(2)}) async-start(), calls=%async_computation.2 | async-start | bytes 3686400 | tf_op jit(solution)/shard_map/reduce_scatter | solution.py:107
  124.7 3.3 %copy-start.23 = (bf16[1,1601,1024]{2,1,0:T(8,128)(2,1)S(1)}, bf16[1,1601,1024]{2,1,0:T(8,128)(2,1)}, u32[]{:S(2)}) copy-start(bf16[1,1601,1024]{2,1,0:T(8,128)(2,1)} %param.9) | copy-start | bytes 9836548
  127.6 2.8 copy-start.12
  127.6 3.4 %copy-start.10 = (bf16[32,32,256]{2,1,0:T(8,128)(2,1)}, bf16[32,32,256]{2,1,0:T(8,128)(2,1)S(1)}, u32[]{:S(2)}) copy-start(bf16[32,32,256]{2,1,0:T(8,128)(2,1)S(1)} %get-tuple-element.14) | copy-start | bytes 1572868
  127.6 4.0 %copy-start.8 = (bf16[32,32,256]{2,1,0:T(8,128)(2,1)}, bf16[32,32,256]{2,1,0:T(8,128)(2,1)S(1)}, u32[]{:S(2)}) copy-start(bf16[32,32,256]{2,1,0:T(8,128)(2,1)S(1)} %get-tuple-element.13) | copy-start | bytes 1572868
  127.6 4.6 %copy-start.6 = (bf16[32,32,256]{2,1,0:T(8,128)(2,1)}, bf16[32,32,256]{2,1,0:T(8,128)(2,1)S(1)}, u32[]{:S(2)}) copy-start(bf16[32,32,256]{2,1,0:T(8,128)(2,1)S(1)} %get-tuple-element.12) | copy-start | bytes 1572868
  134.6 100.4 %reduce-scatter.5.cloned.1.call-start = ((), (), s32[]{:S(2)}) async-start(), calls=%async_computation.3 | async-start | bytes 3723264 | tf_op jit(solution)/shard_map/reduce_scatter | solution.py:107
  134.9 2.4 copy-start.19
  134.9 4.5 %copy-start.17 = (bf16[32,32,256]{2,1,0:T(8,128)(2,1)S(1)}, bf16[32,32,256]{2,1,0:T(8,128)(2,1)}, u32[]{:S(2)}) copy-start(bf16[32,32,256]{2,1,0:T(8,128)(2,1)} %copy-done.16) | copy-start | bytes 1572868
  134.9 4.5 %copy-start.24 = (bf16[1,1601,1024]{2,1,0:T(8,128)(2,1)S(1)}, bf16[1,1601,1024]{2,1,0:T(8,128)(2,1)}, u32[]{:S(2)}) copy-start(bf16[1,1601,1024]{2,1,0:T(8,128)(2,1)} %param.9) | copy-start | bytes 9836548
  137.3 2.7 copy-start.15
  162.3 11.6 %copy-start.25 = (f32[8192]{0:T(1024)S(1)}, f32[8192]{0:T(1024)}, u32[]{:S(2)}) copy-start(f32[8192]{0:T(1024)} %param.10) | copy-start | bytes 98308
  173.9 6.8 %copy-start.22 = (f32[128]{0:T(128)S(1)}, f32[128]{0:T(128)}, u32[]{:S(2)}) copy-start(f32[128]{0:T(128)} %param.13) | copy-start | bytes 1540
  173.9 10.1 %copy-start.21 = (f32[128]{0:T(128)S(1)}, f32[128]{0:T(128)}, u32[]{:S(2)}) copy-start(f32[128]{0:T(128)} %param.14) | copy-start | bytes 1540
  181.7 9.2 %copy-start.5 = (bf16[1,800,256]{2,1,0:T(8,128)(2,1)S(1)}, bf16[1,800,256]{2,1,0:T(8,128)(2,1)}, u32[]{:S(2)}) copy-start(bf16[1,800,256]{2,1,0:T(8,128)(2,1)} %reduce-scatter.3.cloned.1.call-done) | copy-start | bytes 1228804
  184.2 58.6 %collective-permute-start = (bf16[1,800,256]{2,1,0:T(8,128)(2,1)S(1)}, bf16[1,800,256]{2,1,0:T(8,128)(2,1)S(1)}, u32[]{:S(2)}, u32[]{:S(2)}) collective-permute-start(bf16[1,800,256]{2,1,0:T(8,128)(2,1)S(1)} %pad_maximum_fusion.6), channel_id=1, source_target_pairs={{0,16},{8,24},{16,32},{24,40},{32,48},{40,56},{48,64},{56,72},{64,... | collective-permute-start | bytes 1228808 | tf_op jit(solution)/shard_map/ppermute | solution.py:15
  188.6 54.2 %collective-permute-start.1 = (bf16[1,800,256]{2,1,0:T(8,128)(2,1)S(1)}, bf16[1,800,256]{2,1,0:T(8,128)(2,1)S(1)}, u32[]{:S(2)}, u32[]{:S(2)}) collective-permute-start(bf16[1,800,256]{2,1,0:T(8,128)(2,1)S(1)} %pad_maximum_fusion.6), channel_id=1, source_target_pairs={{0,32},{8,40},{16,48},{24,56},{32,64},{40,72},{48,80},{56,88},{64,... | collective-permute-start | bytes 1228808 | tf_op jit(solution)/shard_map/ppermute | solution.py:15
  237.6 10.6 %collective-permute-start.3 = (bf16[1,801,256]{2,1,0:T(8,128)(2,1)S(1)}, bf16[1,801,256]{2,1,0:T(8,128)(2,1)S(1)}, u32[]{:S(2)}, u32[]{:S(2)}) collective-permute-start(bf16[1,801,256]{2,1,0:T(8,128)(2,1)S(1)} %pad_maximum_fusion.5), channel_id=1, source_target_pairs={{0,16},{8,24},{16,32},{24,40},{32,48},{40,56},{48,64},{56,72},{64,... | collective-permute-start | bytes 1230344 | tf_op jit(solution)/shard_map/ppermute | solution.py:15
  239.6 17.0 %collective-permute-start.4 = (bf16[1,801,256]{2,1,0:T(8,128)(2,1)S(1)}, bf16[1,801,256]{2,1,0:T(8,128)(2,1)S(1)}, u32[]{:S(2)}, u32[]{:S(2)}) collective-permute-start(bf16[1,801,256]{2,1,0:T(8,128)(2,1)S(1)} %pad_maximum_fusion.5), channel_id=1, source_target_pairs={{0,32},{8,40},{16,48},{24,56},{32,64},{40,72},{48,80},{56,88},{64,... | collective-permute-start | bytes 1230344 | tf_op jit(solution)/shard_map/ppermute | solution.py:15
  243.0 20.1 %collective-permute-start.2 = (bf16[3,1,800,256]{3,2,1,0:T(8,128)(2,1)S(1)}, bf16[3,1,800,256]{3,2,1,0:T(8,128)(2,1)S(1)}, u32[]{:S(2)}, u32[]{:S(2)}) collective-permute-start(bf16[3,1,800,256]{3,2,1,0:T(8,128)(2,1)S(1)} %pad_maximum_fusion.1), channel_id=1, source_target_pairs={{0,8},{8,0},{16,24},{24,16},{32,40},{40,32},{48,56},{56,48},{64,72... | collective-permute-start | bytes 3686408 | tf_op jit(solution)/shard_map/ppermute | solution.py:125
  256.7 7.4 %collective-permute-start.5 = (bf16[3,1,801,256]{3,2,1,0:T(8,128)(2,1)S(1)}, bf16[3,1,801,256]{3,2,1,0:T(8,128)(2,1)S(1)}, u32[]{:S(2)}, u32[]{:S(2)}) collective-permute-start(bf16[3,1,801,256]{3,2,1,0:T(8,128)(2,1)S(1)} %pad_maximum_fusion), channel_id=1, source_target_pairs={{0,8},{8,0},{16,24},{24,16},{32,40},{40,32},{48,56},{56,48},{64,72... | collective-permute-start | bytes 3691016 | tf_op jit(solution)/shard_map/ppermute | solution.py:125
  274.8 2.7 copy-start.1
  (11 other events, 16.8 us)
Sparse Core Ops, SparseCore 0:
  10.1 114.5 all-gather.2
  134.8 46.8 reduce-scatter.2
  184.4 50.5 reduce-scatter.4

commit v10 on v9

--- a/solution.py
+++ b/solution.py
@@ -108,7 +108,7 @@
         key_part = rms_scale(own_kv[..., :head_dim], key_gain)
         return jnp.concatenate([key_part, own_kv[..., head_dim:]], axis=-1).astype(jnp.bfloat16)
 
-    token_cut = (features.shape[0] // 16) * 8
+    token_cut = (features.shape[0] * 2 // 24) * 8
     packed_halves = [reduced_half(features[:token_cut]), reduced_half(features[token_cut:])]
     span_index = lax.axis_index("seq")
     image_ids = span_index - jnp.arange(IMAGE_LOOKBACK + 1, dtype=jnp.int32)

time: 285 us -> 296 us (1.039)
  waiting for transfers between devices: 170 us -> 181 us
  matrix products: 28.7 us -> 33.1 us
  starting transfers between devices: 20.1 us -> 17 us
    ppermute x4, waiting for transfers between devices: 9.09 us -> 32.2 us  [from_behind(): lax.ppermute(value, axis, [(source, source + steps) for source in range(i...]
    reduce_scatter x2, waiting for transfers between devices: 44.7 us -> 32.8 us  [reduced_half(): lax.psum_scatter(partials, 'fsdp', scatter_dimension=0, tiled=True)]
    dot_general x16, matrix products: 12.8 us -> 18 us  [reduced_half(): jnp.dot(rows, both[:, block * kv_rows:(block + 1) * kv_rows, pair * pair_...]
    ppermute x2, starting transfers between devices: 9.33 us -> 4.44 us  [on_device(): lax.ppermute(jnp.stack([half, two_behind, four_behind]), 'seq', [(source,...]
  transfers between devices with their start and end apart: 9 -> 9, of which waited for: 6 -> 7; matrix products, arithmetic and copies ran while one was open for 17% -> 18% of each run, Pallas kernels for 0% -> 0%
where the time goes in v10:
time: 296 us; the launch traced here: 295 us
  waiting for transfers between devices  181 us (61%)
  matrix products  33.1 us (11%)
  local copies, waits for them, and re-layouts  29.8 us (10%)
  between operations  17.4 us (6%)
  other arithmetic  17.3 us (6%)
  starting transfers between devices  17 us (6%)
    all_gather x1, waiting for transfers between devices, on_device(): lax.all_gather(jnp.concatenate([kv_as_rows, query_weight], axis=0), 'seq'...  115 us
    reduce_scatter x2, waiting for transfers between devices, reduced_half(): lax.psum_scatter(partials, 'fsdp', scatter_dimension=0, tiled=True)  32.8 us
    ppermute x4, waiting for transfers between devices, from_behind(): lax.ppermute(value, axis, [(source, source + steps) for source in range(i...  32.2 us
    dot_general x16, matrix products, reduced_half(): jnp.dot(rows, both[:, block * kv_rows:(block + 1) * kv_rows, pair * pair_...  18 us
    ppermute x4, starting transfers between devices, from_behind(): lax.ppermute(value, axis, [(source, source + steps) for source in range(i...  12.2 us
    reshape x1, local copies, waits for them, and re-layouts, on_device(): query_block = both[:, column_blocks * kv_rows:].reshape(-1, query_width)  11.7 us
    slice x1, local copies, waits for them, and re-layouts, on_device(): query_block = both[:, column_blocks * kv_rows:].reshape(-1, query_width)  7.49 us
    dot_general x2, matrix products, attend_part(): jnp.einsum('kqn,knd->kqd', weights.astype(jnp.bfloat16), key_value_pair[....  6.11 us
  transfers between devices with their start and end apart: 9, of which 7 were waited for; matrix products, arithmetic and copies ran while one was open for 18% of the time, Pallas kernels for 0%

profile of v10, /device:TPU:133, one launch (start us, length us, event | category | flops | bytes accessed | tf_op | source)
XLA Modules:
  0.0 295.4 jit_solution(15976723290219271138)
XLA Ops:
  7.6 1.8 pad_maximum_fusion.6
  9.4 115.3 %all-gather.3.cloned.1.call-done = bf16[12288,512]{1,0:T(8,128)(2,1)} async-done(((bf16[384,512]{1,0:T(8,128)(2,1)}), bf16[12288,512]{1,0:T(8,128)(2,1)}) %all-gather.3.cloned.1.call-update) | async-done | bytes 12582928 | tf_op jit(solution)/shard_map/all_gather | solution.py:82
  124.7 3.0 %fusion.121 = (bf16[32,32,256]{2,1,0:T(8,128)(2,1)S(1)}, bf16[32,32,256]{2,1,0:T(8,128)(2,1)S(1)}, bf16[32,32,256]{2,1,0:T(8,128)(2,1)S(1)}, bf16[32,32,256]{2,1...) fusion(bf16[32,384,512]{2,1,0:T(8,128)(2,1)} %bitcast.226), kind=kLoop, calls=%fused_computation.175 | loop fusion | bytes 8388608 | tf_op jit(solution)/shard_map/slice | solution.py:99
  133.5 3.4 %fusion.21 = bf16[8,1064,256]{2,1,0:T(8,128)(2,1)} fusion(bf16[1024,256]{1,0:T(8,128)(2,1)} %bitcast.251, bf16[1,1601,1024]{2,1,0:T(8,128)(2,1)} %param.9), kind=kOutput, calls=%fused_computation.33 | convolution fusion | flops 558114816 | bytes 3248128 | tf_op jit(solution)/shard_map/dot_general | solution.py:97
  136.9 1.6 fusion.23
  146.2 1.6 fusion.35
  154.6 3.1 %fusion.3 = f32[256]{0:T(256)S(1)} fusion(bf16[256,8192]{1,0:T(8,128)(2,1)} %param.8), kind=kLoop, calls=%fused_computation.8 | loop fusion | flops 6291200 | bytes 4195328 | tf_op jit(solution)/shard_map/reduce_sum | solution.py:19
  157.8 7.5 %slice.128 = bf16[32,256,512]{2,1,0:T(8,128)(2,1)} slice(bf16[32,384,512]{2,1,0:T(8,128)(2,1)} %bitcast.227), slice={[0:32], [128:384], [0:512]} | slice | bytes 16777216 | tf_op jit(solution)/shard_map/slice | solution.py:85
  165.3 11.7 %copy.15 = bf16[8192,512]{0,1:T(8,128)(2,1)} copy(bf16[8192,512]{1,0:T(8,128)(2,1)} %bitcast.225) | data formatting | bytes 16777216 | tf_op jit(solution)/shard_map/reshape | solution.py:85
  179.7 4.9 %collective-permute-start.3 = (bf16[1,537,256]{2,1,0:T(8,128)(2,1)S(1)}, bf16[1,537,256]{2,1,0:T(8,128)(2,1)S(1)}, u32[]{:S(2)}, u32[]{:S(2)}) collective-permute-start(bf16[1,537,256]{2,1,0:T(8,128)(2,1)S(1)} %pad_maximum_fusion.7), channel_id=1, source_target_pairs={{0,16},{8,24},{16,32},{24,40},{32,48},{40,56},{48,64},{56,72},{64,... | collective-permute-start | bytes 824840 | tf_op jit(solution)/shard_map/ppermute | solution.py:15
  184.6 2.3 collective-permute-start.4
  189.0 8.3 %collective-permute-done.4 = bf16[1,537,256]{2,1,0:T(8,128)(2,1)S(1)} collective-permute-done((bf16[1,537,256]{2,1,0:T(8,128)(2,1)S(1)}, bf16[1,537,256]{2,1,0:T(8,128)(2,1)S(1)}, u32[]{:S(2)}, u32[]{:S(2)}) %collective-permute-start.4) | collective-permute-done | bytes 274976 | tf_op jit(solution)/shard_map/ppermute | solution.py:15
  197.4 2.9 collective-permute-start.5
  200.2 5.9 %multiply_reduce_fusion.1 = (f32[256,4]{0,1:T(4,128)S(1)}, f32[256,4,128]{2,0,1:T(8,128)S(1)}) fusion(bf16[4,128,8192]{2,1,0:T(8,128)(2,1)} %bitcast.228, bf16[256,8192]{1,0:T(8,128)(2,1)S(1)} %copy-done.2, f32[8192]{0:T(1024)S(1)} %copy-done.20, f32[256]{0:T(256)S(1)} %add_rsqrt_fusion.3), kind=kOutput, calls=%fused_computation.117 | convolution fusion | flops 2156133376 | bytes 13145088 | tf_op jit(solution)/shard_map/dot_general | solution.py:86
  206.5 32.8 %reduce-scatter.3.cloned.1.call-done = bf16[1,1064,256]{2,1,0:T(8,128)(2,1)} async-done(((bf16[8,1064,256]{2,1,0:T(8,128)(2,1)}), bf16[1,1064,256]{2,1,0:T(8,128)(2,1)}) %reduce-scatter.3.cloned.1.call-update) | async-done | bytes 544784 | tf_op jit(solution)/shard_map/reduce_scatter | solution.py:107
  242.0 2.6 collective-permute-start
  244.5 2.5 collective-permute-start.1
  247.4 11.3 %collective-permute-done = bf16[1,1064,256]{2,1,0:T(8,128)(2,1)S(1)} collective-permute-done((bf16[1,1064,256]{2,1,0:T(8,128)(2,1)S(1)}, bf16[1,1064,256]{2,1,0:T(8,128)(2,1)S(1)}, u32[]{:S(2)}, u32[]{:S(2)}) %collective-permute-start) | collective-permute-done | bytes 544800 | tf_op jit(solution)/shard_map/ppermute | solution.py:15
  258.7 11.6 %collective-permute-done.1 = bf16[1,1064,256]{2,1,0:T(8,128)(2,1)S(1)} collective-permute-done((bf16[1,1064,256]{2,1,0:T(8,128)(2,1)S(1)}, bf16[1,1064,256]{2,1,0:T(8,128)(2,1)S(1)}, u32[]{:S(2)}, u32[]{:S(2)}) %collective-permute-start.1) | collective-permute-done | bytes 544800 | tf_op jit(solution)/shard_map/ppermute | solution.py:15
  270.5 1.6 collective-permute-start.2
  276.0 2.0 fusion
  278.0 3.8 %fusion.1 = f32[1024]{0:T(1024)S(1)} fusion(f32[1024,3202]{0,1:T(8,128)S(1)} %get-tuple-element.29, f32[1024]{0:T(1024)S(1)} %compare_select_fusion, pred[3202]{0:T(1024)(128)(4,1)S(1)} %concatenate.152), kind=kLoop, calls=%fused_computation.6 | loop fusion | flops 13114368 | bytes 13126786 | tf_op jit(solution)/shard_map/reduce_sum | solution.py:30
  281.8 4.4 %fusion.50 = f32[1024,128]{1,0:T(8,128)S(1)} fusion(f32[1024,3202]{0,1:T(8,128)S(1)} %get-tuple-element.29, f32[1024]{0:T(1024)S(1)} %compare_select_fusion, pred[3202]{0:T(1024)(128)(4,1)S(1)} %concatenate.152, bf16[1,1601,256]{2,1,0:T(8,128)(2,1)S(1)} %get-tuple-element.20, bf16[1,1601,256]{2,1,0:T(8,128)(2,1)S(1)} %get-tuple-element.21, ...), kind=kOutput, calls=%fused_computation.61 | convolution fusion | flops 854270976 | bytes 15290498 | tf_op jit(solution)/shard_map/kqn,knd->kqd/dot_general | solution.py:31
  286.2 1.7 fusion.80
  (114 shorter events, 30.5 us)
Async XLA Ops:
  6.5 141.3 %copy-start = (s32[1,32]{1,0:T(1,128)S(1)}, s32[1,32]{1,0:T(1,128)}, u32[]{:S(2)}) copy-start(s32[1,32]{1,0:T(1,128)} %param.15) | copy-start | bytes 388
  6.5 118.2 %all-gather.3.cloned.1.call-start = ((), (), s32[]{:S(2)}) async-start(), calls=%async_computation.4 | async-start | bytes 12976128 | tf_op jit(solution)/shard_map/all_gather | solution.py:82
  9.3 167.6 %reduce-scatter.5.cloned.1.call-start = ((), (), s32[]{:S(2)}) async-start(), calls=%async_computation.3 | async-start | bytes 2506752 | tf_op jit(solution)/shard_map/reduce_scatter | solution.py:107
  124.7 3.3 %copy-start.18 = (bf16[1,1601,1024]{2,1,0:T(8,128)(2,1)S(1)}, bf16[1,1601,1024]{2,1,0:T(8,128)(2,1)}, u32[]{:S(2)}) copy-start(bf16[1,1601,1024]{2,1,0:T(8,128)(2,1)} %param.9) | copy-start | bytes 9836548
  127.7 1.6 copy-start.11
  127.8 1.6 copy-start.13
  127.8 1.6 copy-start.15
  127.8 2.1 copy-start.7
  127.8 2.6 copy-start.5
  133.2 3.7 %copy-start.14 = (bf16[32,32,256]{2,1,0:T(8,128)(2,1)S(1)}, bf16[32,32,256]{2,1,0:T(8,128)(2,1)}, u32[]{:S(2)}) copy-start(bf16[32,32,256]{2,1,0:T(8,128)(2,1)} %copy-done.13) | copy-start | bytes 1572868
  133.2 106.0 %reduce-scatter.3.cloned.1.call-start = ((), (), s32[]{:S(2)}) async-start(), calls=%async_computation.2 | async-start | bytes 4902912 | tf_op jit(solution)/shard_map/reduce_scatter | solution.py:107
  133.5 3.5 %copy-start.19 = (bf16[1,1601,1024]{2,1,0:T(8,128)(2,1)S(1)}, bf16[1,1601,1024]{2,1,0:T(8,128)(2,1)}, u32[]{:S(2)}) copy-start(bf16[1,1601,1024]{2,1,0:T(8,128)(2,1)} %param.9) | copy-start | bytes 9836548
  165.3 14.2 %copy-start.16 = (f32[128]{0:T(128)S(1)}, f32[128]{0:T(128)}, u32[]{:S(2)}) copy-start(f32[128]{0:T(128)} %param.14) | copy-start | bytes 1540
  177.0 23.3 %copy-start.20 = (f32[8192]{0:T(1024)S(1)}, f32[8192]{0:T(1024)}, u32[]{:S(2)}) copy-start(f32[8192]{0:T(1024)} %param.10) | copy-start | bytes 98308
  177.0 23.3 %copy-start.2 = (bf16[256,8192]{1,0:T(8,128)(2,1)S(1)}, bf16[256,8192]{1,0:T(8,128)(2,1)}, u32[]{:S(2)}) copy-start(bf16[256,8192]{1,0:T(8,128)(2,1)} %param.8) | copy-start | bytes 12582916
  179.7 9.3 %collective-permute-start.3 = (bf16[1,537,256]{2,1,0:T(8,128)(2,1)S(1)}, bf16[1,537,256]{2,1,0:T(8,128)(2,1)S(1)}, u32[]{:S(2)}, u32[]{:S(2)}) collective-permute-start(bf16[1,537,256]{2,1,0:T(8,128)(2,1)S(1)} %pad_maximum_fusion.7), channel_id=1, source_target_pairs={{0,16},{8,24},{16,32},{24,40},{32,48},{40,56},{48,64},{56,72},{64,... | collective-permute-start | bytes 824840 | tf_op jit(solution)/shard_map/ppermute | solution.py:15
  184.6 12.7 %collective-permute-start.4 = (bf16[1,537,256]{2,1,0:T(8,128)(2,1)S(1)}, bf16[1,537,256]{2,1,0:T(8,128)(2,1)S(1)}, u32[]{:S(2)}, u32[]{:S(2)}) collective-permute-start(bf16[1,537,256]{2,1,0:T(8,128)(2,1)S(1)} %pad_maximum_fusion.7), channel_id=1, source_target_pairs={{0,32},{8,40},{16,48},{24,56},{32,64},{40,72},{48,80},{56,88},{64,... | collective-permute-start | bytes 824840 | tf_op jit(solution)/shard_map/ppermute | solution.py:15
  197.4 9.0 %collective-permute-start.5 = (bf16[3,1,537,256]{3,2,1,0:T(8,128)(2,1)S(1)}, bf16[3,1,537,256]{3,2,1,0:T(8,128)(2,1)S(1)}, u32[]{:S(2)}, u32[]{:S(2)}) collective-permute-start(bf16[3,1,537,256]{3,2,1,0:T(8,128)(2,1)S(1)} %pad_maximum_fusion.1), channel_id=1, source_target_pairs={{0,8},{8,0},{16,24},{24,16},{32,40},{40,32},{48,56},{56,48},{64,72... | collective-permute-start | bytes 2474504 | tf_op jit(solution)/shard_map/ppermute | solution.py:125
  200.2 5.9 %copy-start.17 = (f32[128]{0:T(128)S(1)}, f32[128]{0:T(128)}, u32[]{:S(2)}) copy-start(f32[128]{0:T(128)} %param.13) | copy-start | bytes 1540
  239.2 7.8 %copy-start.4 = (bf16[1,1064,256]{2,1,0:T(8,128)(2,1)S(1)}, bf16[1,1064,256]{2,1,0:T(8,128)(2,1)}, u32[]{:S(2)}) copy-start(bf16[1,1064,256]{2,1,0:T(8,128)(2,1)} %reduce-scatter.3.cloned.1.call-done) | copy-start | bytes 1634308
  242.0 16.7 %collective-permute-start = (bf16[1,1064,256]{2,1,0:T(8,128)(2,1)S(1)}, bf16[1,1064,256]{2,1,0:T(8,128)(2,1)S(1)}, u32[]{:S(2)}, u32[]{:S(2)}) collective-permute-start(bf16[1,1064,256]{2,1,0:T(8,128)(2,1)S(1)} %pad_maximum_fusion.5), channel_id=1, source_target_pairs={{0,16},{8,24},{16,32},{24,40},{32,48},{40,56},{48,64},{56,72},{64,... | collective-permute-start | bytes 1634312 | tf_op jit(solution)/shard_map/ppermute | solution.py:15
  244.5 25.8 %collective-permute-start.1 = (bf16[1,1064,256]{2,1,0:T(8,128)(2,1)S(1)}, bf16[1,1064,256]{2,1,0:T(8,128)(2,1)S(1)}, u32[]{:S(2)}, u32[]{:S(2)}) collective-permute-start(bf16[1,1064,256]{2,1,0:T(8,128)(2,1)S(1)} %pad_maximum_fusion.5), channel_id=1, source_target_pairs={{0,32},{8,40},{16,48},{24,56},{32,64},{40,72},{48,80},{56,88},{64,... | collective-permute-start | bytes 1634312 | tf_op jit(solution)/shard_map/ppermute | solution.py:15
  270.5 4.7 %collective-permute-start.2 = (bf16[3,1,1064,256]{3,2,1,0:T(8,128)(2,1)S(1)}, bf16[3,1,1064,256]{3,2,1,0:T(8,128)(2,1)S(1)}, u32[]{:S(2)}, u32[]{:S(2)}) collective-permute-start(bf16[3,1,1064,256]{3,2,1,0:T(8,128)(2,1)S(1)} %pad_maximum_fusion), channel_id=1, source_target_pairs={{0,8},{8,0},{16,24},{24,16},{32,40},{40,32},{48,56},{56,48},{64,72... | collective-permute-start | bytes 4902920 | tf_op jit(solution)/shard_map/ppermute | solution.py:125
  286.2 2.7 copy-start.1
  (6 other events, 9.3 us)
Sparse Core Ops, SparseCore 0:
  10.1 114.5 all-gather.2
  133.3 41.5 reduce-scatter.4
  177.7 61.4 reduce-scatter.2

commit v11 on v9

--- a/solution.py
+++ b/solution.py
@@ -104,7 +104,9 @@
                 for pair in range(pairs_per_block)
             ]
         )
-        own_kv = lax.psum_scatter(partials, "fsdp", scatter_dimension=0, tiled=True).astype(jnp.float32)
+        own_kv = jnp.sum(
+            lax.all_to_all(partials, "fsdp", 0, 0, tiled=True).astype(jnp.float32), axis=0, keepdims=True
+        )
         key_part = rms_scale(own_kv[..., :head_dim], key_gain)
         return jnp.concatenate([key_part, own_kv[..., head_dim:]], axis=-1).astype(jnp.bfloat16)
 

time: 285 us -> 294 us (1.032)
  the two profiles are of different devices: /device:TPU:133 before, /device:TPU:85 now
where the time goes in v11:
time: 294 us; the launch traced here: 293 us
  waiting for transfers between devices  158 us (54%)
  matrix products  41.4 us (14%)
  local copies, waits for them, and re-layouts  29.7 us (10%)
  starting transfers between devices  27 us (9%)
  other arithmetic  18.8 us (6%)
  between operations  17.9 us (6%)
    all_gather x1, waiting for transfers between devices, on_device(): lax.all_gather(jnp.concatenate([kv_as_rows, query_weight], axis=0), 'seq'...  111 us
    all_to_all x2, waiting for transfers between devices, reduced_half(): lax.all_to_all(partials, 'fsdp', 0, 0, tiled=True).astype(jnp.float32)  29 us
    dot_general x16, matrix products, reduced_half(): jnp.dot(rows, both[:, block * kv_rows:(block + 1) * kv_rows, pair * pair_...  25.5 us
    ppermute x4, waiting for transfers between devices, from_behind(): lax.ppermute(value, axis, [(source, source + steps) for source in range(i...  18.7 us
    ppermute x4, starting transfers between devices, from_behind(): lax.ppermute(value, axis, [(source, source + steps) for source in range(i...  11.4 us
    reshape x1, local copies, waits for them, and re-layouts, on_device(): query_block = both[:, column_blocks * kv_rows:].reshape(-1, query_width)  11.4 us
    all_to_all x2, starting transfers between devices, reduced_half(): lax.all_to_all(partials, 'fsdp', 0, 0, tiled=True).astype(jnp.float32)  11.4 us
    slice x1, local copies, waits for them, and re-layouts, on_device(): query_block = both[:, column_blocks * kv_rows:].reshape(-1, query_width)  7.46 us
  transfers between devices with their start and end apart: 9, of which 5 were waited for; matrix products, arithmetic and copies ran while one was open for 20% of the time, Pallas kernels for 0%

profile of v11, /device:TPU:85, one launch (start us, length us, event | category | flops | bytes accessed | tf_op | source)
XLA Modules:
  0.0 293.2 jit_solution(13067110564840480457)
XLA Ops:
  16.5 110.8 %all-gather.3.cloned.1.call-done = bf16[12288,512]{1,0:T(8,128)(2,1)} async-done(((bf16[384,512]{1,0:T(8,128)(2,1)}), bf16[12288,512]{1,0:T(8,128)(2,1)}) %all-gather.3.cloned.1.call-update) | async-done | bytes 12582928 | tf_op jit(solution)/shard_map/all_gather | solution.py:82
  127.2 2.8 fusion.249
  130.5 1.8 fusion.160
  141.8 5.8 %all-to-all-start = ((bf16[8,800,256]{2,1,0:T(8,128)(2,1)}), bf16[8,800,256]{2,1,0:T(8,128)(2,1)S(1)}, u32[]{:S(2)}, u32[]{:S(2)}) async-start(bf16[8,800,256]{2,1,0:T(8,128)(2,1)} %fusion.202), calls=%async_computation | async-start | bytes 6553600 | tf_op jit(solution)/shard_map/all_to_all | solution.py:108
  147.5 3.1 %fusion.3 = f32[256]{0:T(256)S(1)} fusion(bf16[256,8192]{1,0:T(8,128)(2,1)} %param.8), kind=kLoop, calls=%fused_computation.8 | loop fusion | flops 6291200 | bytes 4195328 | tf_op jit(solution)/shard_map/reduce_sum | solution.py:19
  150.7 7.5 %slice.128 = bf16[32,256,512]{2,1,0:T(8,128)(2,1)} slice(bf16[32,384,512]{2,1,0:T(8,128)(2,1)} %bitcast.325), slice={[0:32], [128:384], [0:512]} | slice | bytes 16777216 | tf_op jit(solution)/shard_map/slice | solution.py:85
  158.1 11.4 %copy.24 = bf16[8192,512]{0,1:T(8,128)(2,1)} copy(bf16[8192,512]{1,0:T(8,128)(2,1)} %bitcast.323) | data formatting | bytes 16777216 | tf_op jit(solution)/shard_map/reshape | solution.py:85
  169.5 3.1 %fusion.154 = bf16[8,801,256]{2,1,0:T(8,128)(2,1)} fusion(bf16[1024,256]{1,0:T(8,128)(2,1)} %bitcast.357, bf16[1,1601,1024]{2,1,0:T(8,128)(2,1)} %param.9), kind=kOutput, calls=%fused_computation.96 | convolution fusion | flops 420159744 | bytes 2592768 | tf_op jit(solution)/shard_map/dot_general | solution.py:97
  172.7 2.9 fusion.148
  184.4 1.8 copy-done.2
  186.2 5.6 %all-to-all-start.1 = ((bf16[8,801,256]{2,1,0:T(8,128)(2,1)}), bf16[8,801,256]{2,1,0:T(8,128)(2,1)S(1)}, u32[]{:S(2)}, u32[]{:S(2)}) async-start(bf16[8,801,256]{2,1,0:T(8,128)(2,1)} %fusion.112), calls=%async_computation.1 | async-start | bytes 6619136 | tf_op jit(solution)/shard_map/all_to_all | solution.py:108
  191.8 6.7 %multiply_reduce_fusion = (f32[256,4]{0,1:T(4,128)S(1)}, f32[256,4,128]{2,0,1:T(8,128)S(1)}) fusion(bf16[4,128,8192]{2,1,0:T(8,128)(2,1)} %bitcast.326, bf16[256,8192]{1,0:T(8,128)(2,1)} %param.8, f32[8192]{0:T(1024)S(1)} %copy-done.28, f32[256]{0:T(256)S(1)} %add_rsqrt_fusion.3), kind=kOutput, calls=%fused_computation.127 | convolution fusion | flops 2156133376 | bytes 13145088 | tf_op jit(solution)/shard_map/dot_general | solution.py:86
  201.2 3.9 %collective-permute-start = (bf16[1,800,256]{2,1,0:T(8,128)(2,1)}, bf16[1,800,256]{2,1,0:T(8,128)(2,1)}, u32[]{:S(2)}, u32[]{:S(2)}) collective-permute-start(bf16[1,800,256]{2,1,0:T(8,128)(2,1)} %pad_maximum_fusion.6), channel_id=1, source_target_pairs={{0,16},{8,24},{16,32},{24,40},{32,48},{40,56},{48,64},{56,72},{64,... | collective-permute-start | bytes 1228808 | tf_op jit(solution)/shard_map/ppermute | solution.py:15
  205.1 2.6 collective-permute-start.1
  209.3 28.3 %all-to-all-done.1 = bf16[8,801,256]{2,1,0:T(8,128)(2,1)S(1)} async-done(((bf16[8,801,256]{2,1,0:T(8,128)(2,1)}), bf16[8,801,256]{2,1,0:T(8,128)(2,1)S(1)}, u32[]{:S(2)}, u32[]{:S(2)}) %all-to-all-start.1) | async-done | bytes 3280928 | tf_op jit(solution)/shard_map/all_to_all | solution.py:108
  238.8 1.9 collective-permute-start.3
  240.7 3.0 %collective-permute-start.4 = (bf16[1,801,256]{2,1,0:T(8,128)(2,1)S(1)}, bf16[1,801,256]{2,1,0:T(8,128)(2,1)S(1)}, u32[]{:S(2)}, u32[]{:S(2)}) collective-permute-start(bf16[1,801,256]{2,1,0:T(8,128)(2,1)S(1)} %pad_maximum_fusion.5), channel_id=1, source_target_pairs={{0,32},{8,40},{16,48},{24,56},{32,64},{40,72},{48,80},{56,88},{64,... | collective-permute-start | bytes 1230344 | tf_op jit(solution)/shard_map/ppermute | solution.py:15
  246.3 1.9 collective-permute-start.2
  248.2 3.5 %collective-permute-done.3 = bf16[1,801,256]{2,1,0:T(8,128)(2,1)S(1)} collective-permute-done((bf16[1,801,256]{2,1,0:T(8,128)(2,1)S(1)}, bf16[1,801,256]{2,1,0:T(8,128)(2,1)S(1)}, u32[]{:S(2)}, u32[]{:S(2)}) %collective-permute-start.3) | collective-permute-done | bytes 410144 | tf_op jit(solution)/shard_map/ppermute | solution.py:15
  251.7 15.2 %collective-permute-done.4 = bf16[1,801,256]{2,1,0:T(8,128)(2,1)S(1)} collective-permute-done((bf16[1,801,256]{2,1,0:T(8,128)(2,1)S(1)}, bf16[1,801,256]{2,1,0:T(8,128)(2,1)S(1)}, u32[]{:S(2)}, u32[]{:S(2)}) %collective-permute-start.4) | collective-permute-done | bytes 410144 | tf_op jit(solution)/shard_map/ppermute | solution.py:15
  267.0 2.3 collective-permute-start.5
  273.7 2.0 fusion
  275.7 3.5 %fusion.1 = f32[1024]{0:T(1024)S(1)} fusion(f32[1024,3202]{0,1:T(8,128)S(1)} %get-tuple-element.29, f32[1024]{0:T(1024)S(1)} %compare_select_fusion, pred[3202]{0:T(1024)(128)(4,1)S(1)} %concatenate.152), kind=kLoop, calls=%fused_computation.6 | loop fusion | flops 13114368 | bytes 13126786 | tf_op jit(solution)/shard_map/reduce_sum | solution.py:30
  279.3 4.4 %fusion.106 = f32[1024,128]{1,0:T(8,128)S(1)} fusion(f32[1024,3202]{0,1:T(8,128)S(1)} %get-tuple-element.29, f32[1024]{0:T(1024)S(1)} %compare_select_fusion, pred[3202]{0:T(1024)(128)(4,1)S(1)} %concatenate.152, bf16[1,1601,256]{2,1,0:T(8,128)(2,1)S(1)} %get-tuple-element.20, bf16[1,1601,256]{2,1,0:T(8,128)(2,1)S(1)} %get-tuple-element.21, ...), kind=kOutput, calls=%fused_computation.80 | convolution fusion | flops 854270976 | bytes 15290498 | tf_op jit(solution)/shard_map/kqn,knd->kqd/dot_general | solution.py:31
  (128 shorter events, 39.5 us)
Async XLA Ops:
  6.5 120.7 %all-gather.3.cloned.1.call-start = ((), (), s32[]{:S(2)}) async-start(), calls=%async_computation.2 | async-start | bytes 12976128 | tf_op jit(solution)/shard_map/all_gather | solution.py:82
  130.1 3.5 %copy-start.21 = (bf16[32,32,256]{2,1,0:T(8,128)(2,1)}, bf16[32,32,256]{2,1,0:T(8,128)(2,1)S(1)}, u32[]{:S(2)}) copy-start(bf16[32,32,256]{2,1,0:T(8,128)(2,1)S(1)} %get-tuple-element.18) | copy-start | bytes 1572868
  130.1 3.5 %copy-start.23 = (bf16[32,32,256]{2,1,0:T(8,128)(2,1)}, bf16[32,32,256]{2,1,0:T(8,128)(2,1)S(1)}, u32[]{:S(2)}) copy-start(bf16[32,32,256]{2,1,0:T(8,128)(2,1)S(1)} %get-tuple-element.19) | copy-start | bytes 1572868
  130.1 4.9 %copy-start.17 = (bf16[32,32,256]{2,1,0:T(8,128)(2,1)}, bf16[32,32,256]{2,1,0:T(8,128)(2,1)S(1)}, u32[]{:S(2)}) copy-start(bf16[32,32,256]{2,1,0:T(8,128)(2,1)S(1)} %get-tuple-element.16) | copy-start | bytes 1572868
  130.1 6.2 %copy-start.15 = (bf16[32,32,256]{2,1,0:T(8,128)(2,1)}, bf16[32,32,256]{2,1,0:T(8,128)(2,1)S(1)}, u32[]{:S(2)}) copy-start(bf16[32,32,256]{2,1,0:T(8,128)(2,1)S(1)} %get-tuple-element.15) | copy-start | bytes 1572868
  130.1 7.6 %copy-start.13 = (bf16[32,32,256]{2,1,0:T(8,128)(2,1)}, bf16[32,32,256]{2,1,0:T(8,128)(2,1)S(1)}, u32[]{:S(2)}) copy-start(bf16[32,32,256]{2,1,0:T(8,128)(2,1)S(1)} %get-tuple-element.14) | copy-start | bytes 1572868
  130.1 8.9 %copy-start.11 = (bf16[32,32,256]{2,1,0:T(8,128)(2,1)}, bf16[32,32,256]{2,1,0:T(8,128)(2,1)S(1)}, u32[]{:S(2)}) copy-start(bf16[32,32,256]{2,1,0:T(8,128)(2,1)S(1)} %get-tuple-element.13) | copy-start | bytes 1572868
  130.1 10.3 %copy-start.9 = (bf16[32,32,256]{2,1,0:T(8,128)(2,1)}, bf16[32,32,256]{2,1,0:T(8,128)(2,1)S(1)}, u32[]{:S(2)}) copy-start(bf16[32,32,256]{2,1,0:T(8,128)(2,1)S(1)} %get-tuple-element.12) | copy-start | bytes 1572868
  141.8 42.6 %all-to-all-start = ((bf16[8,800,256]{2,1,0:T(8,128)(2,1)}), bf16[8,800,256]{2,1,0:T(8,128)(2,1)S(1)}, u32[]{:S(2)}, u32[]{:S(2)}) async-start(bf16[8,800,256]{2,1,0:T(8,128)(2,1)} %fusion.202), calls=%async_computation | async-start | bytes 6553600 | tf_op jit(solution)/shard_map/all_to_all | solution.py:108
  169.5 6.0 %copy-start.20 = (bf16[32,32,256]{2,1,0:T(8,128)(2,1)S(1)}, bf16[32,32,256]{2,1,0:T(8,128)(2,1)}, u32[]{:S(2)}) copy-start(bf16[32,32,256]{2,1,0:T(8,128)(2,1)} %copy-done.19) | copy-start | bytes 1572868
  169.5 6.0 %copy-start.27 = (bf16[1,1601,1024]{2,1,0:T(8,128)(2,1)S(1)}, bf16[1,1601,1024]{2,1,0:T(8,128)(2,1)}, u32[]{:S(2)}) copy-start(bf16[1,1601,1024]{2,1,0:T(8,128)(2,1)} %param.9) | copy-start | bytes 9836548
  172.7 4.3 %copy-start.18 = (bf16[32,32,256]{2,1,0:T(8,128)(2,1)S(1)}, bf16[32,32,256]{2,1,0:T(8,128)(2,1)}, u32[]{:S(2)}) copy-start(bf16[32,32,256]{2,1,0:T(8,128)(2,1)} %copy-done.17) | copy-start | bytes 1572868
  183.8 8.0 %copy-start.28 = (f32[8192]{0:T(1024)S(1)}, f32[8192]{0:T(1024)}, u32[]{:S(2)}) copy-start(f32[8192]{0:T(1024)} %param.10) | copy-start | bytes 98308
  186.2 51.5 %all-to-all-start.1 = ((bf16[8,801,256]{2,1,0:T(8,128)(2,1)}), bf16[8,801,256]{2,1,0:T(8,128)(2,1)S(1)}, u32[]{:S(2)}, u32[]{:S(2)}) async-start(bf16[8,801,256]{2,1,0:T(8,128)(2,1)} %fusion.112), calls=%async_computation.1 | async-start | bytes 6619136 | tf_op jit(solution)/shard_map/all_to_all | solution.py:108
  191.8 6.8 %copy-start.25 = (f32[128]{0:T(128)S(1)}, f32[128]{0:T(128)}, u32[]{:S(2)}) copy-start(f32[128]{0:T(128)} %param.13) | copy-start | bytes 1540
  191.8 7.7 %copy-start.3 = (bf16[8,800,256]{2,1,0:T(8,128)(2,1)S(1)}, bf16[8,800,256]{2,1,0:T(8,128)(2,1)}, u32[]{:S(2)}) copy-start(bf16[8,800,256]{2,1,0:T(8,128)(2,1)} %copy-done.2) | copy-start | bytes 9830404
  200.4 8.1 %copy-start.5 = (bf16[1,800,128]{2,1,0:T(8,128)(2,1)}, bf16[1,800,128]{2,1,0:T(8,128)(2,1)S(1)}, u32[]{:S(2)}) copy-start(bf16[1,800,128]{2,1,0:T(8,128)(2,1)S(1)} %multiply_convert_fusion.2) | copy-start | bytes 614404
  201.2 43.8 %collective-permute-start = (bf16[1,800,256]{2,1,0:T(8,128)(2,1)}, bf16[1,800,256]{2,1,0:T(8,128)(2,1)}, u32[]{:S(2)}, u32[]{:S(2)}) collective-permute-start(bf16[1,800,256]{2,1,0:T(8,128)(2,1)} %pad_maximum_fusion.6), channel_id=1, source_target_pairs={{0,16},{8,24},{16,32},{24,40},{32,48},{40,56},{48,64},{56,72},{64,... | collective-permute-start | bytes 1228808 | tf_op jit(solution)/shard_map/ppermute | solution.py:15
  205.1 39.9 %collective-permute-start.1 = (bf16[1,800,256]{2,1,0:T(8,128)(2,1)}, bf16[1,800,256]{2,1,0:T(8,128)(2,1)}, u32[]{:S(2)}, u32[]{:S(2)}) collective-permute-start(bf16[1,800,256]{2,1,0:T(8,128)(2,1)} %pad_maximum_fusion.6), channel_id=1, source_target_pairs={{0,32},{8,40},{16,48},{24,56},{32,64},{40,72},{48,80},{56,88},{64,... | collective-permute-start | bytes 1228808 | tf_op jit(solution)/shard_map/ppermute | solution.py:15
  237.7 6.0 %copy-start.4 = (bf16[256,4,128]{2,0,1:T(8,128)(2,1)S(1)}, bf16[256,4,128]{2,0,1:T(8,128)(2,1)}, u32[]{:S(2)}) copy-start(bf16[256,4,128]{2,0,1:T(8,128)(2,1)} %multiply_convert_fusion) | copy-start | bytes 786436
  238.8 12.9 %collective-permute-start.3 = (bf16[1,801,256]{2,1,0:T(8,128)(2,1)S(1)}, bf16[1,801,256]{2,1,0:T(8,128)(2,1)S(1)}, u32[]{:S(2)}, u32[]{:S(2)}) collective-permute-start(bf16[1,801,256]{2,1,0:T(8,128)(2,1)S(1)} %pad_maximum_fusion.5), channel_id=1, source_target_pairs={{0,16},{8,24},{16,32},{24,40},{32,48},{40,56},{48,64},{56,72},{64,... | collective-permute-start | bytes 1230344 | tf_op jit(solution)/shard_map/ppermute | solution.py:15
  240.7 26.2 %collective-permute-start.4 = (bf16[1,801,256]{2,1,0:T(8,128)(2,1)S(1)}, bf16[1,801,256]{2,1,0:T(8,128)(2,1)S(1)}, u32[]{:S(2)}, u32[]{:S(2)}) collective-permute-start(bf16[1,801,256]{2,1,0:T(8,128)(2,1)S(1)} %pad_maximum_fusion.5), channel_id=1, source_target_pairs={{0,32},{8,40},{16,48},{24,56},{32,64},{40,72},{48,80},{56,88},{64,... | collective-permute-start | bytes 1230344 | tf_op jit(solution)/shard_map/ppermute | solution.py:15
  246.3 26.5 %collective-permute-start.2 = (bf16[3,1,800,256]{3,2,1,0:T(8,128)(2,1)S(1)}, bf16[3,1,800,256]{3,2,1,0:T(8,128)(2,1)S(1)}, u32[]{:S(2)}, u32[]{:S(2)}) collective-permute-start(bf16[3,1,800,256]{3,2,1,0:T(8,128)(2,1)S(1)} %pad_maximum_fusion.1), channel_id=1, source_target_pairs={{0,8},{8,0},{16,24},{24,16},{32,40},{40,32},{48,56},{56,48},{64,72... | collective-permute-start | bytes 3686408 | tf_op jit(solution)/shard_map/ppermute | solution.py:127
  267.0 5.9 %collective-permute-start.5 = (bf16[3,1,801,256]{3,2,1,0:T(8,128)(2,1)S(1)}, bf16[3,1,801,256]{3,2,1,0:T(8,128)(2,1)S(1)}, u32[]{:S(2)}, u32[]{:S(2)}) collective-permute-start(bf16[3,1,801,256]{3,2,1,0:T(8,128)(2,1)S(1)} %pad_maximum_fusion), channel_id=1, source_target_pairs={{0,8},{8,0},{16,24},{24,16},{32,40},{40,32},{48,56},{56,48},{64,72... | collective-permute-start | bytes 3691016 | tf_op jit(solution)/shard_map/ppermute | solution.py:127
  (14 other events, 33.5 us)
Sparse Core Ops, SparseCore 0:
  10.1 117.0 all-gather.2

commit v12 on v10

--- a/solution.py
+++ b/solution.py
@@ -108,8 +108,12 @@
         key_part = rms_scale(own_kv[..., :head_dim], key_gain)
         return jnp.concatenate([key_part, own_kv[..., head_dim:]], axis=-1).astype(jnp.bfloat16)
 
-    token_cut = (features.shape[0] * 2 // 24) * 8
-    packed_halves = [reduced_half(features[:token_cut]), reduced_half(features[token_cut:])]
+    token_cut = (features.shape[0] // 24) * 8
+    packed_halves = [
+        reduced_half(features[:token_cut]),
+        reduced_half(features[token_cut : 2 * token_cut]),
+        reduced_half(features[2 * token_cut :]),
+    ]
     span_index = lax.axis_index("seq")
     image_ids = span_index - jnp.arange(IMAGE_LOOKBACK + 1, dtype=jnp.int32)
     admitted = (image_ids >= 0) & (jnp.take(admission[0], jnp.maximum(image_ids, 0)) == 1)

time: 296 us -> 320 us (1.081)
  waiting for transfers between devices: 181 us -> 190 us
  starting transfers between devices: 17 us -> 25.7 us
    reduce_scatter x2 -> x3, waiting for transfers between devices: 32.8 us -> 70.1 us  [reduced_half(): lax.psum_scatter(partials, 'fsdp', scatter_dimension=0, tiled=True)]
    ppermute x4 -> x6, waiting for transfers between devices: 32.2 us -> 3.21 us  [from_behind(): lax.ppermute(value, axis, [(source, source + steps) for source in range(i...]
    ppermute x2 -> x3, starting transfers between devices: 4.44 us -> 10.2 us  [on_device(): lax.ppermute(jnp.stack([half, two_behind, four_behind]), 'seq', [(source,...]
    unnamed x45 -> x67, local copies, waits for them, and re-layouts: 2.48 us -> 5.74 us
    ppermute x4 -> x6, starting transfers between devices: 12.2 us -> 15.2 us  [from_behind(): lax.ppermute(value, axis, [(source, source + steps) for source in range(i...]
    dot_general x16 -> x24, matrix products: 18 us -> 16.8 us  [reduced_half(): jnp.dot(rows, both[:, block * kv_rows:(block + 1) * kv_rows, pair * pair_...]
  transfers between devices with their start and end apart: 9 -> 13, of which waited for: 7 -> 5; matrix products, arithmetic and copies ran while one was open for 18% -> 17% of each run, Pallas kernels for 0% -> 0%
where the time goes in v12:
time: 320 us; the launch traced here: 316 us
  waiting for transfers between devices  190 us (59%)
  matrix products  32.6 us (10%)
  local copies, waits for them, and re-layouts  31.8 us (10%)
  starting transfers between devices  25.7 us (8%)
  between operations  18.1 us (6%)
  other arithmetic  18 us (6%)
    all_gather x1, waiting for transfers between devices, on_device(): lax.all_gather(jnp.concatenate([kv_as_rows, query_weight], axis=0), 'seq'...  115 us
    reduce_scatter x3, waiting for transfers between devices, reduced_half(): lax.psum_scatter(partials, 'fsdp', scatter_dimension=0, tiled=True)  70.1 us
    dot_general x24, matrix products, reduced_half(): jnp.dot(rows, both[:, block * kv_rows:(block + 1) * kv_rows, pair * pair_...  16.8 us
    ppermute x6, starting transfers between devices, from_behind(): lax.ppermute(value, axis, [(source, source + steps) for source in range(i...  15.2 us
    reshape x1, local copies, waits for them, and re-layouts, on_device(): query_block = both[:, column_blocks * kv_rows:].reshape(-1, query_width)  11.5 us
    ppermute x3, starting transfers between devices, on_device(): lax.ppermute(jnp.stack([half, two_behind, four_behind]), 'seq', [(source,...  10.2 us
    slice x1, local copies, waits for them, and re-layouts, on_device(): query_block = both[:, column_blocks * kv_rows:].reshape(-1, query_width)  7.57 us
    dot_general x1, matrix products, on_device(): queries = jnp.dot(normed, query_block, preferred_element_type=jnp.float32)  6.64 us
  transfers between devices with their start and end apart: 13, of which 5 were waited for; matrix products, arithmetic and copies ran while one was open for 17% of the time, Pallas kernels for 0%

profile of v12, /device:TPU:133, one launch (start us, length us, event | category | flops | bytes accessed | tf_op | source)
XLA Modules:
  0.0 316.4 jit_solution(824790858513176411)
XLA Ops:
  9.4 115.1 %all-gather.3.cloned.1.call-done = bf16[12288,512]{1,0:T(8,128)(2,1)} async-done(((bf16[384,512]{1,0:T(8,128)(2,1)}), bf16[12288,512]{1,0:T(8,128)(2,1)}) %all-gather.3.cloned.1.call-update) | async-done | bytes 12582928 | tf_op jit(solution)/shard_map/all_gather | solution.py:82
  124.4 3.0 fusion.155
  132.8 2.0 fusion.62
  134.8 1.9 fusion.64
  142.1 2.0 fusion.30
  144.2 1.9 fusion.32
  157.1 3.1 fusion.3
  160.2 7.6 %slice.165 = bf16[32,256,512]{2,1,0:T(8,128)(2,1)} slice(bf16[32,384,512]{2,1,0:T(8,128)(2,1)} %bitcast.308), slice={[0:32], [128:384], [0:512]} | slice | bytes 16777216 | tf_op jit(solution)/shard_map/slice | solution.py:85
  167.8 11.5 %copy.15 = bf16[8192,512]{0,1:T(8,128)(2,1)} copy(bf16[8192,512]{1,0:T(8,128)(2,1)} %bitcast.306) | data formatting | bytes 16777216 | tf_op jit(solution)/shard_map/reshape | solution.py:85
  179.3 6.6 %multiply_reduce_fusion = (f32[256,4]{0,1:T(4,128)S(1)}, f32[256,4,128]{2,0,1:T(8,128)S(1)}) fusion(bf16[4,128,8192]{2,1,0:T(8,128)(2,1)} %bitcast.309, bf16[256,8192]{1,0:T(8,128)(2,1)} %param.8, f32[8192]{0:T(1024)S(1)} %copy-done.30, f32[256]{0:T(256)S(1)} %add_rsqrt_fusion.4), kind=kOutput, calls=%fused_computation.142 | convolution fusion | flops 2156133376 | bytes 13145088 | tf_op jit(solution)/shard_map/dot_general | solution.py:86
  188.2 33.0 %reduce-scatter.6.cloned.1.call-done = bf16[1,528,256]{2,1,0:T(8,128)(2,1)} async-done(((bf16[8,528,256]{2,1,0:T(8,128)(2,1)}), bf16[1,528,256]{2,1,0:T(8,128)(2,1)}) %reduce-scatter.6.cloned.1.call-update) | async-done | bytes 270352 | tf_op jit(solution)/shard_map/reduce_scatter | solution.py:107
  222.9 2.6 collective-permute-start
  225.5 2.2 collective-permute-start.1
  227.9 4.3 %collective-permute-start.3 = (bf16[1,528,256]{2,1,0:T(8,128)(2,1)S(1)}, bf16[1,528,256]{2,1,0:T(8,128)(2,1)S(1)}, u32[]{:S(2)}, u32[]{:S(2)}) collective-permute-start(bf16[1,528,256]{2,1,0:T(8,128)(2,1)S(1)} %pad_maximum_fusion.9), channel_id=1, source_target_pairs={{0,16},{8,24},{16,32},{24,40},{32,48},{40,56},{48,64},{56,72},{64,... | collective-permute-start | bytes 811016 | tf_op jit(solution)/shard_map/ppermute | solution.py:15
  232.2 2.2 collective-permute-start.4
  234.5 37.1 %reduce-scatter.8.cloned.1.call-done = bf16[1,545,256]{2,1,0:T(8,128)(2,1)} async-done(((bf16[8,545,256]{2,1,0:T(8,128)(2,1)}), bf16[1,545,256]{2,1,0:T(8,128)(2,1)}) %reduce-scatter.8.cloned.1.call-update) | async-done | bytes 279056 | tf_op jit(solution)/shard_map/reduce_scatter | solution.py:107
  275.1 1.9 collective-permute-start.6
  278.6 1.9 collective-permute-start.7
  280.6 6.1 %collective-permute-start.2 = (bf16[3,1,528,256]{3,2,1,0:T(8,128)(2,1)S(1)}, bf16[3,1,528,256]{3,2,1,0:T(8,128)(2,1)S(1)}, u32[]{:S(2)}, u32[]{:S(2)}) collective-permute-start(bf16[3,1,528,256]{3,2,1,0:T(8,128)(2,1)S(1)} %pad_maximum_fusion.4), channel_id=1, source_target_pairs={{0,8},{8,0},{16,24},{24,16},{32,40},{40,32},{48,56},{56,48},{64,72... | collective-permute-start | bytes 2433032 | tf_op jit(solution)/shard_map/ppermute | solution.py:129
  287.0 3.2 %collective-permute-done.7 = bf16[1,545,256]{2,1,0:T(8,128)(2,1)S(1)} collective-permute-done((bf16[1,545,256]{2,1,0:T(8,128)(2,1)S(1)}, bf16[1,545,256]{2,1,0:T(8,128)(2,1)S(1)}, u32[]{:S(2)}, u32[]{:S(2)}) %collective-permute-start.7) | collective-permute-done | bytes 279072 | tf_op jit(solution)/shard_map/ppermute | solution.py:15
  290.3 4.0 %collective-permute-start.8 = (bf16[3,1,545,256]{3,2,1,0:T(8,128)(2,1)S(1)}, bf16[3,1,545,256]{3,2,1,0:T(8,128)(2,1)S(1)}, u32[]{:S(2)}, u32[]{:S(2)}) collective-permute-start(bf16[3,1,545,256]{3,2,1,0:T(8,128)(2,1)S(1)} %pad_maximum_fusion), channel_id=1, source_target_pairs={{0,8},{8,0},{16,24},{24,16},{32,40},{40,32},{48,56},{56,48},{64,72... | collective-permute-start | bytes 2511368 | tf_op jit(solution)/shard_map/ppermute | solution.py:129
  297.3 2.0 fusion
  299.3 3.5 %fusion.1 = f32[1024]{0:T(1024)S(1)} fusion(f32[1024,3202]{0,1:T(8,128)S(1)} %get-tuple-element.31, f32[1024]{0:T(1024)S(1)} %compare_select_fusion, pred[3202]{0:T(1024)(128)(4,1)S(1)} %concatenate.183), kind=kLoop, calls=%fused_computation.6 | loop fusion | flops 13114368 | bytes 13126786 | tf_op jit(solution)/shard_map/reduce_sum | solution.py:30
  302.9 4.4 %fusion.26 = f32[1024,128]{1,0:T(8,128)S(1)} fusion(f32[1024,3202]{0,1:T(8,128)S(1)} %get-tuple-element.31, f32[1024]{0:T(1024)S(1)} %compare_select_fusion, pred[3202]{0:T(1024)(128)(4,1)S(1)} %concatenate.183, bf16[1,1601,256]{2,1,0:T(8,128)(2,1)S(1)} %select_select_fusion, bf16[1,1601,256]{2,1,0:T(8,128)(2,1)S(1)} %select_select_fusion.1, ...), kind=kOutput, calls=%fused_computation.28 | convolution fusion | flops 854270976 | bytes 15290498 | tf_op jit(solution)/shard_map/kqn,knd->kqd/dot_general | solution.py:31
  (161 shorter events, 35.1 us)
Async XLA Ops:
  6.5 134.9 %copy-start = (s32[1,32]{1,0:T(1,128)S(1)}, s32[1,32]{1,0:T(1,128)}, u32[]{:S(2)}) copy-start(s32[1,32]{1,0:T(1,128)} %param.15) | copy-start | bytes 388
  6.5 117.9 %all-gather.3.cloned.1.call-start = ((), (), s32[]{:S(2)}) async-start(), calls=%async_computation.6 | async-start | bytes 12976128 | tf_op jit(solution)/shard_map/all_gather | solution.py:82
  9.3 176.9 %reduce-scatter.4.cloned.1.call-start = ((), (), s32[]{:S(2)}) async-start(), calls=%async_computation.3 | async-start | bytes 2433024 | tf_op jit(solution)/shard_map/reduce_scatter | solution.py:107
  124.4 3.3 %copy-start.27 = (bf16[1,1601,1024]{2,1,0:T(8,128)(2,1)S(1)}, bf16[1,1601,1024]{2,1,0:T(8,128)(2,1)}, u32[]{:S(2)}) copy-start(bf16[1,1601,1024]{2,1,0:T(8,128)(2,1)} %param.9) | copy-start | bytes 9836548
  132.8 88.5 %reduce-scatter.6.cloned.1.call-start = ((), (), s32[]{:S(2)}) async-start(), calls=%async_computation.4 | async-start | bytes 2433024 | tf_op jit(solution)/shard_map/reduce_scatter | solution.py:107
  132.8 3.9 %copy-start.21 = (bf16[32,32,256]{2,1,0:T(8,128)(2,1)S(1)}, bf16[32,32,256]{2,1,0:T(8,128)(2,1)}, u32[]{:S(2)}) copy-start(bf16[32,32,256]{2,1,0:T(8,128)(2,1)} %copy-done.20) | copy-start | bytes 1572868
  132.8 3.9 %copy-start.28 = (bf16[1,1601,1024]{2,1,0:T(8,128)(2,1)S(1)}, bf16[1,1601,1024]{2,1,0:T(8,128)(2,1)}, u32[]{:S(2)}) copy-start(bf16[1,1601,1024]{2,1,0:T(8,128)(2,1)} %param.9) | copy-start | bytes 9836548
  141.2 130.4 %reduce-scatter.8.cloned.1.call-start = ((), (), s32[]{:S(2)}) async-start(), calls=%async_computation.5 | async-start | bytes 2543616 | tf_op jit(solution)/shard_map/reduce_scatter | solution.py:107
  142.1 4.0 %copy-start.22 = (bf16[32,32,256]{2,1,0:T(8,128)(2,1)S(1)}, bf16[32,32,256]{2,1,0:T(8,128)(2,1)}, u32[]{:S(2)}) copy-start(bf16[32,32,256]{2,1,0:T(8,128)(2,1)} %copy-done.20) | copy-start | bytes 1572868
  142.1 4.0 %copy-start.29 = (bf16[1,1601,1024]{2,1,0:T(8,128)(2,1)S(1)}, bf16[1,1601,1024]{2,1,0:T(8,128)(2,1)}, u32[]{:S(2)}) copy-start(bf16[1,1601,1024]{2,1,0:T(8,128)(2,1)} %param.9) | copy-start | bytes 9836548
  167.8 11.6 %copy-start.30 = (f32[8192]{0:T(1024)S(1)}, f32[8192]{0:T(1024)}, u32[]{:S(2)}) copy-start(f32[8192]{0:T(1024)} %param.10) | copy-start | bytes 98308
  179.3 6.7 %copy-start.26 = (f32[128]{0:T(128)S(1)}, f32[128]{0:T(128)}, u32[]{:S(2)}) copy-start(f32[128]{0:T(128)} %param.13) | copy-start | bytes 1540
  186.0 36.7 %copy-start.25 = (f32[128]{0:T(128)S(1)}, f32[128]{0:T(128)}, u32[]{:S(2)}) copy-start(f32[128]{0:T(128)} %param.14) | copy-start | bytes 1540
  186.2 48.2 %copy-start.6 = (bf16[1,528,256]{2,1,0:T(8,128)(2,1)S(1)}, bf16[1,528,256]{2,1,0:T(8,128)(2,1)}, u32[]{:S(2)}) copy-start(bf16[1,528,256]{2,1,0:T(8,128)(2,1)} %reduce-scatter.4.cloned.1.call-done) | copy-start | bytes 811012
  221.2 6.6 %copy-start.7 = (bf16[1,528,256]{2,1,0:T(8,128)(2,1)S(1)}, bf16[1,528,256]{2,1,0:T(8,128)(2,1)}, u32[]{:S(2)}) copy-start(bf16[1,528,256]{2,1,0:T(8,128)(2,1)} %reduce-scatter.6.cloned.1.call-done) | copy-start | bytes 811012
  222.9 55.6 %collective-permute-start = (bf16[1,528,256]{2,1,0:T(8,128)(2,1)S(1)}, bf16[1,528,256]{2,1,0:T(8,128)(2,1)S(1)}, u32[]{:S(2)}, u32[]{:S(2)}) collective-permute-start(bf16[1,528,256]{2,1,0:T(8,128)(2,1)S(1)} %pad_maximum_fusion.8), channel_id=1, source_target_pairs={{0,16},{8,24},{16,32},{24,40},{32,48},{40,56},{48,64},{56,72},{64,... | collective-permute-start | bytes 811016 | tf_op jit(solution)/shard_map/ppermute | solution.py:15
  225.5 55.0 %collective-permute-start.1 = (bf16[1,528,256]{2,1,0:T(8,128)(2,1)S(1)}, bf16[1,528,256]{2,1,0:T(8,128)(2,1)S(1)}, u32[]{:S(2)}, u32[]{:S(2)}) collective-permute-start(bf16[1,528,256]{2,1,0:T(8,128)(2,1)S(1)} %pad_maximum_fusion.8), channel_id=1, source_target_pairs={{0,32},{8,40},{16,48},{24,56},{32,64},{40,72},{48,80},{56,88},{64,... | collective-permute-start | bytes 811016 | tf_op jit(solution)/shard_map/ppermute | solution.py:15
  227.9 58.8 %collective-permute-start.3 = (bf16[1,528,256]{2,1,0:T(8,128)(2,1)S(1)}, bf16[1,528,256]{2,1,0:T(8,128)(2,1)S(1)}, u32[]{:S(2)}, u32[]{:S(2)}) collective-permute-start(bf16[1,528,256]{2,1,0:T(8,128)(2,1)S(1)} %pad_maximum_fusion.9), channel_id=1, source_target_pairs={{0,16},{8,24},{16,32},{24,40},{32,48},{40,56},{48,64},{56,72},{64,... | collective-permute-start | bytes 811016 | tf_op jit(solution)/shard_map/ppermute | solution.py:15
  232.2 54.5 %collective-permute-start.4 = (bf16[1,528,256]{2,1,0:T(8,128)(2,1)S(1)}, bf16[1,528,256]{2,1,0:T(8,128)(2,1)S(1)}, u32[]{:S(2)}, u32[]{:S(2)}) collective-permute-start(bf16[1,528,256]{2,1,0:T(8,128)(2,1)S(1)} %pad_maximum_fusion.9), channel_id=1, source_target_pairs={{0,32},{8,40},{16,48},{24,56},{32,64},{40,72},{48,80},{56,88},{64,... | collective-permute-start | bytes 811016 | tf_op jit(solution)/shard_map/ppermute | solution.py:15
  275.1 11.9 %collective-permute-start.6 = (bf16[1,545,256]{2,1,0:T(8,128)(2,1)S(1)}, bf16[1,545,256]{2,1,0:T(8,128)(2,1)S(1)}, u32[]{:S(2)}, u32[]{:S(2)}) collective-permute-start(bf16[1,545,256]{2,1,0:T(8,128)(2,1)S(1)} %pad_maximum_fusion.7), channel_id=1, source_target_pairs={{0,16},{8,24},{16,32},{24,40},{32,48},{40,56},{48,64},{56,72},{64,... | collective-permute-start | bytes 837128 | tf_op jit(solution)/shard_map/ppermute | solution.py:15
  278.6 11.6 %collective-permute-start.7 = (bf16[1,545,256]{2,1,0:T(8,128)(2,1)S(1)}, bf16[1,545,256]{2,1,0:T(8,128)(2,1)S(1)}, u32[]{:S(2)}, u32[]{:S(2)}) collective-permute-start(bf16[1,545,256]{2,1,0:T(8,128)(2,1)S(1)} %pad_maximum_fusion.7), channel_id=1, source_target_pairs={{0,32},{8,40},{16,48},{24,56},{32,64},{40,72},{48,80},{56,88},{64,... | collective-permute-start | bytes 837128 | tf_op jit(solution)/shard_map/ppermute | solution.py:15
  280.6 13.7 %collective-permute-start.2 = (bf16[3,1,528,256]{3,2,1,0:T(8,128)(2,1)S(1)}, bf16[3,1,528,256]{3,2,1,0:T(8,128)(2,1)S(1)}, u32[]{:S(2)}, u32[]{:S(2)}) collective-permute-start(bf16[3,1,528,256]{3,2,1,0:T(8,128)(2,1)S(1)} %pad_maximum_fusion.4), channel_id=1, source_target_pairs={{0,8},{8,0},{16,24},{24,16},{32,40},{40,32},{48,56},{56,48},{64,72... | collective-permute-start | bytes 2433032 | tf_op jit(solution)/shard_map/ppermute | solution.py:129
  286.8 7.6 %collective-permute-start.5 = (bf16[3,1,528,256]{3,2,1,0:T(8,128)(2,1)S(1)}, bf16[3,1,528,256]{3,2,1,0:T(8,128)(2,1)S(1)}, u32[]{:S(2)}, u32[]{:S(2)}) collective-permute-start(bf16[3,1,528,256]{3,2,1,0:T(8,128)(2,1)S(1)} %pad_maximum_fusion.5), channel_id=1, source_target_pairs={{0,8},{8,0},{16,24},{24,16},{32,40},{40,32},{48,56},{56,48},{64,72... | collective-permute-start | bytes 2433032 | tf_op jit(solution)/shard_map/ppermute | solution.py:129
  290.3 6.0 %collective-permute-start.8 = (bf16[3,1,545,256]{3,2,1,0:T(8,128)(2,1)S(1)}, bf16[3,1,545,256]{3,2,1,0:T(8,128)(2,1)S(1)}, u32[]{:S(2)}, u32[]{:S(2)}) collective-permute-start(bf16[3,1,545,256]{3,2,1,0:T(8,128)(2,1)S(1)} %pad_maximum_fusion), channel_id=1, source_target_pairs={{0,8},{8,0},{16,24},{24,16},{32,40},{40,32},{48,56},{56,48},{64,72... | collective-permute-start | bytes 2511368 | tf_op jit(solution)/shard_map/ppermute | solution.py:129
  (20 other events, 32.2 us)
Sparse Core Ops, SparseCore 0:
  10.1 114.2 all-gather.2
  132.9 41.4 reduce-scatter.3
  176.9 44.2 reduce-scatter.5
  223.7 47.8 reduce-scatter.7

commit v13 on v10

--- a/solution.py
+++ b/solution.py
@@ -108,7 +108,7 @@
         key_part = rms_scale(own_kv[..., :head_dim], key_gain)
         return jnp.concatenate([key_part, own_kv[..., head_dim:]], axis=-1).astype(jnp.bfloat16)
 
-    token_cut = (features.shape[0] * 2 // 24) * 8
+    token_cut = (features.shape[0] // 24) * 8
     packed_halves = [reduced_half(features[:token_cut]), reduced_half(features[token_cut:])]
     span_index = lax.axis_index("seq")
     image_ids = span_index - jnp.arange(IMAGE_LOOKBACK + 1, dtype=jnp.int32)

time: 296 us -> 296 us (level)
  no operation moved by 1% of the time
where the time goes in v13:
time: 296 us
  waiting for transfers between devices  182 us (61%)
  matrix products  33.1 us (11%)
  local copies, waits for them, and re-layouts  29.5 us (10%)
  between operations  17.4 us (6%)
  other arithmetic  17.2 us (6%)
  starting transfers between devices  16.9 us (6%)
    all_gather x1, waiting for transfers between devices, on_device(): lax.all_gather(jnp.concatenate([kv_as_rows, query_weight], axis=0), 'seq'...  115 us
    reduce_scatter x2, waiting for transfers between devices, reduced_half(): lax.psum_scatter(partials, 'fsdp', scatter_dimension=0, tiled=True)  33.6 us
    ppermute x4, waiting for transfers between devices, from_behind(): lax.ppermute(value, axis, [(source, source + steps) for source in range(i...  32 us
    dot_general x16, matrix products, reduced_half(): jnp.dot(rows, both[:, block * kv_rows:(block + 1) * kv_rows, pair * pair_...  18 us
    ppermute x4, starting transfers between devices, from_behind(): lax.ppermute(value, axis, [(source, source + steps) for source in range(i...  12.3 us
    reshape x1, local copies, waits for them, and re-layouts, on_device(): query_block = both[:, column_blocks * kv_rows:].reshape(-1, query_width)  11.5 us
    slice x1, local copies, waits for them, and re-layouts, on_device(): query_block = both[:, column_blocks * kv_rows:].reshape(-1, query_width)  7.5 us
    dot_general x2, matrix products, attend_part(): jnp.einsum('kqn,knd->kqd', weights.astype(jnp.bfloat16), key_value_pair[....  6.1 us
  transfers between devices with their start and end apart: 9, of which 7 were waited for; matrix products, arithmetic and copies ran while one was open for 18% of the time, Pallas kernels for 0%

profile of v13, /device:TPU:133, one launch (start us, length us, event | category | flops | bytes accessed | tf_op | source)
XLA Modules:
  0.0 295.8 jit_solution(9482487556939102441)
XLA Ops:
  7.6 1.8 pad_maximum_fusion.6
  9.4 115.3 %all-gather.3.cloned.1.call-done = bf16[12288,512]{1,0:T(8,128)(2,1)} async-done(((bf16[384,512]{1,0:T(8,128)(2,1)}), bf16[12288,512]{1,0:T(8,128)(2,1)}) %all-gather.3.cloned.1.call-update) | async-done | bytes 12582928 | tf_op jit(solution)/shard_map/all_gather | solution.py:82
  124.7 3.0 %fusion.121 = (bf16[32,32,256]{2,1,0:T(8,128)(2,1)S(1)}, bf16[32,32,256]{2,1,0:T(8,128)(2,1)S(1)}, bf16[32,32,256]{2,1,0:T(8,128)(2,1)S(1)}, bf16[32,32,256]{2,1...) fusion(bf16[32,384,512]{2,1,0:T(8,128)(2,1)} %bitcast.226), kind=kLoop, calls=%fused_computation.175 | loop fusion | bytes 8388608 | tf_op jit(solution)/shard_map/slice | solution.py:99
  133.1 3.5 %fusion.21 = bf16[8,1073,256]{2,1,0:T(8,128)(2,1)} fusion(bf16[1024,256]{1,0:T(8,128)(2,1)} %bitcast.251, bf16[1,1601,1024]{2,1,0:T(8,128)(2,1)} %param.9), kind=kOutput, calls=%fused_computation.33 | convolution fusion | flops 562835712 | bytes 3289088 | tf_op jit(solution)/shard_map/dot_general | solution.py:97
  136.6 1.6 fusion.23
  138.2 1.6 fusion.25
  146.0 1.6 fusion.35
  154.4 3.2 %fusion.3 = f32[256]{0:T(256)S(1)} fusion(bf16[256,8192]{1,0:T(8,128)(2,1)} %param.8), kind=kLoop, calls=%fused_computation.8 | loop fusion | flops 6291200 | bytes 4195328 | tf_op jit(solution)/shard_map/reduce_sum | solution.py:19
  157.6 7.5 %slice.128 = bf16[32,256,512]{2,1,0:T(8,128)(2,1)} slice(bf16[32,384,512]{2,1,0:T(8,128)(2,1)} %bitcast.227), slice={[0:32], [128:384], [0:512]} | slice | bytes 16777216 | tf_op jit(solution)/shard_map/slice | solution.py:85
  165.1 11.5 %copy.15 = bf16[8192,512]{0,1:T(8,128)(2,1)} copy(bf16[8192,512]{1,0:T(8,128)(2,1)} %bitcast.225) | data formatting | bytes 16777216 | tf_op jit(solution)/shard_map/reshape | solution.py:85
  179.2 5.2 %collective-permute-start = (bf16[1,528,256]{2,1,0:T(8,128)(2,1)S(1)}, bf16[1,528,256]{2,1,0:T(8,128)(2,1)S(1)}, u32[]{:S(2)}, u32[]{:S(2)}) collective-permute-start(bf16[1,528,256]{2,1,0:T(8,128)(2,1)S(1)} %pad_maximum_fusion.7), channel_id=1, source_target_pairs={{0,16},{8,24},{16,32},{24,40},{32,48},{40,56},{48,64},{56,72},{64,... | collective-permute-start | bytes 811016 | tf_op jit(solution)/shard_map/ppermute | solution.py:15
  184.4 2.5 collective-permute-start.1
  188.8 7.7 %collective-permute-done.1 = bf16[1,528,256]{2,1,0:T(8,128)(2,1)S(1)} collective-permute-done((bf16[1,528,256]{2,1,0:T(8,128)(2,1)S(1)}, bf16[1,528,256]{2,1,0:T(8,128)(2,1)S(1)}, u32[]{:S(2)}, u32[]{:S(2)}) %collective-permute-start.1) | collective-permute-done | bytes 270368 | tf_op jit(solution)/shard_map/ppermute | solution.py:15
  196.6 3.0 %collective-permute-start.2 = (bf16[3,1,528,256]{3,2,1,0:T(8,128)(2,1)S(1)}, bf16[3,1,528,256]{3,2,1,0:T(8,128)(2,1)S(1)}, u32[]{:S(2)}, u32[]{:S(2)}) collective-permute-start(bf16[3,1,528,256]{3,2,1,0:T(8,128)(2,1)S(1)} %pad_maximum_fusion.4), channel_id=1, source_target_pairs={{0,8},{8,0},{16,24},{24,16},{32,40},{40,32},{48,56},{56,48},{64,72... | collective-permute-start | bytes 2433032 | tf_op jit(solution)/shard_map/ppermute | solution.py:125
  199.6 5.9 %multiply_reduce_fusion.1 = (f32[256,4]{0,1:T(4,128)S(1)}, f32[256,4,128]{2,0,1:T(8,128)S(1)}) fusion(bf16[4,128,8192]{2,1,0:T(8,128)(2,1)} %bitcast.228, bf16[256,8192]{1,0:T(8,128)(2,1)S(1)} %copy-done.2, f32[8192]{0:T(1024)S(1)} %copy-done.20, f32[256]{0:T(256)S(1)} %add_rsqrt_fusion.3), kind=kOutput, calls=%fused_computation.117 | convolution fusion | flops 2156133376 | bytes 13145088 | tf_op jit(solution)/shard_map/dot_general | solution.py:86
  205.9 33.6 %reduce-scatter.5.cloned.1.call-done = bf16[1,1073,256]{2,1,0:T(8,128)(2,1)} async-done(((bf16[8,1073,256]{2,1,0:T(8,128)(2,1)}), bf16[1,1073,256]{2,1,0:T(8,128)(2,1)}) %reduce-scatter.5.cloned.1.call-update) | async-done | bytes 549392 | tf_op jit(solution)/shard_map/reduce_scatter | solution.py:107
  242.2 2.4 collective-permute-start.3
  244.6 2.3 collective-permute-start.4
  247.2 12.0 %collective-permute-done.3 = bf16[1,1073,256]{2,1,0:T(8,128)(2,1)S(1)} collective-permute-done((bf16[1,1073,256]{2,1,0:T(8,128)(2,1)S(1)}, bf16[1,1073,256]{2,1,0:T(8,128)(2,1)S(1)}, u32[]{:S(2)}, u32[]{:S(2)}) %collective-permute-start.3) | collective-permute-done | bytes 549408 | tf_op jit(solution)/shard_map/ppermute | solution.py:15
  259.2 11.6 %collective-permute-done.4 = bf16[1,1073,256]{2,1,0:T(8,128)(2,1)S(1)} collective-permute-done((bf16[1,1073,256]{2,1,0:T(8,128)(2,1)S(1)}, bf16[1,1073,256]{2,1,0:T(8,128)(2,1)S(1)}, u32[]{:S(2)}, u32[]{:S(2)}) %collective-permute-start.4) | collective-permute-done | bytes 549408 | tf_op jit(solution)/shard_map/ppermute | solution.py:15
  276.4 2.0 fusion
  278.4 3.7 %fusion.1 = f32[1024]{0:T(1024)S(1)} fusion(f32[1024,3202]{0,1:T(8,128)S(1)} %get-tuple-element.29, f32[1024]{0:T(1024)S(1)} %compare_select_fusion, pred[3202]{0:T(1024)(128)(4,1)S(1)} %concatenate.152), kind=kLoop, calls=%fused_computation.6 | loop fusion | flops 13114368 | bytes 13126786 | tf_op jit(solution)/shard_map/reduce_sum | solution.py:30
  282.1 4.4 %fusion.50 = f32[1024,128]{1,0:T(8,128)S(1)} fusion(f32[1024,3202]{0,1:T(8,128)S(1)} %get-tuple-element.29, f32[1024]{0:T(1024)S(1)} %compare_select_fusion, pred[3202]{0:T(1024)(128)(4,1)S(1)} %concatenate.152, bf16[1,1601,256]{2,1,0:T(8,128)(2,1)S(1)} %get-tuple-element.20, bf16[1,1601,256]{2,1,0:T(8,128)(2,1)S(1)} %get-tuple-element.21, ...), kind=kOutput, calls=%fused_computation.61 | convolution fusion | flops 854270976 | bytes 15290498 | tf_op jit(solution)/shard_map/kqn,knd->kqd/dot_general | solution.py:31
  286.6 1.7 fusion.80
  (114 shorter events, 30.1 us)
Async XLA Ops:
  6.5 141.1 %copy-start = (s32[1,32]{1,0:T(1,128)S(1)}, s32[1,32]{1,0:T(1,128)}, u32[]{:S(2)}) copy-start(s32[1,32]{1,0:T(1,128)} %param.15) | copy-start | bytes 388
  6.5 118.2 %all-gather.3.cloned.1.call-start = ((), (), s32[]{:S(2)}) async-start(), calls=%async_computation.4 | async-start | bytes 12976128 | tf_op jit(solution)/shard_map/all_gather | solution.py:82
  9.3 167.2 %reduce-scatter.3.cloned.1.call-start = ((), (), s32[]{:S(2)}) async-start(), calls=%async_computation.2 | async-start | bytes 2433024 | tf_op jit(solution)/shard_map/reduce_scatter | solution.py:107
  124.7 3.3 %copy-start.18 = (bf16[1,1601,1024]{2,1,0:T(8,128)(2,1)S(1)}, bf16[1,1601,1024]{2,1,0:T(8,128)(2,1)}, u32[]{:S(2)}) copy-start(bf16[1,1601,1024]{2,1,0:T(8,128)(2,1)} %param.9) | copy-start | bytes 9836548
  127.7 1.6 copy-start.11
  127.8 1.6 copy-start.13
  127.8 1.6 copy-start.15
  127.8 2.0 copy-start.7
  127.8 2.5 copy-start.5
  133.1 3.5 %copy-start.14 = (bf16[32,32,256]{2,1,0:T(8,128)(2,1)S(1)}, bf16[32,32,256]{2,1,0:T(8,128)(2,1)}, u32[]{:S(2)}) copy-start(bf16[32,32,256]{2,1,0:T(8,128)(2,1)} %copy-done.13) | copy-start | bytes 1572868
  133.1 106.4 %reduce-scatter.5.cloned.1.call-start = ((), (), s32[]{:S(2)}) async-start(), calls=%async_computation.3 | async-start | bytes 4976640 | tf_op jit(solution)/shard_map/reduce_scatter | solution.py:107
  133.1 3.5 %copy-start.19 = (bf16[1,1601,1024]{2,1,0:T(8,128)(2,1)S(1)}, bf16[1,1601,1024]{2,1,0:T(8,128)(2,1)}, u32[]{:S(2)}) copy-start(bf16[1,1601,1024]{2,1,0:T(8,128)(2,1)} %param.9) | copy-start | bytes 9836548
  165.1 14.0 %copy-start.16 = (f32[128]{0:T(128)S(1)}, f32[128]{0:T(128)}, u32[]{:S(2)}) copy-start(f32[128]{0:T(128)} %param.14) | copy-start | bytes 1540
  176.5 23.0 %copy-start.20 = (f32[8192]{0:T(1024)S(1)}, f32[8192]{0:T(1024)}, u32[]{:S(2)}) copy-start(f32[8192]{0:T(1024)} %param.10) | copy-start | bytes 98308
  176.5 23.0 %copy-start.2 = (bf16[256,8192]{1,0:T(8,128)(2,1)S(1)}, bf16[256,8192]{1,0:T(8,128)(2,1)}, u32[]{:S(2)}) copy-start(bf16[256,8192]{1,0:T(8,128)(2,1)} %param.8) | copy-start | bytes 12582916
  179.2 9.6 %collective-permute-start = (bf16[1,528,256]{2,1,0:T(8,128)(2,1)S(1)}, bf16[1,528,256]{2,1,0:T(8,128)(2,1)S(1)}, u32[]{:S(2)}, u32[]{:S(2)}) collective-permute-start(bf16[1,528,256]{2,1,0:T(8,128)(2,1)S(1)} %pad_maximum_fusion.7), channel_id=1, source_target_pairs={{0,16},{8,24},{16,32},{24,40},{32,48},{40,56},{48,64},{56,72},{64,... | collective-permute-start | bytes 811016 | tf_op jit(solution)/shard_map/ppermute | solution.py:15
  184.4 12.1 %collective-permute-start.1 = (bf16[1,528,256]{2,1,0:T(8,128)(2,1)S(1)}, bf16[1,528,256]{2,1,0:T(8,128)(2,1)S(1)}, u32[]{:S(2)}, u32[]{:S(2)}) collective-permute-start(bf16[1,528,256]{2,1,0:T(8,128)(2,1)S(1)} %pad_maximum_fusion.7), channel_id=1, source_target_pairs={{0,32},{8,40},{16,48},{24,56},{32,64},{40,72},{48,80},{56,88},{64,... | collective-permute-start | bytes 811016 | tf_op jit(solution)/shard_map/ppermute | solution.py:15
  196.6 9.2 %collective-permute-start.2 = (bf16[3,1,528,256]{3,2,1,0:T(8,128)(2,1)S(1)}, bf16[3,1,528,256]{3,2,1,0:T(8,128)(2,1)S(1)}, u32[]{:S(2)}, u32[]{:S(2)}) collective-permute-start(bf16[3,1,528,256]{3,2,1,0:T(8,128)(2,1)S(1)} %pad_maximum_fusion.4), channel_id=1, source_target_pairs={{0,8},{8,0},{16,24},{24,16},{32,40},{40,32},{48,56},{56,48},{64,72... | collective-permute-start | bytes 2433032 | tf_op jit(solution)/shard_map/ppermute | solution.py:125
  199.6 5.9 %copy-start.17 = (f32[128]{0:T(128)S(1)}, f32[128]{0:T(128)}, u32[]{:S(2)}) copy-start(f32[128]{0:T(128)} %param.13) | copy-start | bytes 1540
  239.5 7.4 %copy-start.3 = (bf16[1,1073,256]{2,1,0:T(8,128)(2,1)S(1)}, bf16[1,1073,256]{2,1,0:T(8,128)(2,1)}, u32[]{:S(2)}) copy-start(bf16[1,1073,256]{2,1,0:T(8,128)(2,1)} %reduce-scatter.5.cloned.1.call-done) | copy-start | bytes 1648132
  242.2 17.0 %collective-permute-start.3 = (bf16[1,1073,256]{2,1,0:T(8,128)(2,1)S(1)}, bf16[1,1073,256]{2,1,0:T(8,128)(2,1)S(1)}, u32[]{:S(2)}, u32[]{:S(2)}) collective-permute-start(bf16[1,1073,256]{2,1,0:T(8,128)(2,1)S(1)} %pad_maximum_fusion.5), channel_id=1, source_target_pairs={{0,16},{8,24},{16,32},{24,40},{32,48},{40,56},{48,64},{56,72},{64,... | collective-permute-start | bytes 1648136 | tf_op jit(solution)/shard_map/ppermute | solution.py:15
  244.6 26.2 %collective-permute-start.4 = (bf16[1,1073,256]{2,1,0:T(8,128)(2,1)S(1)}, bf16[1,1073,256]{2,1,0:T(8,128)(2,1)S(1)}, u32[]{:S(2)}, u32[]{:S(2)}) collective-permute-start(bf16[1,1073,256]{2,1,0:T(8,128)(2,1)S(1)} %pad_maximum_fusion.5), channel_id=1, source_target_pairs={{0,32},{8,40},{16,48},{24,56},{32,64},{40,72},{48,80},{56,88},{64,... | collective-permute-start | bytes 1648136 | tf_op jit(solution)/shard_map/ppermute | solution.py:15
  270.9 4.7 %collective-permute-start.5 = (bf16[3,1,1073,256]{3,2,1,0:T(8,128)(2,1)S(1)}, bf16[3,1,1073,256]{3,2,1,0:T(8,128)(2,1)S(1)}, u32[]{:S(2)}, u32[]{:S(2)}) collective-permute-start(bf16[3,1,1073,256]{3,2,1,0:T(8,128)(2,1)S(1)} %pad_maximum_fusion), channel_id=1, source_target_pairs={{0,8},{8,0},{16,24},{24,16},{32,40},{40,32},{48,56},{56,48},{64,72... | collective-permute-start | bytes 4944392 | tf_op jit(solution)/shard_map/ppermute | solution.py:125
  286.6 2.7 copy-start.1
  (6 other events, 9.3 us)
Sparse Core Ops, SparseCore 0:
  10.1 114.5 all-gather.2
  133.2 41.4 reduce-scatter.2
  177.3 62.0 reduce-scatter.4
